TPU v7x, 256 devices: a whole 4x4x8 slice. The times are simulated.
256 devices in a mesh: seq: 16 (over x, y), head: 16 (over z, core).
Axes of the slice: x: 4, y: 4, z: 8, core: 2. Of those that a mesh axis runs over, the one named last changes fastest.
Arguments:
- queries: bfloat16 [32768, 8192], P(('seq', 'head')), may hold values from -17 to 17
- key_vectors: bfloat16 [32768, 8192], P(('seq', 'head')), may hold values from -6 to 6
- values: bfloat16 [32768, 8192], P(('seq', 'head')), may hold values from -17 to 17
- gate_logits: bfloat16 [32768, 8192], P(('seq', 'head')), may hold values from -6 to 6
- norm_gain: bfloat16 [8192], replicated, may hold values from 0.25 to 1.75
Outputs:
- gated_output: bfloat16 [32768, 8192], P(('seq', 'head'))
All inputs are finite; a program needn't handle non-finite values.
Results may differ from a plain program's by a relative error of at most 0.0058.
Values may be sent and summed in bfloat16 or wider, within the bound.
No kernel may reach another device: no remote copies, remote signals or barrier semaphores. Data moves between devices by JAX's collectives and lax.ppermute only.
A program may use at most 64 MiB of HBM per device.

v0:
```python
import jax
import jax.numpy as jnp
from jax import lax
from jax.sharding import PartitionSpec as P

E = 128
BLK = 512


def entering(part, axis, combine, identity):
    place = lax.axis_index(axis)
    gathered = lax.all_gather(part, axis)
    state = jnp.zeros_like(part) + jnp.asarray(identity, part.dtype)

    def one(lap, state):
        return combine(state, lax.dynamic_index_in_dim(gathered, lap, 0, False))

    return lax.fori_loop(0, place, one, state)


def block_output(blocks):
    query_block, key_block, value_block, prefix_block = blocks
    scores = jnp.einsum("bhe,che->hbc", query_block, key_block, preferred_element_type=jnp.float32)
    length = scores.shape[1]
    lower_mask = lax.broadcasted_iota(jnp.int32, (length, length), 0) >= lax.broadcasted_iota(
        jnp.int32, (length, length), 1
    )
    weights = jnp.where(lower_mask[None], scores, 0.0).astype(jnp.bfloat16)
    local_part = jnp.einsum(
        "hbc,che->bhe", weights, value_block, preferred_element_type=jnp.float32
    )
    carried_part = jnp.einsum(
        "bhe,hef->bhf", query_block, prefix_block, preferred_element_type=jnp.float32
    )
    return (local_part + carried_part).astype(jnp.bfloat16)


def on_device(queries, key_vectors, values, gate_logits, norm_gain):
    groups = lax.axis_size("head")
    local_heads = queries.shape[1] // groups // E
    query_heads, key_heads, value_heads = (
        lax.all_to_all(queries, "head", split_axis=1, concat_axis=0, tiled=True),
        lax.all_to_all(key_vectors, "head", split_axis=1, concat_axis=0, tiled=True),
        lax.all_to_all(values, "head", split_axis=1, concat_axis=0, tiled=True),
    )
    seq_rows = key_heads.shape[0]
    block_count = seq_rows // BLK
    key_blocks = key_heads.reshape(block_count, BLK, local_heads, E)
    value_blocks = value_heads.reshape(block_count, BLK, local_heads, E)
    block_state = jnp.einsum(
        "nbhe,nbhf->nhef", key_blocks, value_blocks, preferred_element_type=jnp.float32
    )
    shard_state = jnp.sum(block_state, axis=0)
    zero_state = jnp.zeros_like(shard_state)
    carried = entering(shard_state, "seq", jnp.add, zero_state)
    within_shard = jnp.concatenate(
        [jnp.zeros_like(block_state[:1]), jnp.cumsum(block_state[:-1], axis=0)], axis=0
    )
    prefix_blocks = (carried[None] + within_shard).astype(jnp.bfloat16)
    query_blocks = query_heads.reshape(block_count, BLK, local_heads, E)
    attended = lax.map(block_output, (query_blocks, key_blocks, value_blocks, prefix_blocks))
    attended = attended.reshape(seq_rows, local_heads * E)
    features = lax.all_to_all(attended, "head", split_axis=0, concat_axis=1, tiled=True).astype(
        jnp.float32
    )
    mean_square = jnp.mean(features * features, axis=1, keepdims=True)
    scaled = features * lax.rsqrt(mean_square + 1e-06) * norm_gain.astype(jnp.float32)[None, :]
    scaled = scaled * jax.nn.sigmoid(gate_logits.astype(jnp.float32))
    return scaled.astype(jnp.bfloat16)


def solution(mesh):
    placed = (
        P(("seq", "head"), None),
        P(("seq", "head"), None),
        P(("seq", "head"), None),
        P(("seq", "head"), None),
        P(),
    )
    return jax.shard_map(
        on_device, mesh=mesh, in_specs=placed, out_specs=P(("seq", "head"), None), check_vma=False
    )
```

profile of v0, /device:TPU:31, one launch (start us, length us, event | category | flops | bytes accessed | tf_op | source)
XLA Modules:
  0.0 313.5 jit_solution(13645746460259131030)
XLA Ops:
  6.5 3.1 %copy.73 = bf16[16,16,8,512]{3,2,0,1:T(8,128)(2,1)} copy(bf16[16,16,8,512]{3,2,1,0:T(8,128)(2,1)} %bitcast.67) | data formatting | bytes 4194304 | tf_op jit(solution)/shard_map/all_to_all | solution.py:44
  9.7 9.2 %all-to-all-start = ((bf16[128,16,512]{2,0,1:T(8,128)(2,1)}), bf16[128,16,512]{2,0,1:T(8,128)(2,1)S(1)}, u32[]{:S(2)}, u32[]{:S(2)}) async-start(bf16[128,16,512]{2,0,1:T(8,128)(2,1)} %bitcast.66), calls=%async_computation | async-start | bytes 4194304 | tf_op jit(solution)/shard_map/all_to_all | solution.py:44
  18.8 3.1 copy.71
  22.0 45.8 %all-to-all-done = bf16[128,16,512]{2,0,1:T(8,128)(2,1)S(1)} async-done(((bf16[128,16,512]{2,0,1:T(8,128)(2,1)}), bf16[128,16,512]{2,0,1:T(8,128)(2,1)S(1)}, u32[]{:S(2)}, u32[]{:S(2)}) %all-to-all-start) | async-done | bytes 2097184 | tf_op jit(solution)/shard_map/all_to_all | solution.py:44
  69.1 5.0 %all-to-all-start.2 = ((bf16[128,16,512]{2,0,1:T(8,128)(2,1)}), bf16[128,16,512]{2,0,1:T(8,128)(2,1)}, u32[]{:S(2)}, u32[]{:S(2)}) async-start(bf16[128,16,512]{2,0,1:T(8,128)(2,1)} %bitcast.65), calls=%async_computation.2 | async-start | bytes 4194304 | tf_op jit(solution)/shard_map/all_to_all | solution.py:43
  74.1 2.6 reshape.45
  76.7 46.4 %all-to-all-done.2 = bf16[128,16,512]{2,0,1:T(8,128)(2,1)} async-done(((bf16[128,16,512]{2,0,1:T(8,128)(2,1)}), bf16[128,16,512]{2,0,1:T(8,128)(2,1)}, u32[]{:S(2)}, u32[]{:S(2)}) %all-to-all-start.2) | async-done | bytes 2097184 | tf_op jit(solution)/shard_map/all_to_all | solution.py:43
  123.1 4.0 %reshape.47 = bf16[4,512,4,128]{3,2,1,0:T(4,128)(2,1)} reshape(bf16[16,128,512]{2,1,0:T(8,128)(2,1)} %bitcast.9) | data formatting | bytes 4194304 | tf_op jit(solution)/shard_map/reshape | solution.py:48
  127.2 3.3 %fusion.19 = (f32[4,128,128]{2,1,0:T(8,128)}, f32[4,4,128,128]{3,2,1,0:T(8,128)S(1)}) fusion(bf16[4,512,4,128]{3,2,1,0:T(4,128)(2,1)S(1)} %reshape.45, bf16[4,512,4,128]{3,2,1,0:T(4,128)(2,1)} %reshape.47), kind=kOutput, calls=%fused_computation.36 | convolution fusion | flops 268632064 | bytes 5505024 | tf_op jit(solution)/shard_map/nbhe,nbhf->nhef/dot_general | solution.py:50
  130.4 3.2 %copy.72 = bf16[16,16,8,512]{3,2,0,1:T(8,128)(2,1)} copy(bf16[16,16,8,512]{3,2,1,0:T(8,128)(2,1)} %bitcast.69) | data formatting | bytes 4194304 | tf_op jit(solution)/shard_map/all_to_all | solution.py:42
  133.6 5.0 %all-to-all-start.1 = ((bf16[128,16,512]{2,0,1:T(8,128)(2,1)}), bf16[128,16,512]{2,0,1:T(8,128)(2,1)S(1)}, u32[]{:S(2)}, u32[]{:S(2)}) async-start(bf16[128,16,512]{2,0,1:T(8,128)(2,1)} %bitcast.64), calls=%async_computation.1 | async-start | bytes 4194304 | tf_op jit(solution)/shard_map/all_to_all | solution.py:42
  138.6 48.9 %all-to-all-done.1 = bf16[128,16,512]{2,0,1:T(8,128)(2,1)S(1)} async-done(((bf16[128,16,512]{2,0,1:T(8,128)(2,1)}), bf16[128,16,512]{2,0,1:T(8,128)(2,1)S(1)}, u32[]{:S(2)}, u32[]{:S(2)}) %all-to-all-start.1) | async-done | bytes 2097184 | tf_op jit(solution)/shard_map/all_to_all | solution.py:42
  187.5 2.1 reshape.46
  189.8 15.6 %while.20 = (s32[]{:T(128)}, f32[4,128,128]{2,1,0:T(8,128)S(1)}, s32[]{:T(128)}, f32[16,4,128,128]{3,2,1,0:T(8,128)}, s32[]{:T(128)}, /*index=5*/s32[]{:T(128)}, s32[]{:T(128)}) while((s32[]{:T(128)}, f32[4,128,128]{2,1,0:T(8,128)S(1)}, s32[]{:T(128)}, f32[16,4,128,128]{3,2,1,0:T(8,128)}, s32[]{:T(128)}, /*index=5*/s32[]{:T(128)}, ...), condition=%wide.region_2.3_spmd, body=%wide.region_1.2_spmd.sunk | while | flops 65541 | bytes 786547 | solution.py:18
  205.5 25.7 %while.21 = (s32[]{:T(128)}, bf16[4,512,4,128]{3,2,1,0:T(4,128)(2,1)}, bf16[4,512,4,128]{3,2,1,0:T(4,128)(2,1)}, bf16[4,512,4,128]{3,2,1,0:T(4,128)(2,1)}, bf16[...) while((s32[]{:T(128)}, bf16[4,512,4,128]{3,2,1,0:T(4,128)(2,1)}, ...), condition=%wide.region_5.6_spmd, body=%wide.region_4.5_spmd.sunk | while | flops 606863360 | bytes 15860369 | solution.py:61
  205.6 1.8 constant_dynamic-slice_fusion.5
  231.3 4.1 %all_to_all.55 = bf16[16,128,512]{2,1,0:T(8,128)(2,1)} reshape(bf16[4,512,4,128]{3,2,1,0:T(4,128)(2,1)} %get-tuple-element.61) | data formatting | bytes 4194304 | tf_op jit(solution)/shard_map/all_to_all | solution.py:63
  235.4 5.0 %all-to-all-start.3 = ((bf16[16,128,512]{2,1,0:T(8,128)(2,1)}), bf16[16,128,512]{2,1,0:T(8,128)(2,1)S(1)}, u32[]{:S(2)}, u32[]{:S(2)}) async-start(bf16[16,128,512]{2,1,0:T(8,128)(2,1)} %all_to_all.55), calls=%async_computation.3 | async-start | bytes 4194304 | tf_op jit(solution)/shard_map/all_to_all | solution.py:63
  240.4 4.1 %copy.42 = bf16[128,8192]{0,1:T(8,128)(2,1)} copy(bf16[128,8192]{1,0:T(8,128)(2,1)} %param.12) | data formatting | bytes 4194304 | tf_op args[3]
  244.5 44.9 %all-to-all-done.3 = bf16[16,128,512]{2,1,0:T(8,128)(2,1)S(1)} async-done(((bf16[16,128,512]{2,1,0:T(8,128)(2,1)}), bf16[16,128,512]{2,1,0:T(8,128)(2,1)S(1)}, u32[]{:S(2)}, u32[]{:S(2)}) %all-to-all-start.3) | async-done | bytes 2097184 | tf_op jit(solution)/shard_map/all_to_all | solution.py:63
  289.3 2.5 convert_bitcast_fusion
  291.8 5.4 %copy.41 = f32[128,16,512]{0,2,1:T(8,128)} copy(f32[128,16,512]{2,0,1:T(8,128)} %convert_bitcast_fusion) | data formatting | bytes 8388608 | tf_op jit(solution)/shard_map/convert_element_type | solution.py:63
  298.8 5.0 %fusion.13 = bf16[128,8192]{0,1:T(8,128)(2,1)S(1)} fusion(f32[128,16,512]{0,2,1:T(8,128)} %copy.41, bf16[128,8192]{0,1:T(8,128)(2,1)S(1)} %copy-done.2, f32[8192]{0:T(1024)S(1)} %convert_element_type.39, f32[128]{0:T(128)S(1)} %add_rsqrt_fusion), kind=kLoop, calls=%fused_computation.25 | loop fusion | flops 8388608 | bytes 8421888 | tf_op jit(solution)/shard_map/convert_element_type | solution.py:69
  303.8 2.9 copy.43
  (80 shorter events, 42.1 us)
Async XLA Ops:
  9.7 58.1 %all-to-all-start = ((bf16[128,16,512]{2,0,1:T(8,128)(2,1)}), bf16[128,16,512]{2,0,1:T(8,128)(2,1)S(1)}, u32[]{:S(2)}, u32[]{:S(2)}) async-start(bf16[128,16,512]{2,0,1:T(8,128)(2,1)} %bitcast.66), calls=%async_computation | async-start | bytes 4194304 | tf_op jit(solution)/shard_map/all_to_all | solution.py:44
  67.8 1.3 copy-start.1
  69.1 54.0 %all-to-all-start.2 = ((bf16[128,16,512]{2,0,1:T(8,128)(2,1)}), bf16[128,16,512]{2,0,1:T(8,128)(2,1)}, u32[]{:S(2)}, u32[]{:S(2)}) async-start(bf16[128,16,512]{2,0,1:T(8,128)(2,1)} %bitcast.65), calls=%async_computation.2 | async-start | bytes 4194304 | tf_op jit(solution)/shard_map/all_to_all | solution.py:43
  74.1 115.7 %all-gather.3.cloned.1.call-start = ((), (), s32[]{:S(2)}) async-start(), calls=%async_computation.4 | async-start | bytes 4456448 | tf_op jit(solution)/shard_map/all_gather | solution.py:12
  76.7 50.5 %copy-start = (bf16[4,512,4,128]{3,2,1,0:T(4,128)(2,1)}, bf16[4,512,4,128]{3,2,1,0:T(4,128)(2,1)S(1)}, u32[]{:S(2)}) copy-start(bf16[4,512,4,128]{3,2,1,0:T(4,128)(2,1)S(1)} %reshape.45) | copy-start | bytes 6291460
  133.6 53.9 %all-to-all-start.1 = ((bf16[128,16,512]{2,0,1:T(8,128)(2,1)}), bf16[128,16,512]{2,0,1:T(8,128)(2,1)S(1)}, u32[]{:S(2)}, u32[]{:S(2)}) async-start(bf16[128,16,512]{2,0,1:T(8,128)(2,1)} %bitcast.64), calls=%async_computation.1 | async-start | bytes 4194304 | tf_op jit(solution)/shard_map/all_to_all | solution.py:42
  205.5 2.1 copy-start.3
  210.7 1.3 copy-start.4
  212.0 2.1 copy-start.3
  217.1 1.3 copy-start.4
  218.4 2.1 copy-start.3
  223.5 1.3 copy-start.4
  224.8 2.1 copy-start.3
  230.0 1.3 copy-start.4
  235.4 53.9 %all-to-all-start.3 = ((bf16[16,128,512]{2,1,0:T(8,128)(2,1)}), bf16[16,128,512]{2,1,0:T(8,128)(2,1)S(1)}, u32[]{:S(2)}, u32[]{:S(2)}) async-start(bf16[16,128,512]{2,1,0:T(8,128)(2,1)} %all_to_all.55), calls=%async_computation.3 | async-start | bytes 4194304 | tf_op jit(solution)/shard_map/all_to_all | solution.py:63
  240.4 4.1 %copy-start.5 = (bf16[8192]{0:T(1024)(128)(2,1)S(1)}, bf16[8192]{0:T(1024)(128)(2,1)}, u32[]{:S(2)}) copy-start(bf16[8192]{0:T(1024)(128)(2,1)} %param.13) | copy-start | bytes 49156
  297.2 1.6 copy-start.2
Sparse Core Ops, SparseCore 0:
  130.5 53.1 all-gather.2
where the time goes:
time: 315 us; the launch traced here: 314 us
  waiting for transfers between devices  186 us (59%)
  local copies, waits for them, and re-layouts  55.4 us (18%)
  starting transfers between devices  24.1 us (8%)
  other arithmetic  23.7 us (8%)
  between operations  13.5 us (4%)
  matrix products  10 us (3%)
    all_to_all x1, waiting for transfers between devices, on_device(): lax.all_to_all(queries, 'head', split_axis=1, concat_axis=0, tiled=True)  48.9 us
    all_to_all x1, waiting for transfers between devices, on_device(): lax.all_to_all(key_vectors, 'head', split_axis=1, concat_axis=0, tiled=True)  46.4 us
    all_to_all x1, waiting for transfers between devices, on_device(): lax.all_to_all(values, 'head', split_axis=1, concat_axis=0, tiled=True)  45.8 us
    all_to_all x1, waiting for transfers between devices, on_device(): lax.all_to_all(attended, 'head', split_axis=0, concat_axis=1, tiled=True)  44.9 us
    add x15, other arithmetic, one(): return combine(state, lax.dynamic_index_in_dim(gathered, lap, 0, False))  15.2 us
    dynamic_slice x12, local copies, waits for them, and re-layouts, on_device(): lax.map(block_output, (query_blocks, key_blocks, value_blocks, prefix_blo...  13.2 us
    all_to_all x1, starting transfers between devices, on_device(): lax.all_to_all(values, 'head', split_axis=1, concat_axis=0, tiled=True)  9.15 us
    unnamed x9, local copies, waits for them, and re-layouts  6.49 us
  transfers between devices with their start and end apart: 5, of which 4 were waited for; matrix products, arithmetic and copies ran while one was open for 5% of the time, Pallas kernels for 0%

commit v1 on v0

v1 whole, which is shorter than its diff:
```python
import jax
import jax.numpy as jnp
from jax import lax
from jax.sharding import Mesh
from jax.sharding import PartitionSpec as P

E = 128
SWAP = [(0, 1), (1, 0)]


def on_device(queries, key_vectors, values, gate_logits, norm_gain):
    tokens = queries.shape[0]
    heads = queries.shape[1] // E
    chips = lax.axis_size("z")
    core = lax.axis_index("core")
    shard = lax.axis_index("seq")
    query_heads = queries.reshape(tokens, heads, E)
    key_heads = key_vectors.reshape(tokens, heads, E)
    value_heads = values.reshape(tokens, heads, E)

    state = jnp.einsum("the,thf->hef", key_heads, value_heads, preferred_element_type=jnp.float32)

    scores = jnp.einsum("the,she->hts", query_heads, key_heads, preferred_element_type=jnp.float32)
    lower_mask = lax.broadcasted_iota(jnp.int32, (tokens, tokens), 0) >= lax.broadcasted_iota(
        jnp.int32, (tokens, tokens), 1
    )
    weights = jnp.where(lower_mask[None], scores, 0.0).astype(jnp.bfloat16)
    local_part = jnp.einsum("hts,she->the", weights, value_heads, preferred_element_type=jnp.float32)

    other_state = lax.ppermute(state, "core", SWAP)
    chip_state = state + other_state
    half = lax.dynamic_index_in_dim(chip_state.reshape(2, heads // 2, E, E), core, 0, False)
    pieces = half.reshape(chips, heads // 2 // chips, E, E).astype(jnp.bfloat16)
    by_chip = lax.all_to_all(pieces, "z", 0, 0, tiled=True).astype(jnp.float32)

    shard_total = jnp.sum(by_chip, axis=0)
    totals = lax.all_gather(shard_total, "seq")
    earlier = (lax.broadcasted_iota(jnp.int32, (totals.shape[0], 1, 1, 1), 0) < shard).astype(jnp.float32)
    entering = jnp.sum(totals * earlier, axis=0)
    within = jnp.cumsum(by_chip, axis=0) - by_chip
    prefix_pieces = (entering[None] + within).astype(jnp.bfloat16)

    own_half = lax.all_to_all(prefix_pieces, "z", 0, 0, tiled=True).reshape(heads // 2, E, E)
    other_half = lax.ppermute(own_half, "core", SWAP)
    first = core == 0
    prefix = jnp.concatenate(
        [jnp.where(first, own_half, other_half), jnp.where(first, other_half, own_half)], axis=0
    )
    before_me = jnp.where(first, 0.0, other_state).astype(jnp.bfloat16)

    carried_part = jnp.einsum("the,hef->thf", query_heads, prefix, preferred_element_type=jnp.float32)
    carried_part += jnp.einsum("the,hef->thf", query_heads, before_me, preferred_element_type=jnp.float32)
    attended = (local_part + carried_part).astype(jnp.bfloat16).reshape(tokens, heads * E)

    features = attended.astype(jnp.float32)
    mean_square = jnp.mean(features * features, axis=1, keepdims=True)
    scaled = features * lax.rsqrt(mean_square + 1e-06) * norm_gain.astype(jnp.float32)[None, :]
    scaled = scaled * jax.nn.sigmoid(gate_logits.astype(jnp.float32))
    return scaled.astype(jnp.bfloat16)


def solution(mesh):
    seq = mesh.shape["seq"]
    cores = 2
    chips = mesh.shape["head"] // cores
    split = Mesh(mesh.devices.reshape(seq, chips, cores), ("seq", "z", "core"))
    rows = P(("seq", "z", "core"), None)
    return jax.shard_map(
        on_device,
        mesh=split,
        in_specs=(rows, rows, rows, rows, P()),
        out_specs=rows,
        check_vma=False,
    )
```

time: 315 us -> 197 us (0.63)
  the two profiles are of different devices: /device:TPU:31 before, /device:TPU:1 now
where the time goes in v1:
time: 197 us; the launch traced here: 196 us
  blocking collectives  68.1 us (35%)
  waiting for transfers between devices  61.2 us (31%)
  matrix products  18.7 us (9%)
  other arithmetic  15.3 us (8%)
  local copies, waits for them, and re-layouts  13.9 us (7%)
  between operations  13.5 us (7%)
  starting transfers between devices  5.69 us (3%)
    all_gather x1, waiting for transfers between devices, on_device(): totals = lax.all_gather(shard_total, 'seq')  54.1 us
    all_to_all x1, blocking collectives, on_device(): by_chip = lax.all_to_all(pieces, 'z', 0, 0, tiled=True).astype(jnp.float32)  34.4 us
    all_to_all x1, blocking collectives, on_device(): lax.all_to_all(prefix_pieces, 'z', 0, 0, tiled=True)  33.8 us
    ppermute x1, waiting for transfers between devices, on_device(): other_state = lax.ppermute(state, 'core', SWAP)  7.13 us
    dot_general x1, matrix products, on_device(): jnp.einsum('hts,she->the', weights, value_heads, preferred_element_type=j...  6.35 us
    convert_element_type x1, local copies, waits for them, and re-layouts, on_device(): features = attended.astype(jnp.float32)  5.65 us
    convert_element_type x1, other arithmetic, on_device(): return scaled.astype(jnp.bfloat16)  5.32 us
    dot_general x1, matrix products, on_device(): jnp.einsum('the,thf->hef', key_heads, value_heads, preferred_element_type...  4.9 us
  transfers between devices with their start and end apart: 3, of which 2 were waited for; matrix products, arithmetic and copies ran while one was open for 5% of the time, Pallas kernels for 0%

profile of v1, /device:TPU:1, one launch (start us, length us, event | category | flops | bytes accessed | tf_op | source)
XLA Modules:
  0.0 196.5 jit_solution(17251080674852763775)
XLA Ops:
  6.5 4.2 %copy.36 = bf16[128,8192]{0,1:T(8,128)(2,1)} copy(bf16[128,8192]{1,0:T(8,128)(2,1)} %param.6) | data formatting | bytes 4194304 | tf_op jit(solution)/shard_map/reshape | solution.py:18
  10.8 4.9 %fusion.8 = f32[64,128,128]{2,1,0:T(8,128)} fusion(bf16[128,64,128]{0,2,1:T(8,128)(2,1)} %bitcast.56, bf16[128,8192]{1,0:T(8,128)(2,1)} %param.7), kind=kOutput, calls=%fused_computation.16 | convolution fusion | flops 268435456 | bytes 8388608 | tf_op jit(solution)/shard_map/the,thf->hef/dot_general | solution.py:21
  15.7 3.2 %collective-permute-start = (f32[64,128,128]{2,1,0:T(8,128)}, f32[64,128,128]{2,1,0:T(8,128)}, u32[]{:S(2)}, u32[]{:S(2)}) collective-permute-start(f32[64,128,128]{2,1,0:T(8,128)} %fusion.8), channel_id=1, source_target_pairs={{0,1},{1,0},{2,3},{3,2},{4,5},{5,4},{6,7},{7,6},{8,9},{9,8},{10,11... | collective-permute-start | bytes 12582920 | tf_op jit(solution)/shard_map/ppermute | solution.py:30
  18.9 7.1 %collective-permute-done = f32[64,128,128]{2,1,0:T(8,128)} collective-permute-done((f32[64,128,128]{2,1,0:T(8,128)}, f32[64,128,128]{2,1,0:T(8,128)}, u32[]{:S(2)}, u32[]{:S(2)}) %collective-permute-start) | collective-permute-done | bytes 4194336 | tf_op jit(solution)/shard_map/ppermute | solution.py:30
  26.0 4.4 %add.38 = bf16[64,128,128]{2,1,0:T(8,128)(2,1)S(1)} add(f32[64,128,128]{2,1,0:T(8,128)} %fusion.8, f32[64,128,128]{2,1,0:T(8,128)} %collective-permute-done) | non-fusion elementwise | flops 1048576 | bytes 10485760 | tf_op jit(solution)/shard_map/add | solution.py:31
  30.4 0.1 dynamic-slice_convert_fusion
  30.5 1.3 copy.28
  31.8 34.4 %all_to_all.10 = bf16[8,4,128,128]{2,3,1,0:T(8,128)(2,1)S(1)} all-to-all(bf16[8,4,128,128]{2,3,1,0:T(8,128)(2,1)} %bitcast.62), channel_id=1, replica_groups=mesh['seq'=16,'z'=8,'core'=2] {'z'}, dimensions={0} | all-to-all | bytes 2097152 | tf_op jit(solution)/shard_map/all_to_all | solution.py:34
  66.2 0.1 convert_reduce_fusion
  66.3 0.8 copy.29
  67.2 0.0 all-gather.3.cloned.1.call-update
  67.2 54.1 %all-gather.3.cloned.1.call-done = f32[64,128,128]{2,1,0:T(8,128)} async-done(((f32[4,128,128]{2,1,0:T(8,128)}), f32[64,128,128]{2,1,0:T(8,128)}) %all-gather.3.cloned.1.call-update) | async-done | bytes 4194320 | tf_op jit(solution)/shard_map/all_gather | solution.py:37
  121.3 2.6 %multiply_reduce_fusion.1 = f32[4,128,128]{2,1,0:T(8,128)S(1)} fusion(f32[16,4,128,128]{3,2,1,0:T(8,128)} %bitcast.61, f32[16]{0:T(128)S(1)} %compare_convert_fusion), kind=kLoop, calls=%fused_computation.5 | loop fusion | flops 2031616 | bytes 4456512 | tf_op jit(solution)/shard_map/reduce_sum | solution.py:39
  124.0 0.8 copy.30
  124.8 1.3 fusion.4
  126.1 33.8 %all_to_all.11 = bf16[8,4,128,128]{2,3,1,0:T(8,128)(2,1)S(1)} all-to-all(bf16[8,4,128,128]{2,3,1,0:T(8,128)(2,1)S(1)} %fusion.4), channel_id=1, replica_groups=mesh['seq'=16,'z'=8,'core'=2] {'z'}, dimensions={0} | all-to-all | bytes 2097152 | tf_op jit(solution)/shard_map/all_to_all | solution.py:43
  159.9 2.5 %collective-permute-start.1 = (bf16[32,128,128]{1,2,0:T(8,128)(2,1)S(1)}, bf16[32,128,128]{1,2,0:T(8,128)(2,1)}, u32[]{:S(2)}, u32[]{:S(2)}) collective-permute-start(bf16[32,128,128]{1,2,0:T(8,128)(2,1)S(1)} %bitcast.60), channel_id=1, source_target_pairs={{0,1},{1,0},{2,3},{3,2},{4,5},{5,4},{6,7},{7,6},{8,9},{9,8},{10,11... | collective-permute-start | bytes 3145736 | tf_op jit(solution)/shard_map/ppermute | solution.py:44
  162.4 6.3 %fusion.6 = f32[64,128,128]{1,2,0:T(8,128)} fusion(bf16[128,64,128]{0,2,1:T(8,128)(2,1)} %bitcast.57, pred[128,128]{1,0:T(8,128)(4,1)S(1)} %iota_compare_fusion, bf16[128,8192]{1,0:T(8,128)(2,1)} %param.7, bf16[128,8192]{1,0:T(8,128)(2,1)S(1)} %copy-done), kind=kOutput, calls=%fused_computation.14 | convolution fusion | flops 538968064 | bytes 10502144 | tf_op jit(solution)/shard_map/hts,she->the/dot_general | solution.py:28
  168.7 3.8 %fusion.5 = f32[64,128,128]{2,1,0:T(8,128)S(1)} fusion(f32[64,128,128]{2,1,0:T(8,128)} %collective-permute-done, pred[]{:T(512)S(6)} %eq.3, bf16[128,8192]{1,0:T(8,128)(2,1)S(1)} %copy-done), kind=kOutput, calls=%fused_computation.13 | convolution fusion | flops 269484032 | bytes 10485761 | tf_op jit(solution)/shard_map/the,hef->thf/dot_general | solution.py:52
  172.5 1.5 broadcast_select_fusion.1
  174.1 1.0 copy-done.1
  175.0 3.6 %multiply_reduce_fusion = (f32[128]{0:T(128)S(1)}, f32[128,64,128]{0,2,1:T(8,128)}) fusion(f32[64,128,128]{2,1,0:T(8,128)S(1)} %fusion.5, bf16[32,128,128]{1,2,0:T(8,128)(2,1)S(1)} %get-tuple-element.6, bf16[32,128,128]{1,2,0:T(8,128)(2,1)S(1)} %get-tuple-element.5, f32[64,128,128]{1,2,0:T(8,128)S(1)} %copy-done.1, bf16[128,8192]{1,0:T(8,128)(2,1)S(1)} %copy-done), kind=kOutput, calls=%fused_computation.3 | convolution fusion | flops 275775360 | bytes 16777728 | tf_op jit(solution)/shard_map/the,hef->thf/dot_general | solution.py:51
  178.7 5.6 %copy.34 = f32[128,8192]{1,0:T(8,128)} copy(f32[128,8192]{0,1:T(8,128)} %bitcast.58) | data formatting | bytes 8388608 | tf_op jit(solution)/shard_map/convert_element_type | solution.py:55
  184.3 5.3 %multiply_convert_fusion = bf16[128,8192]{1,0:T(8,128)(2,1)} fusion(bf16[128,8192]{1,0:T(8,128)(2,1)} %param.8, f32[128,8192]{1,0:T(8,128)} %copy.34, f32[8192]{0:T(1024)S(1)} %convert_element_type.58, f32[128]{0:T(128)S(1)} %add_rsqrt_fusion), kind=kLoop, calls=%fused_computation.2 | loop fusion | flops 8388608 | bytes 8421888 | tf_op jit(solution)/shard_map/convert_element_type | solution.py:59
  (11 shorter events, 0.0 us)
Async XLA Ops:
  6.5 155.8 %copy-start = (bf16[128,8192]{1,0:T(8,128)(2,1)S(1)}, bf16[128,8192]{1,0:T(8,128)(2,1)}, u32[]{:S(2)}) copy-start(bf16[128,8192]{1,0:T(8,128)(2,1)} %param.5) | copy-start | bytes 6291460
  6.5 114.8 %all-gather.3.cloned.1.call-start = ((), (), s32[]{:S(2)}) async-start(), calls=%async_computation.2 | async-start | bytes 4456448 | tf_op jit(solution)/shard_map/all_gather | solution.py:37
  15.7 10.4 %collective-permute-start = (f32[64,128,128]{2,1,0:T(8,128)}, f32[64,128,128]{2,1,0:T(8,128)}, u32[]{:S(2)}, u32[]{:S(2)}) collective-permute-start(f32[64,128,128]{2,1,0:T(8,128)} %fusion.8), channel_id=1, source_target_pairs={{0,1},{1,0},{2,3},{3,2},{4,5},{5,4},{6,7},{7,6},{8,9},{9,8},{10,11... | collective-permute-start | bytes 12582920 | tf_op jit(solution)/shard_map/ppermute | solution.py:30
  124.8 37.6 %copy-start.2 = (bf16[8192]{0:T(1024)(128)(2,1)S(1)}, bf16[8192]{0:T(1024)(128)(2,1)}, u32[]{:S(2)}) copy-start(bf16[8192]{0:T(1024)(128)(2,1)} %param.9) | copy-start | bytes 49156
  159.9 12.7 %collective-permute-start.1 = (bf16[32,128,128]{1,2,0:T(8,128)(2,1)S(1)}, bf16[32,128,128]{1,2,0:T(8,128)(2,1)}, u32[]{:S(2)}, u32[]{:S(2)}) collective-permute-start(bf16[32,128,128]{1,2,0:T(8,128)(2,1)S(1)} %bitcast.60), channel_id=1, source_target_pairs={{0,1},{1,0},{2,3},{3,2},{4,5},{5,4},{6,7},{7,6},{8,9},{9,8},{10,11... | collective-permute-start | bytes 3145736 | tf_op jit(solution)/shard_map/ppermute | solution.py:44
  172.5 2.5 %copy-start.1 = (f32[64,128,128]{1,2,0:T(8,128)S(1)}, f32[64,128,128]{1,2,0:T(8,128)}, u32[]{:S(2)}) copy-start(f32[64,128,128]{1,2,0:T(8,128)} %fusion.6) | copy-start | bytes 12582916
Sparse Core Ops, SparseCore 0:
  67.3 53.9 all-gather.2

commit v2 on v1

v2 whole, which is shorter than its diff:
```python
import jax
import jax.numpy as jnp
from jax import lax
from jax.sharding import PartitionSpec as P

E = 128


def on_device(queries, key_vectors, values, gate_logits, norm_gain):
    tokens = queries.shape[0]
    heads = queries.shape[1] // E
    chips = lax.axis_size("head") // 2
    core = lax.axis_index("head") % 2
    pieces_of = heads // 2 // chips
    pairs = [(h, h ^ 1) for h in range(2 * chips)]
    query_heads = queries.reshape(tokens, heads, E)
    key_heads = key_vectors.reshape(tokens, heads, E)
    value_heads = values.reshape(tokens, heads, E)

    state = jnp.einsum("the,thf->hef", key_heads, value_heads, preferred_element_type=jnp.float32)

    scores = jnp.einsum("the,she->hts", query_heads, key_heads, preferred_element_type=jnp.float32)
    lower_mask = lax.broadcasted_iota(jnp.int32, (tokens, tokens), 0) >= lax.broadcasted_iota(
        jnp.int32, (tokens, tokens), 1
    )
    weights = jnp.where(lower_mask[None], scores, 0.0).astype(jnp.bfloat16)
    local_part = jnp.einsum("hts,she->the", weights, value_heads, preferred_element_type=jnp.float32)

    other_state = lax.ppermute(state, "head", pairs)
    chip_state = (state + other_state).reshape(2, chips, pieces_of, 2, E // 2, E)
    my_rows = lax.dynamic_index_in_dim(chip_state, core, 3, False)
    outgoing = jnp.swapaxes(my_rows, 0, 1).reshape(2 * chips, pieces_of, E // 2, E)
    incoming = lax.all_to_all(outgoing.astype(jnp.bfloat16), "head", 0, 0, tiled=True)
    by_chip = jnp.swapaxes(incoming.reshape(chips, 2, pieces_of, E // 2, E), 1, 2)
    by_chip = by_chip.reshape(chips, pieces_of, E, E).astype(jnp.float32)

    shard_total = jnp.sum(by_chip, axis=0)
    shards = lax.axis_size("seq")
    parts = jnp.swapaxes(shard_total.reshape(pieces_of, shards, E // shards, E), 0, 1)
    per_shard = lax.all_to_all(parts, "seq", 0, 0, tiled=True)
    running = jnp.cumsum(per_shard, axis=0)
    before = jnp.concatenate([jnp.zeros_like(running[:1]), running[:-1]], axis=0)
    entering = lax.all_to_all(before, "seq", 0, 0, tiled=True)
    entering = jnp.swapaxes(entering, 0, 1).reshape(pieces_of, E, E)

    running = jnp.cumsum(by_chip, axis=0)
    within = jnp.concatenate([jnp.zeros_like(running[:1]), running[:-1]], axis=0)
    prefix_pieces = (entering[None] + within).astype(jnp.bfloat16)
    outgoing = jnp.swapaxes(prefix_pieces.reshape(chips, pieces_of, 2, E // 2, E), 1, 2)
    outgoing = outgoing.reshape(2 * chips, pieces_of, E // 2, E)
    returned = lax.all_to_all(outgoing, "head", 0, 0, tiled=True)
    own_rows = jnp.swapaxes(returned.reshape(chips, 2, pieces_of, E // 2, E), 0, 1)
    own_rows = own_rows.reshape(heads, E // 2, E)
    other_rows = lax.ppermute(own_rows, "head", pairs)
    first = core == 0
    prefix = jnp.concatenate(
        [jnp.where(first, own_rows, other_rows), jnp.where(first, other_rows, own_rows)], axis=1
    )
    before_me = jnp.where(first, 0.0, other_state).astype(jnp.bfloat16)

    carried_part = jnp.einsum("the,hef->thf", query_heads, prefix, preferred_element_type=jnp.float32)
    carried_part += jnp.einsum("the,hef->thf", query_heads, before_me, preferred_element_type=jnp.float32)
    attended = (local_part + carried_part).astype(jnp.bfloat16).reshape(tokens, heads * E)

    features = attended.astype(jnp.float32)
    mean_square = jnp.mean(features * features, axis=1, keepdims=True)
    scaled = features * lax.rsqrt(mean_square + 1e-06) * norm_gain.astype(jnp.float32)[None, :]
    scaled = scaled * jax.nn.sigmoid(gate_logits.astype(jnp.float32))
    return scaled.astype(jnp.bfloat16)


def solution(mesh):
    rows = P(("seq", "head"), None)
    return jax.shard_map(
        on_device,
        mesh=mesh,
        in_specs=(rows, rows, rows, rows, P()),
        out_specs=rows,
        check_vma=False,
    )
```

time: 197 us -> 166 us (0.84)
  waiting for transfers between devices: 61.2 us -> 16.6 us
  between operations: 13.5 us -> 0.15 us
  local copies, waits for them, and re-layouts: 13.9 us -> 24.5 us
  starting transfers between devices: 5.69 us -> 13.5 us
  other arithmetic: 15.3 us -> 21.8 us
    all_gather x1 -> x0, waiting for transfers between devices: 54.1 us -> none  [on_device(): totals = lax.all_gather(shard_total, 'seq')]
    all_to_all x0 -> x2, starting transfers between devices: none -> 10.3 us  [the longest x1 6.75 us: on_device(): per_shard = lax.all_to_all(parts, 'seq', 0, 0, tiled=True)]
    all_to_all x0 -> x2, waiting for transfers between devices: none -> 9.44 us  [the longest x1 5.03 us: on_device(): per_shard = lax.all_to_all(parts, 'seq', 0, 0, tiled=True)]
    convert_element_type x1 -> x2, other arithmetic: 0.01 us -> 3.36 us  [the longest x1 1.78 us: on_device(): prefix_pieces = (entering[None] + within).astype(jnp.bfloat16)]
    another operation x1 -> x2, other arithmetic: 1.3 us -> 4.26 us  [the longest x1 2.49 us: on_device(): running = jnp.cumsum(per_shard, axis=0)]
    reshape x0 -> x1, local copies, waits for them, and re-layouts: none -> 2.72 us  [on_device(): own_rows = own_rows.reshape(heads, E // 2, E)]
    reduce_sum x1 -> x0, other arithmetic: 2.64 us -> none  [on_device(): entering = jnp.sum(totals * earlier, axis=0)]
    transpose x0 -> x2, local copies, waits for them, and re-layouts: none -> 2.52 us  [the longest x1 1.77 us: on_device(): jnp.swapaxes(returned.reshape(chips, 2, pieces_of, E // 2, E), 0, 1)]
  transfers between devices with their start and end apart: 3 -> 4, of which waited for: 2 -> 3; matrix products, arithmetic and copies ran while one was open for 5% -> 11% of each run, Pallas kernels for 0% -> 0%
where the time goes in v2:
time: 166 us; the launch traced here: 165 us
  blocking collectives  68.6 us (41%)
  local copies, waits for them, and re-layouts  24.5 us (15%)
  other arithmetic  21.8 us (13%)
  matrix products  20.2 us (12%)
  waiting for transfers between devices  16.6 us (10%)
  starting transfers between devices  13.5 us (8%)
    all_to_all x1, blocking collectives, on_device(): lax.all_to_all(outgoing.astype(jnp.bfloat16), 'head', 0, 0, tiled=True)  35.5 us
    all_to_all x1, blocking collectives, on_device(): returned = lax.all_to_all(outgoing, 'head', 0, 0, tiled=True)  33.1 us
    ppermute x1, waiting for transfers between devices, on_device(): other_state = lax.ppermute(state, 'head', pairs)  7.13 us
    all_to_all x1, starting transfers between devices, on_device(): per_shard = lax.all_to_all(parts, 'seq', 0, 0, tiled=True)  6.75 us
    dot_general x1, matrix products, on_device(): jnp.einsum('hts,she->the', weights, value_heads, preferred_element_type=j...  6.34 us
    dot_general x1, matrix products, on_device(): jnp.einsum('the,hef->thf', query_heads, before_me, preferred_element_type...  5.76 us
    convert_element_type x1, local copies, waits for them, and re-layouts, on_device(): features = attended.astype(jnp.float32)  5.59 us
    convert_element_type x1, other arithmetic, on_device(): return scaled.astype(jnp.bfloat16)  5.32 us
  transfers between devices with their start and end apart: 4, of which 3 were waited for; matrix products, arithmetic and copies ran while one was open for 11% of the time, Pallas kernels for 0%

profile of v2, /device:TPU:1, one launch (start us, length us, event | category | flops | bytes accessed | tf_op | source)
XLA Modules:
  0.0 165.3 jit_solution(1804036789340136867)
XLA Ops:
  0.0 4.2 %copy.45 = bf16[128,8192]{0,1:T(8,128)(2,1)} copy(bf16[128,8192]{1,0:T(8,128)(2,1)} %param.6) | data formatting | bytes 4194304 | tf_op jit(solution)/shard_map/reshape | solution.py:17
  4.2 4.9 %fusion.4 = f32[64,128,128]{2,1,0:T(8,128)} fusion(bf16[128,64,128]{0,2,1:T(8,128)(2,1)} %bitcast.80, bf16[128,8192]{1,0:T(8,128)(2,1)} %param.7), kind=kOutput, calls=%fused_computation.9 | convolution fusion | flops 268435456 | bytes 8388608 | tf_op jit(solution)/shard_map/the,thf->hef/dot_general | solution.py:20
  9.1 3.2 %collective-permute-start = (f32[64,128,128]{2,1,0:T(8,128)}, f32[64,128,128]{2,1,0:T(8,128)}, u32[]{:S(2)}, u32[]{:S(2)}) collective-permute-start(f32[64,128,128]{2,1,0:T(8,128)} %fusion.4), channel_id=1, source_target_pairs={{0,1},{1,0},{2,3},{3,2},{4,5},{5,4},{6,7},{7,6},{8,9},{9,8},{10,11... | collective-permute-start | bytes 12582920 | tf_op jit(solution)/shard_map/ppermute | solution.py:29
  12.3 7.1 %collective-permute-done = f32[64,128,128]{2,1,0:T(8,128)} collective-permute-done((f32[64,128,128]{2,1,0:T(8,128)}, f32[64,128,128]{2,1,0:T(8,128)}, u32[]{:S(2)}, u32[]{:S(2)}) %collective-permute-start) | collective-permute-done | bytes 4194336 | tf_op jit(solution)/shard_map/ppermute | solution.py:29
  19.5 4.4 %add.49 = bf16[64,128,128]{2,1,0:T(8,128)(2,1)S(1)} add(f32[64,128,128]{2,1,0:T(8,128)} %fusion.4, f32[64,128,128]{2,1,0:T(8,128)} %collective-permute-done) | non-fusion elementwise | flops 1048576 | bytes 10485760 | tf_op jit(solution)/shard_map/add | solution.py:30
  24.0 35.5 %all_to_all.20 = bf16[16,4,64,128]{3,2,1,0:T(8,128)(2,1)S(1)} all-to-all(bf16[16,4,64,128]{3,2,1,0:T(8,128)(2,1)S(1)} %bitcast.88), channel_id=1, replica_groups=mesh['seq'=16,'head'=16] {'head'}, dimensions={0} | all-to-all | bytes 2097152 | tf_op jit(solution)/shard_map/all_to_all | solution.py:33
  63.6 6.8 %all-to-all-start.1 = ((f32[16,4,8,128]{3,2,1,0:T(8,128)}), f32[16,4,8,128]{3,2,1,0:T(8,128)S(1)}, u32[]{:S(2)}, u32[]{:S(2)}) async-start(f32[16,4,8,128]{3,2,1,0:T(8,128)} %copy.32), calls=%async_computation.1 | async-start | bytes 524288 | tf_op jit(solution)/shard_map/all_to_all | solution.py:40
  70.4 3.2 %copy.34 = f32[8,2,4,64,128]{4,3,1,2,0:T(8,128)} copy(f32[8,2,4,64,128]{4,3,2,1,0:T(8,128)} %bitcast_convert_fusion) | data formatting | bytes 4194304 | tf_op jit(solution)/shard_map/convert_element_type | solution.py:35
  73.5 5.0 %all-to-all-done.1 = f32[16,4,8,128]{3,2,1,0:T(8,128)S(1)} async-done(((f32[16,4,8,128]{3,2,1,0:T(8,128)}), f32[16,4,8,128]{3,2,1,0:T(8,128)S(1)}, u32[]{:S(2)}, u32[]{:S(2)}) %all-to-all-start.1) | async-done | bytes 262176 | tf_op jit(solution)/shard_map/all_to_all | solution.py:40
  78.6 2.5 %fusion.31 = f32[16,4,8,128]{3,2,1,0:T(8,128)S(1)} fusion(f32[16,4,8,128]{3,2,1,0:T(8,128)S(1)} %all-to-all-done.1), kind=kOutput, calls=%fused_computation.39 | output fusion | flops 983040 | bytes 524288 | tf_op jit(solution)/shard_map/jit(cumsum)/reduce_window_sum | solution.py:41
  81.8 3.5 %all-to-all-start.2 = ((f32[16,4,8,128]{3,2,1,0:T(8,128)}), f32[16,4,8,128]{3,2,1,0:T(8,128)S(1)}, u32[]{:S(2)}, u32[]{:S(2)}) async-start(f32[16,4,8,128]{3,2,1,0:T(8,128)} %concatenate.12), calls=%async_computation.2 | async-start | bytes 524288 | tf_op jit(solution)/shard_map/all_to_all | solution.py:43
  85.4 1.8 %fusion.32 = f32[8,4,128,128]{3,2,1,0:T(8,128)S(1)} fusion(f32[8,4,128,128]{3,2,1,0:T(8,128)} %bitcast.84), kind=kOutput, calls=%fused_computation.40 | output fusion | flops 3670016 | bytes 4194304 | tf_op jit(solution)/shard_map/jit(cumsum)/reduce_window_sum | solution.py:46
  88.5 4.4 %all-to-all-done.2 = f32[16,4,8,128]{3,2,1,0:T(8,128)S(1)} async-done(((f32[16,4,8,128]{3,2,1,0:T(8,128)}), f32[16,4,8,128]{3,2,1,0:T(8,128)S(1)}, u32[]{:S(2)}, u32[]{:S(2)}) %all-to-all-start.2) | async-done | bytes 262176 | tf_op jit(solution)/shard_map/all_to_all | solution.py:43
  93.0 1.8 %add_convert_fusion = bf16[8,4,128,128]{3,2,1,0:T(8,128)(2,1)S(1)} fusion(f32[7,4,128,128]{3,2,1,0:T(8,128)} %slice.17, f32[4,128,128]{2,1,0:T(8,128)S(1)} %copy_bitcast_fusion), kind=kLoop, calls=%fused_computation.18 | loop fusion | flops 1048576 | bytes 3145728 | tf_op jit(solution)/shard_map/convert_element_type | solution.py:48
  94.9 33.1 %all_to_all.21 = bf16[16,4,64,128]{3,2,1,0:T(8,128)(2,1)S(1)} all-to-all(bf16[16,4,64,128]{3,2,1,0:T(8,128)(2,1)S(1)} %bitcast.87), channel_id=1, replica_groups=mesh['seq'=16,'head'=16] {'head'}, dimensions={0} | all-to-all | bytes 2097152 | tf_op jit(solution)/shard_map/all_to_all | solution.py:51
  128.0 1.8 %copy.35 = bf16[2,8,4,64,128]{3,4,2,1,0:T(8,128)(2,1)} copy(bf16[2,8,4,64,128]{4,3,2,0,1:T(8,128)(2,1)S(1)} %bitcast.86) | data formatting | bytes 2097152 | tf_op jit(solution)/shard_map/transpose | solution.py:52
  129.8 2.7 %copy.36 = bf16[64,64,128]{2,1,0:T(8,128)(2,1)} copy(bf16[64,64,128]{1,2,0:T(8,128)(2,1)} %bitcast.82) | data formatting | bytes 2097152 | tf_op jit(solution)/shard_map/reshape | solution.py:53
  132.6 6.3 %fusion.2 = f32[64,128,128]{1,2,0:T(8,128)} fusion(bf16[128,64,128]{0,2,1:T(8,128)(2,1)} %bitcast.81, pred[128,128]{1,0:T(8,128)(4,1)S(1)} %iota_compare_fusion, bf16[128,8192]{1,0:T(8,128)(2,1)} %param.7, bf16[128,8192]{1,0:T(8,128)(2,1)S(1)} %copy-done), kind=kOutput, calls=%fused_computation.7 | convolution fusion | flops 538968064 | bytes 10502144 | tf_op jit(solution)/shard_map/hts,she->the/dot_general | solution.py:27
  138.9 5.8 %fusion.1 = f32[64,128,128]{2,1,0:T(8,128)} fusion(f32[64,128,128]{2,1,0:T(8,128)} %collective-permute-done, pred[]{:T(512)S(6)} %eq.5, bf16[128,8192]{1,0:T(8,128)(2,1)S(1)} %copy-done), kind=kOutput, calls=%fused_computation.6 | convolution fusion | flops 269484032 | bytes 10485761 | tf_op jit(solution)/shard_map/the,hef->thf/dot_general | solution.py:62
  144.7 1.8 %copy.37 = bf16[64,64,128]{1,2,0:T(8,128)(2,1)} copy(bf16[64,64,128]{2,1,0:T(8,128)(2,1)S(1)} %collective-permute-done.1) | data formatting | bytes 2097152 | tf_op jit(solution)/shard_map/ppermute | solution.py:54
  146.4 2.6 %broadcast_select_fusion.1 = (bf16[64,64,128]{1,2,0:T(8,128)(2,1)S(1)}, bf16[64,64,128]{1,2,0:T(8,128)(2,1)S(1)}) fusion(bf16[64,64,128]{1,2,0:T(8,128)(2,1)} %copy.37, pred[]{:T(512)S(6)} %eq.5, bf16[2,8,4,64,128]{3,4,2,1,0:T(8,128)(2,1)} %copy.35), kind=kLoop, calls=%fused_computation.22 | loop fusion | flops 1048576 | bytes 4194305 | tf_op jit(solution)/shard_map/jit(_where)/select_n | solution.py:57
  151.2 3.2 %multiply_reduce_fusion = (f32[128]{0:T(128)S(1)}, f32[128,64,128]{0,2,1:T(8,128)}) fusion(f32[64,128,128]{2,1,0:T(8,128)S(1)} %copy-done.2, bf16[64,64,128]{1,2,0:T(8,128)(2,1)S(1)} %get-tuple-element.6, bf16[64,64,128]{1,2,0:T(8,128)(2,1)S(1)} %get-tuple-element.5, f32[64,128,128]{1,2,0:T(8,128)S(1)} %copy-done.1, bf16[128,8192]{1,0:T(8,128)(2,1)S(1)} %copy-done), kind=kOutput, calls=%fused_computation.3 | convolution fusion | flops 278921088 | bytes 16777728 | tf_op jit(solution)/shard_map/the,hef->thf/dot_general | solution.py:61
  154.4 5.6 %copy.42 = f32[128,8192]{1,0:T(8,128)} copy(f32[128,8192]{0,1:T(8,128)} %bitcast.83) | data formatting | bytes 8388608 | tf_op jit(solution)/shard_map/convert_element_type | solution.py:65
  160.0 5.3 %multiply_convert_fusion = bf16[128,8192]{1,0:T(8,128)(2,1)} fusion(bf16[128,8192]{1,0:T(8,128)(2,1)} %param.8, f32[128,8192]{1,0:T(8,128)} %copy.42, f32[8192]{0:T(1024)S(1)} %convert_element_type.75, f32[128]{0:T(128)S(1)} %add_rsqrt_fusion), kind=kLoop, calls=%fused_computation.2 | loop fusion | flops 8388608 | bytes 8421888 | tf_op jit(solution)/shard_map/convert_element_type | solution.py:69
  (25 shorter events, 8.7 us)
Async XLA Ops:
  0.0 132.6 %copy-start = (bf16[128,8192]{1,0:T(8,128)(2,1)S(1)}, bf16[128,8192]{1,0:T(8,128)(2,1)}, u32[]{:S(2)}) copy-start(bf16[128,8192]{1,0:T(8,128)(2,1)} %param.5) | copy-start | bytes 6291460
  9.1 10.4 %collective-permute-start = (f32[64,128,128]{2,1,0:T(8,128)}, f32[64,128,128]{2,1,0:T(8,128)}, u32[]{:S(2)}, u32[]{:S(2)}) collective-permute-start(f32[64,128,128]{2,1,0:T(8,128)} %fusion.4), channel_id=1, source_target_pairs={{0,1},{1,0},{2,3},{3,2},{4,5},{5,4},{6,7},{7,6},{8,9},{9,8},{10,11... | collective-permute-start | bytes 12582920 | tf_op jit(solution)/shard_map/ppermute | solution.py:29
  63.6 15.0 %all-to-all-start.1 = ((f32[16,4,8,128]{3,2,1,0:T(8,128)}), f32[16,4,8,128]{3,2,1,0:T(8,128)S(1)}, u32[]{:S(2)}, u32[]{:S(2)}) async-start(f32[16,4,8,128]{3,2,1,0:T(8,128)} %copy.32), calls=%async_computation.1 | async-start | bytes 524288 | tf_op jit(solution)/shard_map/all_to_all | solution.py:40
  81.8 11.1 %all-to-all-start.2 = ((f32[16,4,8,128]{3,2,1,0:T(8,128)}), f32[16,4,8,128]{3,2,1,0:T(8,128)S(1)}, u32[]{:S(2)}, u32[]{:S(2)}) async-start(f32[16,4,8,128]{3,2,1,0:T(8,128)} %concatenate.12), calls=%async_computation.2 | async-start | bytes 524288 | tf_op jit(solution)/shard_map/all_to_all | solution.py:43
  129.8 2.8 %copy-start.3 = (bf16[8192]{0:T(1024)(128)(2,1)S(1)}, bf16[8192]{0:T(1024)(128)(2,1)}, u32[]{:S(2)}) copy-start(bf16[8192]{0:T(1024)(128)(2,1)} %param.9) | copy-start | bytes 49156
  132.5 12.2 %collective-permute-start.1 = (bf16[64,64,128]{2,1,0:T(8,128)(2,1)}, bf16[64,64,128]{2,1,0:T(8,128)(2,1)S(1)}, u32[]{:S(2)}, u32[]{:S(2)}) collective-permute-start(bf16[64,64,128]{2,1,0:T(8,128)(2,1)} %copy.36), channel_id=1, source_target_pairs={{0,1},{1,0},{2,3},{3,2},{4,5},{5,4},{6,7},{7,6},{8,9},{9,8},{10,11... | collective-permute-start | bytes 3145736 | tf_op jit(solution)/shard_map/ppermute | solution.py:54
  146.4 3.4 %copy-start.1 = (f32[64,128,128]{1,2,0:T(8,128)S(1)}, f32[64,128,128]{1,2,0:T(8,128)}, u32[]{:S(2)}) copy-start(f32[64,128,128]{1,2,0:T(8,128)} %fusion.2) | copy-start | bytes 12582916
  146.4 4.7 %copy-start.2 = (f32[64,128,128]{2,1,0:T(8,128)S(1)}, f32[64,128,128]{2,1,0:T(8,128)}, u32[]{:S(2)}) copy-start(f32[64,128,128]{2,1,0:T(8,128)} %fusion.1) | copy-start | bytes 12582916

commit v3 on v2

v3 whole, which is shorter than its diff:
```python
import jax
import jax.numpy as jnp
from jax import lax
from jax.experimental import pallas as pl
from jax.experimental.pallas import tpu as pltpu
from jax.sharding import PartitionSpec as P

E = 128
GROUP = 8


def state_kernel(key_ref, value_ref, state_ref):
    for j in range(GROUP):
        cols = slice(j * E, (j + 1) * E)
        state_ref[j] = lax.dot_general(
            key_ref[:, cols], value_ref[:, cols], (((0,), (0,)), ((), ())),
            preferred_element_type=jnp.float32,
        )


def block_states(key_vectors, values):
    tokens, width = key_vectors.shape
    heads = width // E
    cols = pl.BlockSpec((tokens, GROUP * E), lambda i: (0, i))
    return pl.pallas_call(
        state_kernel,
        grid=(heads // GROUP,),
        in_specs=[cols, cols],
        out_specs=pl.BlockSpec((GROUP, E, E), lambda i: (i, 0, 0)),
        out_shape=jax.ShapeDtypeStruct((heads, E, E), jnp.float32),
    )(key_vectors, values)


def output_kernel(query_ref, key_ref, value_ref, prefix_ref, before_ref, gate_ref, gain_ref,
                  out_ref, attended_ref, square_ref):
    step = pl.program_id(0)
    tokens = query_ref.shape[0]

    @pl.when(step == 0)
    def _():
        square_ref[...] = jnp.zeros_like(square_ref)

    lower_mask = lax.broadcasted_iota(jnp.int32, (tokens, tokens), 0) >= lax.broadcasted_iota(
        jnp.int32, (tokens, tokens), 1
    )
    for j in range(GROUP):
        cols = slice(j * E, (j + 1) * E)
        query = query_ref[:, cols]
        value = value_ref[:, cols]
        scores = lax.dot_general(
            query, key_ref[:, cols], (((1,), (1,)), ((), ())), preferred_element_type=jnp.float32
        )
        weights = jnp.where(lower_mask, scores, 0.0).astype(jnp.bfloat16)
        total = jnp.dot(weights, value, preferred_element_type=jnp.float32)
        total += jnp.dot(query, prefix_ref[j], preferred_element_type=jnp.float32)
        total += jnp.dot(query, before_ref[j], preferred_element_type=jnp.float32)
        attended = total.astype(jnp.bfloat16)
        start = pl.multiple_of((step * GROUP + j) * E, E)
        attended_ref[:, pl.ds(start, E)] = attended
        features = attended.astype(jnp.float32)
        square_ref[...] += features * features

    @pl.when(step == pl.num_programs(0) - 1)
    def _():
        width = attended_ref.shape[1]
        mean_square = jnp.sum(square_ref[...], axis=1, keepdims=True) / width
        scale = lax.rsqrt(mean_square + 1e-06)

        def chunk(c, carry):
            start = pl.multiple_of(c * E, E)
            window = pl.ds(start, E)
            features = attended_ref[:, window].astype(jnp.float32)
            gain = gain_ref[:, window].astype(jnp.float32)
            gate = gate_ref[:, window].astype(jnp.float32)
            scaled = features * scale * gain
            scaled = scaled * (1.0 / (1.0 + jnp.exp(-gate)))
            out_ref[:, window] = scaled.astype(out_ref.dtype)
            return carry

        lax.fori_loop(0, width // E, chunk, 0)


def gated_attention(queries, key_vectors, values, prefix, before, gate_logits, norm_gain):
    tokens, width = queries.shape
    heads = width // E
    cols = pl.BlockSpec((tokens, GROUP * E), lambda i: (0, i))
    states = pl.BlockSpec((GROUP, E, E), lambda i: (i, 0, 0))
    whole = pl.BlockSpec((tokens, width), lambda i: (0, 0))
    return pl.pallas_call(
        output_kernel,
        grid=(heads // GROUP,),
        in_specs=[cols, cols, cols, states, states, whole, pl.BlockSpec((1, width), lambda i: (0, 0))],
        out_specs=whole,
        out_shape=jax.ShapeDtypeStruct((tokens, width), jnp.bfloat16),
        scratch_shapes=[pltpu.VMEM((tokens, width), jnp.bfloat16), pltpu.VMEM((tokens, E), jnp.float32)],
    )(queries, key_vectors, values, prefix, before, gate_logits, norm_gain.reshape(1, width))


def on_device(queries, key_vectors, values, gate_logits, norm_gain):
    heads = queries.shape[1] // E
    chips = lax.axis_size("head") // 2
    core = lax.axis_index("head") % 2
    pieces_of = heads // 2 // chips
    pairs = [(h, h ^ 1) for h in range(2 * chips)]

    state = block_states(key_vectors, values)

    other_state = lax.ppermute(state, "head", pairs)
    layout = (2, chips, pieces_of, 2, E // 2, E)
    my_rows = lax.dynamic_index_in_dim(state.reshape(layout), core, 3, False) + lax.dynamic_index_in_dim(
        other_state.reshape(layout), core, 3, False
    )
    outgoing = jnp.swapaxes(my_rows, 0, 1).reshape(2 * chips, pieces_of, E // 2, E)
    incoming = lax.all_to_all(outgoing.astype(jnp.bfloat16), "head", 0, 0, tiled=True)
    by_chip = jnp.swapaxes(incoming.reshape(chips, 2, pieces_of, E // 2, E), 1, 2)
    by_chip = by_chip.reshape(chips, pieces_of, E, E).astype(jnp.float32)

    shard_total = jnp.sum(by_chip, axis=0)
    shards = lax.axis_size("seq")
    parts = jnp.swapaxes(shard_total.reshape(pieces_of, shards, E // shards, E), 0, 1)
    per_shard = lax.all_to_all(parts, "seq", 0, 0, tiled=True)
    running = jnp.cumsum(per_shard, axis=0)
    before = jnp.concatenate([jnp.zeros_like(running[:1]), running[:-1]], axis=0)
    entering = lax.all_to_all(before, "seq", 0, 0, tiled=True)
    entering = jnp.swapaxes(entering, 0, 1).reshape(pieces_of, E, E)

    running = jnp.cumsum(by_chip, axis=0)
    within = jnp.concatenate([jnp.zeros_like(running[:1]), running[:-1]], axis=0)
    prefix_pieces = (entering[None] + within).astype(jnp.bfloat16)
    outgoing = jnp.swapaxes(prefix_pieces.reshape(chips, pieces_of, 2, E // 2, E), 1, 2)
    outgoing = outgoing.reshape(2 * chips, pieces_of, E // 2, E)
    returned = lax.all_to_all(outgoing, "head", 0, 0, tiled=True)
    own_rows = jnp.swapaxes(returned.reshape(chips, 2, pieces_of, E // 2, E), 0, 1)
    own_rows = own_rows.reshape(heads, E // 2, E)
    other_rows = lax.ppermute(own_rows, "head", pairs)
    first = core == 0
    prefix = jnp.concatenate(
        [jnp.where(first, own_rows, other_rows), jnp.where(first, other_rows, own_rows)], axis=1
    )
    before_me = jnp.where(first, 0.0, other_state).astype(jnp.bfloat16)

    return gated_attention(queries, key_vectors, values, prefix, before_me, gate_logits, norm_gain)


def solution(mesh):
    rows = P(("seq", "head"), None)
    return jax.shard_map(
        on_device,
        mesh=mesh,
        in_specs=(rows, rows, rows, rows, P()),
        out_specs=rows,
        check_vma=False,
    )
```

time: 166 us -> 142 us (0.86)
  Pallas kernels: 0 us -> 21.8 us
  local copies, waits for them, and re-layouts: 24.5 us -> 3.91 us
  matrix products: 20.2 us -> 0 us
  other arithmetic: 21.8 us -> 13.5 us
  waiting for transfers between devices: 16.6 us -> 19.5 us
    pallas_call x0 -> x2, Pallas kernels: none -> 21.8 us  [the longest x1 14.4 us: gated_attention(): pl.pallas_call(output_kernel, grid=(heads // GROUP,), in_specs=[cols, col...]
    dot_general x4 -> x0, matrix products: 20.2 us -> none  [the longest x1 6.34 us: on_device(): jnp.einsum('hts,she->the', weights, value_heads, preferred_element_type=j...]
    reshape x2 -> x1, local copies, waits for them, and re-layouts: 6.93 us -> 0.63 us  [gated_attention(): norm_gain.reshape(1, width)]
    convert_element_type x1 -> x0, local copies, waits for them, and re-layouts: 5.59 us -> none  [on_device(): features = attended.astype(jnp.float32)]
    add x1 -> x0, other arithmetic: 4.36 us -> none  [on_device(): state + other_state]
    select_n x1, other arithmetic: 2.65 us -> 0.2 us  [on_device(): jnp.where(first, own_rows, other_rows)]
    unnamed x9 -> x2, local copies, waits for them, and re-layouts: 2.17 us -> 0.01 us
    ppermute x1 -> x0, local copies, waits for them, and re-layouts: 1.76 us -> none  [on_device(): other_rows = lax.ppermute(own_rows, 'head', pairs)]
  transfers between devices with their start and end apart: 4 -> 4, of which waited for: 3 -> 3; matrix products, arithmetic and copies ran while one was open for 11% -> 6% of each run, Pallas kernels for 0% -> 0%
where the time goes in v3:
time: 142 us; the launch traced here: 141 us
  blocking collectives  68.6 us (48%)
  Pallas kernels  21.8 us (15%)
  waiting for transfers between devices  19.5 us (14%)
  starting transfers between devices  13.6 us (10%)
  other arithmetic  13.5 us (10%)
  local copies, waits for them, and re-layouts  3.91 us (3%)
    all_to_all x1, blocking collectives, on_device(): lax.all_to_all(outgoing.astype(jnp.bfloat16), 'head', 0, 0, tiled=True)  35.5 us
    all_to_all x1, blocking collectives, on_device(): returned = lax.all_to_all(outgoing, 'head', 0, 0, tiled=True)  33.1 us
    pallas_call x1, Pallas kernels, gated_attention(): pl.pallas_call(output_kernel, grid=(heads // GROUP,), in_specs=[cols, col...  14.4 us
    pallas_call x1, Pallas kernels, block_states(): pl.pallas_call(state_kernel, grid=(heads // GROUP,), in_specs=[cols, cols...  7.42 us
    ppermute x1, waiting for transfers between devices, on_device(): other_state = lax.ppermute(state, 'head', pairs)  7.13 us
    all_to_all x1, starting transfers between devices, on_device(): per_shard = lax.all_to_all(parts, 'seq', 0, 0, tiled=True)  6.75 us
    all_to_all x1, waiting for transfers between devices, on_device(): per_shard = lax.all_to_all(parts, 'seq', 0, 0, tiled=True)  6.74 us
    all_to_all x1, waiting for transfers between devices, on_device(): entering = lax.all_to_all(before, 'seq', 0, 0, tiled=True)  5.62 us
  transfers between devices with their start and end apart: 4, of which 3 were waited for; matrix products, arithmetic and copies ran while one was open for 6% of the time, Pallas kernels for 0%

profile of v3, /device:TPU:1, one launch (start us, length us, event | category | flops | bytes accessed | tf_op | source)
XLA Modules:
  0.0 141.0 jit_solution(10399837482399405829)
XLA Ops:
  0.0 7.4 %shard_map.55 = f32[64,128,128]{2,1,0:T(8,128)} custom-call(bf16[128,8192]{1,0:T(8,128)(2,1)} %key_ref.3, bf16[128,8192]{1,0:T(8,128)(2,1)} %value_ref.3), custom_call_target="tpu_custom_call" | custom-call | tf_op jit(solution)/shard_map/pallas_call | solution.py:25
  7.4 3.2 %collective-permute-start = (f32[64,128,128]{2,1,0:T(8,128)}, f32[64,128,128]{2,1,0:T(8,128)}, u32[]{:S(2)}, u32[]{:S(2)}) collective-permute-start(f32[64,128,128]{2,1,0:T(8,128)} %shard_map.55), channel_id=1, source_target_pairs={{0,1},{1,0},{2,3},{3,2},{4,5},{5,4},{6,7},{7,6},{8,9},{9,8},{10,11... | collective-permute-start | bytes 12582920 | tf_op jit(solution)/shard_map/ppermute | solution.py:108
  10.6 7.1 %collective-permute-done = f32[64,128,128]{2,1,0:T(8,128)} collective-permute-done((f32[64,128,128]{2,1,0:T(8,128)}, f32[64,128,128]{2,1,0:T(8,128)}, u32[]{:S(2)}, u32[]{:S(2)}) %collective-permute-start) | collective-permute-done | bytes 4194336 | tf_op jit(solution)/shard_map/ppermute | solution.py:108
  17.8 2.7 %fusion = bf16[2,8,4,1,64,128]{5,4,2,0,1,3:T(8,128)(2,1)S(1)} fusion(f32[2,8,4,2,64,128]{5,4,3,2,1,0:T(8,128)} %bitcast.31, s32[]{:T(128)S(6)} %select_n.34, f32[2,8,4,2,64,128]{5,4,3,2,1,0:T(8,128)} %bitcast.1), kind=kLoop, calls=%fused_computation.3 | loop fusion | flops 1048576 | bytes 5243904 | tf_op jit(solution)/shard_map/convert_element_type | solution.py:114
  20.5 35.5 %all_to_all.20 = bf16[16,4,64,128]{3,2,1,0:T(8,128)(2,1)S(1)} all-to-all(bf16[16,4,64,128]{3,2,1,0:T(8,128)(2,1)S(1)} %bitcast.36), channel_id=1, replica_groups=mesh['seq'=16,'head'=16] {'head'}, dimensions={0} | all-to-all | bytes 2097152 | tf_op jit(solution)/shard_map/all_to_all | solution.py:114
  55.9 0.2 bitcast_convert_fusion
  56.2 0.1 reduce_sum.11
  56.4 0.7 copy.15
  57.1 6.8 %all-to-all-start.1 = ((f32[16,4,8,128]{3,2,1,0:T(8,128)}), f32[16,4,8,128]{3,2,1,0:T(8,128)S(1)}, u32[]{:S(2)}, u32[]{:S(2)}) async-start(f32[16,4,8,128]{3,2,1,0:T(8,128)} %copy.15), calls=%async_computation.1 | async-start | bytes 524288 | tf_op jit(solution)/shard_map/all_to_all | solution.py:121
  63.8 1.5 %copy.17 = f32[8,2,4,64,128]{4,3,1,2,0:T(8,128)} copy(f32[8,2,4,64,128]{4,3,2,1,0:T(8,128)S(1)} %bitcast_convert_fusion) | data formatting | bytes 4194304 | tf_op jit(solution)/shard_map/convert_element_type | solution.py:116
  65.3 6.7 %all-to-all-done.1 = f32[16,4,8,128]{3,2,1,0:T(8,128)S(1)} async-done(((f32[16,4,8,128]{3,2,1,0:T(8,128)}), f32[16,4,8,128]{3,2,1,0:T(8,128)S(1)}, u32[]{:S(2)}, u32[]{:S(2)}) %all-to-all-start.1) | async-done | bytes 262176 | tf_op jit(solution)/shard_map/all_to_all | solution.py:121
  72.0 2.5 %fusion.2 = f32[16,4,8,128]{3,2,1,0:T(8,128)S(1)} fusion(f32[16,4,8,128]{3,2,1,0:T(8,128)S(1)} %all-to-all-done.1), kind=kOutput, calls=%fused_computation.13 | output fusion | flops 983040 | bytes 524288 | tf_op jit(solution)/shard_map/jit(cumsum)/reduce_window_sum | solution.py:122
  74.6 0.7 concatenate.12
  75.3 3.5 %all-to-all-start.2 = ((f32[16,4,8,128]{3,2,1,0:T(8,128)}), f32[16,4,8,128]{3,2,1,0:T(8,128)S(1)}, u32[]{:S(2)}, u32[]{:S(2)}) async-start(f32[16,4,8,128]{3,2,1,0:T(8,128)} %concatenate.12), calls=%async_computation.2 | async-start | bytes 524288 | tf_op jit(solution)/shard_map/all_to_all | solution.py:124
  78.8 1.8 %fusion.3 = f32[8,4,128,128]{3,2,1,0:T(8,128)S(1)} fusion(f32[8,4,128,128]{3,2,1,0:T(8,128)} %bitcast.32), kind=kOutput, calls=%fused_computation.14 | output fusion | flops 3670016 | bytes 4194304 | tf_op jit(solution)/shard_map/jit(cumsum)/reduce_window_sum | solution.py:127
  80.6 0.2 slice.17
  80.8 5.6 %all-to-all-done.2 = f32[16,4,8,128]{3,2,1,0:T(8,128)S(1)} async-done(((f32[16,4,8,128]{3,2,1,0:T(8,128)}), f32[16,4,8,128]{3,2,1,0:T(8,128)S(1)}, u32[]{:S(2)}, u32[]{:S(2)}) %all-to-all-start.2) | async-done | bytes 262176 | tf_op jit(solution)/shard_map/all_to_all | solution.py:124
  86.4 0.3 add_convert_fusion
  86.9 33.1 %all_to_all.21 = bf16[16,4,64,128]{3,2,1,0:T(8,128)(2,1)S(1)} all-to-all(bf16[16,4,64,128]{3,2,1,0:T(8,128)(2,1)S(1)} %bitcast.34), channel_id=1, replica_groups=mesh['seq'=16,'head'=16] {'head'}, dimensions={0} | all-to-all | bytes 2097152 | tf_op jit(solution)/shard_map/all_to_all | solution.py:132
  120.2 0.6 reshape.43.gain_ref
  120.8 4.1 %select_convert_fusion.before_ref = bf16[64,128,128]{2,1,0:T(8,128)(2,1)} fusion(f32[64,128,128]{2,1,0:T(8,128)} %collective-permute-done, pred[]{:T(512)S(6)} %eq.5), kind=kLoop, calls=%fused_computation | loop fusion | flops 1048576 | bytes 6291457 | tf_op jit(solution)/shard_map/convert_element_type | solution.py:140
  124.9 0.2 broadcast_select_fusion.1
  125.1 1.5 %pad_maximum_fusion.prefix_ref = bf16[64,128,128]{2,1,0:T(8,128)(2,1)} fusion(bf16[64,64,128]{2,1,0:T(8,128)(2,1)S(1)} %get-tuple-element.6, bf16[64,64,128]{2,1,0:T(8,128)(2,1)S(1)} %get-tuple-element.5), kind=kLoop, calls=%fused_computation.1 | loop fusion | flops 4194304 | bytes 4194304 | tf_op jit(solution)/shard_map/concatenate | solution.py:137
  126.6 14.4 %shard_map.56 = bf16[128,8192]{1,0:T(8,128)(2,1)} custom-call(bf16[128,8192]{1,0:T(8,128)(2,1)} %query_ref.1, bf16[128,8192]{1,0:T(8,128)(2,1)} %key_ref.3, bf16[128,8192]{1,0:T(8,128)(2,1)} %value_ref.3, bf16[64,128,128]{2,1,0:T(8,128)(2,1)} %pad_maximum_fusion.prefix_ref, bf16[64,128,128]{2,1,0:T(8,128)(2,1)} %select_convert_fusion.before_ref, ...), custom_call_target="tpu_custom_call" | custom-call | tf_op jit(solution)/shard_map/pallas_call | solution.py:89
  (10 shorter events, 0.4 us)
Async XLA Ops:
  7.4 10.3 %collective-permute-start = (f32[64,128,128]{2,1,0:T(8,128)}, f32[64,128,128]{2,1,0:T(8,128)}, u32[]{:S(2)}, u32[]{:S(2)}) collective-permute-start(f32[64,128,128]{2,1,0:T(8,128)} %shard_map.55), channel_id=1, source_target_pairs={{0,1},{1,0},{2,3},{3,2},{4,5},{5,4},{6,7},{7,6},{8,9},{9,8},{10,11... | collective-permute-start | bytes 12582920 | tf_op jit(solution)/shard_map/ppermute | solution.py:108
  57.1 15.0 %all-to-all-start.1 = ((f32[16,4,8,128]{3,2,1,0:T(8,128)}), f32[16,4,8,128]{3,2,1,0:T(8,128)S(1)}, u32[]{:S(2)}, u32[]{:S(2)}) async-start(f32[16,4,8,128]{3,2,1,0:T(8,128)} %copy.15), calls=%async_computation.1 | async-start | bytes 524288 | tf_op jit(solution)/shard_map/all_to_all | solution.py:121
  75.3 11.1 %all-to-all-start.2 = ((f32[16,4,8,128]{3,2,1,0:T(8,128)}), f32[16,4,8,128]{3,2,1,0:T(8,128)S(1)}, u32[]{:S(2)}, u32[]{:S(2)}) async-start(f32[16,4,8,128]{3,2,1,0:T(8,128)} %concatenate.12), calls=%async_computation.2 | async-start | bytes 524288 | tf_op jit(solution)/shard_map/all_to_all | solution.py:124
  86.9 33.3 %copy-start = (bf16[8192]{0:T(1024)(128)(2,1)S(1)}, bf16[8192]{0:T(1024)(128)(2,1)}, u32[]{:S(2)}) copy-start(bf16[8192]{0:T(1024)(128)(2,1)} %param.9) | copy-start | bytes 49156
  120.1 4.8 %collective-permute-start.1 = (bf16[64,64,128]{2,1,0:T(8,128)(2,1)S(1)}, bf16[64,64,128]{2,1,0:T(8,128)(2,1)S(1)}, u32[]{:S(2)}, u32[]{:S(2)}) collective-permute-start(bf16[64,64,128]{2,1,0:T(8,128)(2,1)S(1)} %bitcast.33), channel_id=1, source_target_pairs={{0,1},{1,0},{2,3},{3,2},{4,5},{5,4},{6,7},{7,6},{8,9},{9,8},{10,11... | collective-permute-start | bytes 3145736 | tf_op jit(solution)/shard_map/ppermute | solution.py:135

commit v4 on v3

--- a/solution.py
+++ b/solution.py
@@ -96,6 +96,16 @@
     )(queries, key_vectors, values, prefix, before, gate_logits, norm_gain.reshape(1, width))
 
 
+def exchange(pieces, axis):
+    count = pieces.shape[0]
+    me = lax.axis_index(axis)
+    arrived = [lax.dynamic_index_in_dim(pieces, me, 0, True)]
+    for shift in range(1, count):
+        piece = lax.dynamic_index_in_dim(pieces, (me + shift) % count, 0, True)
+        arrived.append(lax.ppermute(piece, axis, [(i, (i + shift) % count) for i in range(count)]))
+    return jnp.roll(jnp.concatenate(arrived[::-1], axis=0), me + 1, axis=0)
+
+
 def on_device(queries, key_vectors, values, gate_logits, norm_gain):
     heads = queries.shape[1] // E
     chips = lax.axis_size("head") // 2
@@ -111,7 +121,7 @@
         other_state.reshape(layout), core, 3, False
     )
     outgoing = jnp.swapaxes(my_rows, 0, 1).reshape(2 * chips, pieces_of, E // 2, E)
-    incoming = lax.all_to_all(outgoing.astype(jnp.bfloat16), "head", 0, 0, tiled=True)
+    incoming = exchange(outgoing.astype(jnp.bfloat16), "head")
     by_chip = jnp.swapaxes(incoming.reshape(chips, 2, pieces_of, E // 2, E), 1, 2)
     by_chip = by_chip.reshape(chips, pieces_of, E, E).astype(jnp.float32)
 
@@ -129,7 +139,7 @@
     prefix_pieces = (entering[None] + within).astype(jnp.bfloat16)
     outgoing = jnp.swapaxes(prefix_pieces.reshape(chips, pieces_of, 2, E // 2, E), 1, 2)
     outgoing = outgoing.reshape(2 * chips, pieces_of, E // 2, E)
-    returned = lax.all_to_all(outgoing, "head", 0, 0, tiled=True)
+    returned = exchange(outgoing, "head")
     own_rows = jnp.swapaxes(returned.reshape(chips, 2, pieces_of, E // 2, E), 0, 1)
     own_rows = own_rows.reshape(heads, E // 2, E)
     other_rows = lax.ppermute(own_rows, "head", pairs)

time: 142 us -> 231 us (1.63)
  waiting for transfers between devices: 19.5 us -> 111 us
  blocking collectives: 68.6 us -> 0 us
  starting transfers between devices: 13.6 us -> 78 us
    ppermute x0 -> x30, waiting for transfers between devices: none -> 92.7 us  [exchange(): lax.ppermute(piece, axis, [(i, (i + shift) % count) for i in range(count)])]
    all_to_all x2 -> x0, blocking collectives: 68.6 us -> none  [the longest x1 35.5 us: on_device(): lax.all_to_all(outgoing.astype(jnp.bfloat16), 'head', 0, 0, tiled=True)]
    ppermute x0 -> x30, starting transfers between devices: none -> 63.2 us  [exchange(): lax.ppermute(piece, axis, [(i, (i + shift) % count) for i in range(count)])]
  transfers between devices with their start and end apart: 4 -> 34, of which waited for: 3 -> 23; matrix products, arithmetic and copies ran while one was open for 6% -> 4% of each run, Pallas kernels for 0% -> 0%
where the time goes in v4:
time: 231 us
  waiting for transfers between devices  111 us (48%)
  starting transfers between devices  78 us (34%)
  Pallas kernels  21.8 us (9%)
  other arithmetic  14.2 us (6%)
  local copies, waits for them, and re-layouts  4.93 us (2%)
    ppermute x30, waiting for transfers between devices, exchange(): lax.ppermute(piece, axis, [(i, (i + shift) % count) for i in range(count)])  92.7 us
    ppermute x30, starting transfers between devices, exchange(): lax.ppermute(piece, axis, [(i, (i + shift) % count) for i in range(count)])  63.2 us
    pallas_call x1, Pallas kernels, gated_attention(): pl.pallas_call(output_kernel, grid=(heads // GROUP,), in_specs=[cols, col...  14.4 us
    pallas_call x1, Pallas kernels, block_states(): pl.pallas_call(state_kernel, grid=(heads // GROUP,), in_specs=[cols, cols...  7.43 us
    ppermute x1, waiting for transfers between devices, on_device(): other_state = lax.ppermute(state, 'head', pairs)  7.13 us
    all_to_all x1, starting transfers between devices, on_device(): per_shard = lax.all_to_all(parts, 'seq', 0, 0, tiled=True)  6.75 us
    all_to_all x1, waiting for transfers between devices, on_device(): per_shard = lax.all_to_all(parts, 'seq', 0, 0, tiled=True)  6.12 us
    all_to_all x1, waiting for transfers between devices, on_device(): entering = lax.all_to_all(before, 'seq', 0, 0, tiled=True)  5.36 us
  transfers between devices with their start and end apart: 34, of which 23 were waited for; matrix products, arithmetic and copies ran while one was open for 4% of the time, Pallas kernels for 0%

profile of v4, /device:TPU:1, one launch (start us, length us, event | category | flops | bytes accessed | tf_op | source)
XLA Modules:
  0.0 230.5 jit_solution(4703111045992704212)
XLA Ops:
  0.0 7.4 %shard_map.55 = f32[64,128,128]{2,1,0:T(8,128)} custom-call(bf16[128,8192]{1,0:T(8,128)(2,1)} %key_ref.3, bf16[128,8192]{1,0:T(8,128)(2,1)} %value_ref.3), custom_call_target="tpu_custom_call" | custom-call | tf_op jit(solution)/shard_map/pallas_call | solution.py:25
  10.7 7.1 %collective-permute-done = f32[64,128,128]{2,1,0:T(8,128)} collective-permute-done((f32[64,128,128]{2,1,0:T(8,128)}, f32[64,128,128]{2,1,0:T(8,128)}, u32[]{:S(2)}, u32[]{:S(2)}) %collective-permute-start) | collective-permute-done | bytes 4194336 | tf_op jit(solution)/shard_map/ppermute | solution.py:118
  31.7 3.9 %collective-permute-start.3 = (bf16[1,4,64,128]{3,2,1,0:T(8,128)(2,1)S(1)}, bf16[1,4,64,128]{3,2,1,0:T(8,128)(2,1)S(1)}, u32[]{:S(2)}, u32[]{:S(2)}) collective-permute-start(bf16[1,4,64,128]{3,2,1,0:T(8,128)(2,1)S(1)} %get-tuple-element.37), channel_id=1, source_target_pairs={{0,13},{1,14},{2,15},{3,0},{4,1},{5,2},{6,3},{7,4},{8,5},{9,6},{10... | collective-permute-start | bytes 196616 | tf_op jit(solution)/shard_map/ppermute | solution.py:105
  44.6 8.1 %collective-permute-done.5 = bf16[1,4,64,128]{3,2,1,0:T(8,128)(2,1)S(1)} collective-permute-done((bf16[1,4,64,128]{3,2,1,0:T(8,128)(2,1)S(1)}, bf16[1,4,64,128]{3,2,1,0:T(8,128)(2,1)S(1)}, u32[]{:S(2)}, u32[]{:S(2)}) %collective-permute-start.5) | collective-permute-done | bytes 65568 | tf_op jit(solution)/shard_map/ppermute | solution.py:105
  53.6 6.9 %collective-permute-done.6 = bf16[1,4,64,128]{3,2,1,0:T(8,128)(2,1)S(1)} collective-permute-done((bf16[1,4,64,128]{3,2,1,0:T(8,128)(2,1)S(1)}, bf16[1,4,64,128]{3,2,1,0:T(8,128)(2,1)S(1)}, u32[]{:S(2)}, u32[]{:S(2)}) %collective-permute-start.6) | collective-permute-done | bytes 65568 | tf_op jit(solution)/shard_map/ppermute | solution.py:105
  62.5 5.7 %collective-permute-done.7 = bf16[1,4,64,128]{3,2,1,0:T(8,128)(2,1)S(1)} collective-permute-done((bf16[1,4,64,128]{3,2,1,0:T(8,128)(2,1)S(1)}, bf16[1,4,64,128]{3,2,1,0:T(8,128)(2,1)S(1)}, u32[]{:S(2)}, u32[]{:S(2)}) %collective-permute-start.7) | collective-permute-done | bytes 65568 | tf_op jit(solution)/shard_map/ppermute | solution.py:105
  68.2 7.7 %collective-permute-done.8 = bf16[1,4,64,128]{3,2,1,0:T(8,128)(2,1)S(1)} collective-permute-done((bf16[1,4,64,128]{3,2,1,0:T(8,128)(2,1)S(1)}, bf16[1,4,64,128]{3,2,1,0:T(8,128)(2,1)S(1)}, u32[]{:S(2)}, u32[]{:S(2)}) %collective-permute-start.8) | collective-permute-done | bytes 65568 | tf_op jit(solution)/shard_map/ppermute | solution.py:105
  76.6 6.3 %collective-permute-done.9 = bf16[1,4,64,128]{3,2,1,0:T(8,128)(2,1)S(1)} collective-permute-done((bf16[1,4,64,128]{3,2,1,0:T(8,128)(2,1)S(1)}, bf16[1,4,64,128]{3,2,1,0:T(8,128)(2,1)S(1)}, u32[]{:S(2)}, u32[]{:S(2)}) %collective-permute-start.9) | collective-permute-done | bytes 65568 | tf_op jit(solution)/shard_map/ppermute | solution.py:105
  85.3 3.8 %collective-permute-done.10 = bf16[1,4,64,128]{3,2,1,0:T(8,128)(2,1)S(1)} collective-permute-done((bf16[1,4,64,128]{3,2,1,0:T(8,128)(2,1)S(1)}, bf16[1,4,64,128]{3,2,1,0:T(8,128)(2,1)S(1)}, u32[]{:S(2)}, u32[]{:S(2)}) %collective-permute-start.10) | collective-permute-done | bytes 65568 | tf_op jit(solution)/shard_map/ppermute | solution.py:105
  89.1 5.6 %collective-permute-start.11 = (bf16[1,4,64,128]{3,2,1,0:T(8,128)(2,1)S(1)}, bf16[1,4,64,128]{3,2,1,0:T(8,128)(2,1)S(1)}, u32[]{:S(2)}, u32[]{:S(2)}) collective-permute-start(bf16[1,4,64,128]{3,2,1,0:T(8,128)(2,1)S(1)} %get-tuple-element.29), channel_id=1, source_target_pairs={{0,5},{1,6},{2,7},{3,8},{4,9},{5,10},{6,11},{7,12},{8,13},{9,14},{... | collective-permute-start | bytes 196616 | tf_op jit(solution)/shard_map/ppermute | solution.py:105
  94.7 4.1 %collective-permute-done.11 = bf16[1,4,64,128]{3,2,1,0:T(8,128)(2,1)S(1)} collective-permute-done((bf16[1,4,64,128]{3,2,1,0:T(8,128)(2,1)S(1)}, bf16[1,4,64,128]{3,2,1,0:T(8,128)(2,1)S(1)}, u32[]{:S(2)}, u32[]{:S(2)}) %collective-permute-start.11) | collective-permute-done | bytes 65568 | tf_op jit(solution)/shard_map/ppermute | solution.py:105
  100.3 6.8 %all-to-all-start = ((f32[16,4,8,128]{3,2,1,0:T(8,128)}), f32[16,4,8,128]{3,2,1,0:T(8,128)S(1)}, u32[]{:S(2)}, u32[]{:S(2)}) async-start(f32[16,4,8,128]{3,2,1,0:T(8,128)} %copy.15), calls=%async_computation | async-start | bytes 524288 | tf_op jit(solution)/shard_map/all_to_all | solution.py:131
  108.5 6.1 %all-to-all-done = f32[16,4,8,128]{3,2,1,0:T(8,128)S(1)} async-done(((f32[16,4,8,128]{3,2,1,0:T(8,128)}), f32[16,4,8,128]{3,2,1,0:T(8,128)S(1)}, u32[]{:S(2)}, u32[]{:S(2)}) %all-to-all-start) | async-done | bytes 262176 | tf_op jit(solution)/shard_map/all_to_all | solution.py:131
  123.6 5.4 %all-to-all-done.1 = f32[16,4,8,128]{3,2,1,0:T(8,128)S(1)} async-done(((f32[16,4,8,128]{3,2,1,0:T(8,128)}), f32[16,4,8,128]{3,2,1,0:T(8,128)S(1)}, u32[]{:S(2)}, u32[]{:S(2)}) %all-to-all-start.1) | async-done | bytes 262176 | tf_op jit(solution)/shard_map/all_to_all | solution.py:134
  151.2 4.3 %collective-permute-start.20 = (bf16[1,4,64,128]{3,2,1,0:T(8,128)(2,1)S(1)}, bf16[1,4,64,128]{3,2,1,0:T(8,128)(2,1)S(1)}, u32[]{:S(2)}, u32[]{:S(2)}) collective-permute-start(bf16[1,4,64,128]{3,2,1,0:T(8,128)(2,1)S(1)} %get-tuple-element.18), channel_id=1, source_target_pairs={{0,11},{1,12},{2,13},{3,14},{4,15},{5,0},{6,1},{7,2},{8,3},{9,4},{... | collective-permute-start | bytes 196616 | tf_op jit(solution)/shard_map/ppermute | solution.py:105
  155.5 6.8 %collective-permute-done.20 = bf16[1,4,64,128]{3,2,1,0:T(8,128)(2,1)S(1)} collective-permute-done((bf16[1,4,64,128]{3,2,1,0:T(8,128)(2,1)S(1)}, bf16[1,4,64,128]{3,2,1,0:T(8,128)(2,1)S(1)}, u32[]{:S(2)}, u32[]{:S(2)}) %collective-permute-start.20) | collective-permute-done | bytes 65568 | tf_op jit(solution)/shard_map/ppermute | solution.py:105
  162.4 7.0 %collective-permute-done.21 = bf16[1,4,64,128]{3,2,1,0:T(8,128)(2,1)S(1)} collective-permute-done((bf16[1,4,64,128]{3,2,1,0:T(8,128)(2,1)S(1)}, bf16[1,4,64,128]{3,2,1,0:T(8,128)(2,1)S(1)}, u32[]{:S(2)}, u32[]{:S(2)}) %collective-permute-start.21) | collective-permute-done | bytes 65568 | tf_op jit(solution)/shard_map/ppermute | solution.py:105
  173.2 3.8 %collective-permute-done.22 = bf16[1,4,64,128]{3,2,1,0:T(8,128)(2,1)S(1)} collective-permute-done((bf16[1,4,64,128]{3,2,1,0:T(8,128)(2,1)S(1)}, bf16[1,4,64,128]{3,2,1,0:T(8,128)(2,1)S(1)}, u32[]{:S(2)}, u32[]{:S(2)}) %collective-permute-start.22) | collective-permute-done | bytes 65568 | tf_op jit(solution)/shard_map/ppermute | solution.py:105
  179.3 5.1 %collective-permute-done.23 = bf16[1,4,64,128]{3,2,1,0:T(8,128)(2,1)S(1)} collective-permute-done((bf16[1,4,64,128]{3,2,1,0:T(8,128)(2,1)S(1)}, bf16[1,4,64,128]{3,2,1,0:T(8,128)(2,1)S(1)}, u32[]{:S(2)}, u32[]{:S(2)}) %collective-permute-start.23) | collective-permute-done | bytes 65568 | tf_op jit(solution)/shard_map/ppermute | solution.py:105
  185.3 6.6 %collective-permute-done.24 = bf16[1,4,64,128]{3,2,1,0:T(8,128)(2,1)S(1)} collective-permute-done((bf16[1,4,64,128]{3,2,1,0:T(8,128)(2,1)S(1)}, bf16[1,4,64,128]{3,2,1,0:T(8,128)(2,1)S(1)}, u32[]{:S(2)}, u32[]{:S(2)}) %collective-permute-start.24) | collective-permute-done | bytes 65568 | tf_op jit(solution)/shard_map/ppermute | solution.py:105
  194.6 5.0 %collective-permute-done.25 = bf16[1,4,64,128]{3,2,1,0:T(8,128)(2,1)S(1)} collective-permute-done((bf16[1,4,64,128]{3,2,1,0:T(8,128)(2,1)S(1)}, bf16[1,4,64,128]{3,2,1,0:T(8,128)(2,1)S(1)}, u32[]{:S(2)}, u32[]{:S(2)}) %collective-permute-start.25) | collective-permute-done | bytes 65568 | tf_op jit(solution)/shard_map/ppermute | solution.py:105
  202.9 5.1 %collective-permute-done.26 = bf16[1,4,64,128]{3,2,1,0:T(8,128)(2,1)S(1)} collective-permute-done((bf16[1,4,64,128]{3,2,1,0:T(8,128)(2,1)S(1)}, bf16[1,4,64,128]{3,2,1,0:T(8,128)(2,1)S(1)}, u32[]{:S(2)}, u32[]{:S(2)}) %collective-permute-start.26) | collective-permute-done | bytes 65568 | tf_op jit(solution)/shard_map/ppermute | solution.py:105
  210.3 4.1 %select_convert_fusion.before_ref = bf16[64,128,128]{2,1,0:T(8,128)(2,1)} fusion(f32[64,128,128]{2,1,0:T(8,128)} %collective-permute-done, pred[]{:T(512)S(6)} %eq.37), kind=kLoop, calls=%fused_computation | loop fusion | flops 1048576 | bytes 6291457 | tf_op jit(solution)/shard_map/convert_element_type | solution.py:150
  216.2 14.4 %shard_map.56 = bf16[128,8192]{1,0:T(8,128)(2,1)} custom-call(bf16[128,8192]{1,0:T(8,128)(2,1)} %query_ref.1, bf16[128,8192]{1,0:T(8,128)(2,1)} %key_ref.3, bf16[128,8192]{1,0:T(8,128)(2,1)} %value_ref.3, bf16[64,128,128]{2,1,0:T(8,128)(2,1)} %pad_maximum_fusion.prefix_ref, bf16[64,128,128]{2,1,0:T(8,128)(2,1)} %select_convert_fusion.before_ref, ...), custom_call_target="tpu_custom_call" | custom-call | tf_op jit(solution)/shard_map/pallas_call | solution.py:89
  (103 shorter events, 83.2 us)
Async XLA Ops:
  7.4 10.4 %collective-permute-start = (f32[64,128,128]{2,1,0:T(8,128)}, f32[64,128,128]{2,1,0:T(8,128)}, u32[]{:S(2)}, u32[]{:S(2)}) collective-permute-start(f32[64,128,128]{2,1,0:T(8,128)} %shard_map.55), channel_id=1, source_target_pairs={{0,1},{1,0},{2,3},{3,2},{4,5},{5,4},{6,7},{7,6},{8,9},{9,8},{10,11... | collective-permute-start | bytes 12582920 | tf_op jit(solution)/shard_map/ppermute | solution.py:118
  20.8 7.5 %collective-permute-start.1 = (bf16[1,4,64,128]{3,2,1,0:T(8,128)(2,1)S(1)}, bf16[1,4,64,128]{3,2,1,0:T(8,128)(2,1)S(1)}, u32[]{:S(2)}, u32[]{:S(2)}) collective-permute-start(bf16[1,4,64,128]{3,2,1,0:T(8,128)(2,1)S(1)} %get-tuple-element.39), channel_id=1, source_target_pairs={{0,15},{1,0},{2,1},{3,2},{4,3},{5,4},{6,5},{7,6},{8,7},{9,8},{10,9... | collective-permute-start | bytes 196616 | tf_op jit(solution)/shard_map/ppermute | solution.py:105
  21.2 77.7 %collective-permute-start.15 = (bf16[1,4,64,128]{3,2,1,0:T(8,128)(2,1)S(1)}, bf16[1,4,64,128]{3,2,1,0:T(8,128)(2,1)S(1)}, u32[]{:S(2)}, u32[]{:S(2)}) collective-permute-start(bf16[1,4,64,128]{3,2,1,0:T(8,128)(2,1)S(1)} %get-tuple-element.25), channel_id=1, source_target_pairs={{0,1},{1,2},{2,3},{3,4},{4,5},{5,6},{6,7},{7,8},{8,9},{9,10},{10,1... | collective-permute-start | bytes 196616 | tf_op jit(solution)/shard_map/ppermute | solution.py:105
  22.5 76.3 %collective-permute-start.14 = (bf16[1,4,64,128]{3,2,1,0:T(8,128)(2,1)S(1)}, bf16[1,4,64,128]{3,2,1,0:T(8,128)(2,1)S(1)}, u32[]{:S(2)}, u32[]{:S(2)}) collective-permute-start(bf16[1,4,64,128]{3,2,1,0:T(8,128)(2,1)S(1)} %get-tuple-element.26), channel_id=1, source_target_pairs={{0,2},{1,3},{2,4},{3,5},{4,6},{5,7},{6,8},{7,9},{8,10},{9,11},{10,... | collective-permute-start | bytes 196616 | tf_op jit(solution)/shard_map/ppermute | solution.py:105
  22.6 76.2 %collective-permute-start.13 = (bf16[1,4,64,128]{3,2,1,0:T(8,128)(2,1)S(1)}, bf16[1,4,64,128]{3,2,1,0:T(8,128)(2,1)S(1)}, u32[]{:S(2)}, u32[]{:S(2)}) collective-permute-start(bf16[1,4,64,128]{3,2,1,0:T(8,128)(2,1)S(1)} %get-tuple-element.27), channel_id=1, source_target_pairs={{0,3},{1,4},{2,5},{3,6},{4,7},{5,8},{6,9},{7,10},{8,11},{9,12},{10... | collective-permute-start | bytes 196616 | tf_op jit(solution)/shard_map/ppermute | solution.py:105
  24.7 74.0 %collective-permute-start.12 = (bf16[1,4,64,128]{3,2,1,0:T(8,128)(2,1)S(1)}, bf16[1,4,64,128]{3,2,1,0:T(8,128)(2,1)S(1)}, u32[]{:S(2)}, u32[]{:S(2)}) collective-permute-start(bf16[1,4,64,128]{3,2,1,0:T(8,128)(2,1)S(1)} %get-tuple-element.28), channel_id=1, source_target_pairs={{0,4},{1,5},{2,6},{3,7},{4,8},{5,9},{6,10},{7,11},{8,12},{9,13},{1... | collective-permute-start | bytes 196616 | tf_op jit(solution)/shard_map/ppermute | solution.py:105
  40.9 11.8 %collective-permute-start.5 = (bf16[1,4,64,128]{3,2,1,0:T(8,128)(2,1)S(1)}, bf16[1,4,64,128]{3,2,1,0:T(8,128)(2,1)S(1)}, u32[]{:S(2)}, u32[]{:S(2)}) collective-permute-start(bf16[1,4,64,128]{3,2,1,0:T(8,128)(2,1)S(1)} %get-tuple-element.35), channel_id=1, source_target_pairs={{0,11},{1,12},{2,13},{3,14},{4,15},{5,0},{6,1},{7,2},{8,3},{9,4},{... | collective-permute-start | bytes 196616 | tf_op jit(solution)/shard_map/ppermute | solution.py:105
  52.7 7.8 %collective-permute-start.6 = (bf16[1,4,64,128]{3,2,1,0:T(8,128)(2,1)S(1)}, bf16[1,4,64,128]{3,2,1,0:T(8,128)(2,1)S(1)}, u32[]{:S(2)}, u32[]{:S(2)}) collective-permute-start(bf16[1,4,64,128]{3,2,1,0:T(8,128)(2,1)S(1)} %get-tuple-element.34), channel_id=1, source_target_pairs={{0,10},{1,11},{2,12},{3,13},{4,14},{5,15},{6,0},{7,1},{8,2},{9,3},... | collective-permute-start | bytes 196616 | tf_op jit(solution)/shard_map/ppermute | solution.py:105
  60.5 7.6 %collective-permute-start.7 = (bf16[1,4,64,128]{3,2,1,0:T(8,128)(2,1)S(1)}, bf16[1,4,64,128]{3,2,1,0:T(8,128)(2,1)S(1)}, u32[]{:S(2)}, u32[]{:S(2)}) collective-permute-start(bf16[1,4,64,128]{3,2,1,0:T(8,128)(2,1)S(1)} %get-tuple-element.33), channel_id=1, source_target_pairs={{0,9},{1,10},{2,11},{3,12},{4,13},{5,14},{6,15},{7,0},{8,1},{9,2},... | collective-permute-start | bytes 196616 | tf_op jit(solution)/shard_map/ppermute | solution.py:105
  68.1 7.7 %collective-permute-start.8 = (bf16[1,4,64,128]{3,2,1,0:T(8,128)(2,1)S(1)}, bf16[1,4,64,128]{3,2,1,0:T(8,128)(2,1)S(1)}, u32[]{:S(2)}, u32[]{:S(2)}) collective-permute-start(bf16[1,4,64,128]{3,2,1,0:T(8,128)(2,1)S(1)} %get-tuple-element.32), channel_id=1, source_target_pairs={{0,8},{1,9},{2,10},{3,11},{4,12},{5,13},{6,14},{7,15},{8,0},{9,1},... | collective-permute-start | bytes 196616 | tf_op jit(solution)/shard_map/ppermute | solution.py:105
  89.1 9.7 %collective-permute-start.11 = (bf16[1,4,64,128]{3,2,1,0:T(8,128)(2,1)S(1)}, bf16[1,4,64,128]{3,2,1,0:T(8,128)(2,1)S(1)}, u32[]{:S(2)}, u32[]{:S(2)}) collective-permute-start(bf16[1,4,64,128]{3,2,1,0:T(8,128)(2,1)S(1)} %get-tuple-element.29), channel_id=1, source_target_pairs={{0,5},{1,6},{2,7},{3,8},{4,9},{5,10},{6,11},{7,12},{8,13},{9,14},{... | collective-permute-start | bytes 196616 | tf_op jit(solution)/shard_map/ppermute | solution.py:105
  100.3 14.3 %all-to-all-start = ((f32[16,4,8,128]{3,2,1,0:T(8,128)}), f32[16,4,8,128]{3,2,1,0:T(8,128)S(1)}, u32[]{:S(2)}, u32[]{:S(2)}) async-start(f32[16,4,8,128]{3,2,1,0:T(8,128)} %copy.15), calls=%async_computation | async-start | bytes 524288 | tf_op jit(solution)/shard_map/all_to_all | solution.py:131
  117.9 11.1 %all-to-all-start.1 = ((f32[16,4,8,128]{3,2,1,0:T(8,128)}), f32[16,4,8,128]{3,2,1,0:T(8,128)S(1)}, u32[]{:S(2)}, u32[]{:S(2)}) async-start(f32[16,4,8,128]{3,2,1,0:T(8,128)} %concatenate.22), calls=%async_computation.1 | async-start | bytes 524288 | tf_op jit(solution)/shard_map/all_to_all | solution.py:134
  129.7 9.2 %collective-permute-start.16 = (bf16[1,4,64,128]{3,2,1,0:T(8,128)(2,1)S(1)}, bf16[1,4,64,128]{3,2,1,0:T(8,128)(2,1)S(1)}, u32[]{:S(2)}, u32[]{:S(2)}) collective-permute-start(bf16[1,4,64,128]{3,2,1,0:T(8,128)(2,1)S(1)} %get-tuple-element.22), channel_id=1, source_target_pairs={{0,15},{1,0},{2,1},{3,2},{4,3},{5,4},{6,5},{7,6},{8,7},{9,8},{10,9... | collective-permute-start | bytes 196616 | tf_op jit(solution)/shard_map/ppermute | solution.py:105
  132.7 75.4 %collective-permute-start.30 = (bf16[1,4,64,128]{3,2,1,0:T(8,128)(2,1)S(1)}, bf16[1,4,64,128]{3,2,1,0:T(8,128)(2,1)S(1)}, u32[]{:S(2)}, u32[]{:S(2)}) collective-permute-start(bf16[1,4,64,128]{3,2,1,0:T(8,128)(2,1)S(1)} %get-tuple-element.8), channel_id=1, source_target_pairs={{0,1},{1,2},{2,3},{3,4},{4,5},{5,6},{6,7},{7,8},{8,9},{9,10},{10,1... | collective-permute-start | bytes 196616 | tf_op jit(solution)/shard_map/ppermute | solution.py:105
  135.0 73.0 %collective-permute-start.29 = (bf16[1,4,64,128]{3,2,1,0:T(8,128)(2,1)S(1)}, bf16[1,4,64,128]{3,2,1,0:T(8,128)(2,1)S(1)}, u32[]{:S(2)}, u32[]{:S(2)}) collective-permute-start(bf16[1,4,64,128]{3,2,1,0:T(8,128)(2,1)S(1)} %get-tuple-element.9), channel_id=1, source_target_pairs={{0,2},{1,3},{2,4},{3,5},{4,6},{5,7},{6,8},{7,9},{8,10},{9,11},{10,... | collective-permute-start | bytes 196616 | tf_op jit(solution)/shard_map/ppermute | solution.py:105
  136.5 71.5 %collective-permute-start.28 = (bf16[1,4,64,128]{3,2,1,0:T(8,128)(2,1)S(1)}, bf16[1,4,64,128]{3,2,1,0:T(8,128)(2,1)S(1)}, u32[]{:S(2)}, u32[]{:S(2)}) collective-permute-start(bf16[1,4,64,128]{3,2,1,0:T(8,128)(2,1)S(1)} %get-tuple-element.10), channel_id=1, source_target_pairs={{0,3},{1,4},{2,5},{3,6},{4,7},{5,8},{6,9},{7,10},{8,11},{9,12},{10... | collective-permute-start | bytes 196616 | tf_op jit(solution)/shard_map/ppermute | solution.py:105
  136.7 71.3 %collective-permute-start.27 = (bf16[1,4,64,128]{3,2,1,0:T(8,128)(2,1)S(1)}, bf16[1,4,64,128]{3,2,1,0:T(8,128)(2,1)S(1)}, u32[]{:S(2)}, u32[]{:S(2)}) collective-permute-start(bf16[1,4,64,128]{3,2,1,0:T(8,128)(2,1)S(1)} %get-tuple-element.11), channel_id=1, source_target_pairs={{0,4},{1,5},{2,6},{3,7},{4,8},{5,9},{6,10},{7,11},{8,12},{9,13},{1... | collective-permute-start | bytes 196616 | tf_op jit(solution)/shard_map/ppermute | solution.py:105
  151.2 11.1 %collective-permute-start.20 = (bf16[1,4,64,128]{3,2,1,0:T(8,128)(2,1)S(1)}, bf16[1,4,64,128]{3,2,1,0:T(8,128)(2,1)S(1)}, u32[]{:S(2)}, u32[]{:S(2)}) collective-permute-start(bf16[1,4,64,128]{3,2,1,0:T(8,128)(2,1)S(1)} %get-tuple-element.18), channel_id=1, source_target_pairs={{0,11},{1,12},{2,13},{3,14},{4,15},{5,0},{6,1},{7,2},{8,3},{9,4},{... | collective-permute-start | bytes 196616 | tf_op jit(solution)/shard_map/ppermute | solution.py:105
  169.4 7.6 %collective-permute-start.22 = (bf16[1,4,64,128]{3,2,1,0:T(8,128)(2,1)S(1)}, bf16[1,4,64,128]{3,2,1,0:T(8,128)(2,1)S(1)}, u32[]{:S(2)}, u32[]{:S(2)}) collective-permute-start(bf16[1,4,64,128]{3,2,1,0:T(8,128)(2,1)S(1)} %get-tuple-element.16), channel_id=1, source_target_pairs={{0,9},{1,10},{2,11},{3,12},{4,13},{5,14},{6,15},{7,0},{8,1},{9,2},... | collective-permute-start | bytes 196616 | tf_op jit(solution)/shard_map/ppermute | solution.py:105
  177.0 7.4 %collective-permute-start.23 = (bf16[1,4,64,128]{3,2,1,0:T(8,128)(2,1)S(1)}, bf16[1,4,64,128]{3,2,1,0:T(8,128)(2,1)S(1)}, u32[]{:S(2)}, u32[]{:S(2)}) collective-permute-start(bf16[1,4,64,128]{3,2,1,0:T(8,128)(2,1)S(1)} %get-tuple-element.15), channel_id=1, source_target_pairs={{0,8},{1,9},{2,10},{3,11},{4,12},{5,13},{6,14},{7,15},{8,0},{9,1},... | collective-permute-start | bytes 196616 | tf_op jit(solution)/shard_map/ppermute | solution.py:105
  184.4 7.5 %collective-permute-start.24 = (bf16[1,4,64,128]{3,2,1,0:T(8,128)(2,1)S(1)}, bf16[1,4,64,128]{3,2,1,0:T(8,128)(2,1)S(1)}, u32[]{:S(2)}, u32[]{:S(2)}) collective-permute-start(bf16[1,4,64,128]{3,2,1,0:T(8,128)(2,1)S(1)} %get-tuple-element.14), channel_id=1, source_target_pairs={{0,7},{1,8},{2,9},{3,10},{4,11},{5,12},{6,13},{7,14},{8,15},{9,0},... | collective-permute-start | bytes 196616 | tf_op jit(solution)/shard_map/ppermute | solution.py:105
  191.9 7.7 %collective-permute-start.25 = (bf16[1,4,64,128]{3,2,1,0:T(8,128)(2,1)S(1)}, bf16[1,4,64,128]{3,2,1,0:T(8,128)(2,1)S(1)}, u32[]{:S(2)}, u32[]{:S(2)}) collective-permute-start(bf16[1,4,64,128]{3,2,1,0:T(8,128)(2,1)S(1)} %get-tuple-element.13), channel_id=1, source_target_pairs={{0,6},{1,7},{2,8},{3,9},{4,10},{5,11},{6,12},{7,13},{8,14},{9,15},... | collective-permute-start | bytes 196616 | tf_op jit(solution)/shard_map/ppermute | solution.py:105
  199.6 8.3 %collective-permute-start.26 = (bf16[1,4,64,128]{3,2,1,0:T(8,128)(2,1)S(1)}, bf16[1,4,64,128]{3,2,1,0:T(8,128)(2,1)S(1)}, u32[]{:S(2)}, u32[]{:S(2)}) collective-permute-start(bf16[1,4,64,128]{3,2,1,0:T(8,128)(2,1)S(1)} %get-tuple-element.12), channel_id=1, source_target_pairs={{0,5},{1,6},{2,7},{3,8},{4,9},{5,10},{6,11},{7,12},{8,13},{9,14},{... | collective-permute-start | bytes 196616 | tf_op jit(solution)/shard_map/ppermute | solution.py:105
  (11 other events, 52.6 us)

commit v5 on v3

--- a/solution.py
+++ b/solution.py
@@ -110,27 +110,19 @@
     my_rows = lax.dynamic_index_in_dim(state.reshape(layout), core, 3, False) + lax.dynamic_index_in_dim(
         other_state.reshape(layout), core, 3, False
     )
-    outgoing = jnp.swapaxes(my_rows, 0, 1).reshape(2 * chips, pieces_of, E // 2, E)
-    incoming = lax.all_to_all(outgoing.astype(jnp.bfloat16), "head", 0, 0, tiled=True)
-    by_chip = jnp.swapaxes(incoming.reshape(chips, 2, pieces_of, E // 2, E), 1, 2)
-    by_chip = by_chip.reshape(chips, pieces_of, E, E).astype(jnp.float32)
-
-    shard_total = jnp.sum(by_chip, axis=0)
     shards = lax.axis_size("seq")
-    parts = jnp.swapaxes(shard_total.reshape(pieces_of, shards, E // shards, E), 0, 1)
-    per_shard = lax.all_to_all(parts, "seq", 0, 0, tiled=True)
-    running = jnp.cumsum(per_shard, axis=0)
-    before = jnp.concatenate([jnp.zeros_like(running[:1]), running[:-1]], axis=0)
-    entering = lax.all_to_all(before, "seq", 0, 0, tiled=True)
-    entering = jnp.swapaxes(entering, 0, 1).reshape(pieces_of, E, E)
+    rows_of = E // 2 // shards
+    outgoing = my_rows.reshape(2, chips, pieces_of, shards, rows_of, E).transpose(3, 1, 0, 2, 4, 5)
+    outgoing = outgoing.reshape(shards * 2 * chips, pieces_of, rows_of, E).astype(jnp.bfloat16)
+    incoming = lax.all_to_all(outgoing, ("seq", "head"), 0, 0, tiled=True)
+    by_chip = incoming.reshape(shards * chips, 2, pieces_of, rows_of, E).astype(jnp.float32)
 
     running = jnp.cumsum(by_chip, axis=0)
-    within = jnp.concatenate([jnp.zeros_like(running[:1]), running[:-1]], axis=0)
-    prefix_pieces = (entering[None] + within).astype(jnp.bfloat16)
-    outgoing = jnp.swapaxes(prefix_pieces.reshape(chips, pieces_of, 2, E // 2, E), 1, 2)
-    outgoing = outgoing.reshape(2 * chips, pieces_of, E // 2, E)
-    returned = lax.all_to_all(outgoing, "head", 0, 0, tiled=True)
-    own_rows = jnp.swapaxes(returned.reshape(chips, 2, pieces_of, E // 2, E), 0, 1)
+    before = jnp.concatenate([jnp.zeros_like(running[:1]), running[:-1]], axis=0).astype(jnp.bfloat16)
+    returned = lax.all_to_all(
+        before.reshape(shards * chips * 2, pieces_of, rows_of, E), ("seq", "head"), 0, 0, tiled=True
+    )
+    own_rows = returned.reshape(shards, chips, 2, pieces_of, rows_of, E).transpose(2, 1, 3, 0, 4, 5)
     own_rows = own_rows.reshape(heads, E // 2, E)
     other_rows = lax.ppermute(own_rows, "head", pairs)
     first = core == 0

time: 142 us -> 127 us (0.89)
  blocking collectives: 68.6 us -> 82 us
  waiting for transfers between devices: 19.5 us -> 7.13 us
  starting transfers between devices: 13.6 us -> 3.31 us
  other arithmetic: 13.5 us -> 8.82 us
    all_to_all x2, blocking collectives: 68.6 us -> 82 us  [the longest x1 45.1 us: on_device(): incoming = lax.all_to_all(outgoing, ('seq', 'head'), 0, 0, tiled=True)]
    all_to_all x2 -> x0, waiting for transfers between devices: 12.4 us -> none  [the longest x1 6.74 us: on_device(): per_shard = lax.all_to_all(parts, 'seq', 0, 0, tiled=True)]
    all_to_all x2 -> x0, starting transfers between devices: 10.3 us -> none  [the longest x1 6.75 us: on_device(): per_shard = lax.all_to_all(parts, 'seq', 0, 0, tiled=True)]
    another operation x1 -> x0, other arithmetic: 2.49 us -> none  [on_device(): running = jnp.cumsum(per_shard, axis=0)]
    convert_element_type x3 -> x1, other arithmetic: 3.21 us -> 2.7 us  [on_device(): outgoing.reshape(shards * 2 * chips, pieces_of, rows_of, E)]
  transfers between devices with their start and end apart: 4 -> 2, of which waited for: 3 -> 1; matrix products, arithmetic and copies ran while one was open for 6% -> 4% of each run, Pallas kernels for 0% -> 0%
where the time goes in v5:
time: 127 us; the launch traced here: 126 us
  blocking collectives  82 us (65%)
  Pallas kernels  21.8 us (17%)
  other arithmetic  8.82 us (7%)
  waiting for transfers between devices  7.13 us (6%)
  starting transfers between devices  3.31 us (3%)
  local copies, waits for them, and re-layouts  2.95 us (2%)
    all_to_all x1, blocking collectives, on_device(): incoming = lax.all_to_all(outgoing, ('seq', 'head'), 0, 0, tiled=True)  45.1 us
    all_to_all x1, blocking collectives, on_device(): lax.all_to_all(before.reshape(shards * chips * 2, pieces_of, rows_of, E),...  36.9 us
    pallas_call x1, Pallas kernels, gated_attention(): pl.pallas_call(output_kernel, grid=(heads // GROUP,), in_specs=[cols, col...  14.4 us
    pallas_call x1, Pallas kernels, block_states(): pl.pallas_call(state_kernel, grid=(heads // GROUP,), in_specs=[cols, cols...  7.42 us
    ppermute x1, waiting for transfers between devices, on_device(): other_state = lax.ppermute(state, 'head', pairs)  7.13 us
    convert_element_type x1, other arithmetic, on_device(): before_me = jnp.where(first, 0.0, other_state).astype(jnp.bfloat16)  4.05 us
    ppermute x1, starting transfers between devices, on_device(): other_state = lax.ppermute(state, 'head', pairs)  3.22 us
    convert_element_type x1, other arithmetic, on_device(): outgoing.reshape(shards * 2 * chips, pieces_of, rows_of, E)  2.7 us
  transfers between devices with their start and end apart: 2, of which 1 were waited for; matrix products, arithmetic and copies ran while one was open for 4% of the time, Pallas kernels for 0%

profile of v5, /device:TPU:1, one launch (start us, length us, event | category | flops | bytes accessed | tf_op | source)
XLA Modules:
  0.0 126.1 jit_solution(18362920905106491434)
XLA Ops:
  0.0 7.4 %shard_map.55 = f32[64,128,128]{2,1,0:T(8,128)} custom-call(bf16[128,8192]{1,0:T(8,128)(2,1)} %key_ref.3, bf16[128,8192]{1,0:T(8,128)(2,1)} %value_ref.3), custom_call_target="tpu_custom_call" | custom-call | tf_op jit(solution)/shard_map/pallas_call | solution.py:25
  7.4 3.2 %collective-permute-start = (f32[64,128,128]{2,1,0:T(8,128)}, f32[64,128,128]{2,1,0:T(8,128)}, u32[]{:S(2)}, u32[]{:S(2)}) collective-permute-start(f32[64,128,128]{2,1,0:T(8,128)} %shard_map.55), channel_id=1, source_target_pairs={{0,1},{1,0},{2,3},{3,2},{4,5},{5,4},{6,7},{7,6},{8,9},{9,8},{10,11... | collective-permute-start | bytes 12582920 | tf_op jit(solution)/shard_map/ppermute | solution.py:108
  10.6 7.1 %collective-permute-done = f32[64,128,128]{2,1,0:T(8,128)} collective-permute-done((f32[64,128,128]{2,1,0:T(8,128)}, f32[64,128,128]{2,1,0:T(8,128)}, u32[]{:S(2)}, u32[]{:S(2)}) %collective-permute-start) | collective-permute-done | bytes 4194336 | tf_op jit(solution)/shard_map/ppermute | solution.py:108
  17.8 2.7 %add_convert_fusion = bf16[2,8,4,1,64,128]{5,4,3,2,1,0:T(8,128)(2,1)S(1)} fusion(f32[2,8,4,2,64,128]{5,4,3,2,1,0:T(8,128)} %bitcast.1, s32[]{:T(128)S(6)} %select_n.34, f32[2,8,4,2,64,128]{5,4,3,2,1,0:T(8,128)} %bitcast.13), kind=kLoop, calls=%fused_computation.4 | loop fusion | flops 1048576 | bytes 5242884 | tf_op jit(solution)/shard_map/convert_element_type | solution.py:116
  20.5 0.5 copy.10
  21.0 45.1 %all_to_all.10 = bf16[256,4,4,128]{3,2,1,0:T(4,128)(2,1)S(1)} all-to-all(bf16[256,4,4,128]{3,2,1,0:T(4,128)(2,1)S(1)} %bitcast.17), channel_id=1, replica_groups=mesh['seq'=16,'head'=16] {'seq','head'}, dimensions={0} | all-to-all | bytes 2097152 | tf_op jit(solution)/shard_map/all_to_all | solution.py:117
  66.1 0.4 fusion
  66.5 0.4 slice.7
  66.8 0.4 concatenate.6
  67.3 36.9 %all_to_all.11 = bf16[256,4,4,128]{3,2,1,0:T(4,128)(2,1)S(1)} all-to-all(bf16[256,4,4,128]{3,2,1,0:T(4,128)(2,1)S(1)} %bitcast.16), channel_id=1, replica_groups=mesh['seq'=16,'head'=16] {'seq','head'}, dimensions={0} | all-to-all | bytes 2097152 | tf_op jit(solution)/shard_map/all_to_all | solution.py:122
  104.1 0.0 copy-start
  104.1 0.3 copy.11
  104.4 0.8 copy.12
  105.2 0.1 collective-permute-start.1
  105.3 0.0 copy-done
  105.3 0.6 reshape.33.gain_ref
  106.0 4.0 %select_convert_fusion.before_ref = bf16[64,128,128]{2,1,0:T(8,128)(2,1)} fusion(f32[64,128,128]{2,1,0:T(8,128)} %collective-permute-done, pred[]{:T(512)S(6)} %eq.5), kind=kLoop, calls=%fused_computation | loop fusion | flops 1048576 | bytes 6291457 | tf_op jit(solution)/shard_map/convert_element_type | solution.py:132
  110.0 0.0 collective-permute-done.1
  110.0 0.1 broadcast_select_fusion.1
  110.2 1.5 %pad_maximum_fusion.prefix_ref = bf16[64,128,128]{2,1,0:T(8,128)(2,1)} fusion(bf16[64,64,128]{2,1,0:T(8,128)(2,1)S(1)} %get-tuple-element.6, bf16[64,64,128]{2,1,0:T(8,128)(2,1)S(1)} %get-tuple-element.5), kind=kLoop, calls=%fused_computation.1 | loop fusion | flops 4194304 | bytes 4194304 | tf_op jit(solution)/shard_map/concatenate | solution.py:129
  111.7 14.4 %shard_map.56 = bf16[128,8192]{1,0:T(8,128)(2,1)} custom-call(bf16[128,8192]{1,0:T(8,128)(2,1)} %query_ref.1, bf16[128,8192]{1,0:T(8,128)(2,1)} %key_ref.3, bf16[128,8192]{1,0:T(8,128)(2,1)} %value_ref.3, bf16[64,128,128]{2,1,0:T(8,128)(2,1)} %pad_maximum_fusion.prefix_ref, bf16[64,128,128]{2,1,0:T(8,128)(2,1)} %select_convert_fusion.before_ref, ...), custom_call_target="tpu_custom_call" | custom-call | tf_op jit(solution)/shard_map/pallas_call | solution.py:89
Async XLA Ops:
  7.4 10.3 %collective-permute-start = (f32[64,128,128]{2,1,0:T(8,128)}, f32[64,128,128]{2,1,0:T(8,128)}, u32[]{:S(2)}, u32[]{:S(2)}) collective-permute-start(f32[64,128,128]{2,1,0:T(8,128)} %shard_map.55), channel_id=1, source_target_pairs={{0,1},{1,0},{2,3},{3,2},{4,5},{5,4},{6,7},{7,6},{8,9},{9,8},{10,11... | collective-permute-start | bytes 12582920 | tf_op jit(solution)/shard_map/ppermute | solution.py:108
  104.1 1.2 copy-start
  105.2 4.8 %collective-permute-start.1 = (bf16[64,64,128]{2,1,0:T(8,128)(2,1)S(1)}, bf16[64,64,128]{2,1,0:T(8,128)(2,1)S(1)}, u32[]{:S(2)}, u32[]{:S(2)}) collective-permute-start(bf16[64,64,128]{2,1,0:T(8,128)(2,1)S(1)} %bitcast.14), channel_id=1, source_target_pairs={{0,1},{1,0},{2,3},{3,2},{4,5},{5,4},{6,7},{7,6},{8,9},{9,8},{10,11... | collective-permute-start | bytes 3145736 | tf_op jit(solution)/shard_map/ppermute | solution.py:127

commit v6 on v5

--- a/solution.py
+++ b/solution.py
@@ -6,7 +6,7 @@
 from jax.sharding import PartitionSpec as P
 
 E = 128
-GROUP = 8
+GROUP = 16
 
 
 def state_kernel(key_ref, value_ref, state_ref):
@@ -105,11 +105,10 @@
 
     state = block_states(key_vectors, values)
 
-    other_state = lax.ppermute(state, "head", pairs)
-    layout = (2, chips, pieces_of, 2, E // 2, E)
-    my_rows = lax.dynamic_index_in_dim(state.reshape(layout), core, 3, False) + lax.dynamic_index_in_dim(
-        other_state.reshape(layout), core, 3, False
-    )
+    halves = state.reshape(heads, 2, E // 2, E)
+    partner_half = lax.ppermute(lax.dynamic_index_in_dim(halves, 1 - core, 1, False), "head", pairs)
+    my_rows = lax.dynamic_index_in_dim(halves, core, 1, False) + partner_half
+    first_half = lax.ppermute(halves[:, 0].astype(jnp.bfloat16), "head", [(h, h + 1) for h in range(0, 2 * chips, 2)])
     shards = lax.axis_size("seq")
     rows_of = E // 2 // shards
     outgoing = my_rows.reshape(2, chips, pieces_of, shards, rows_of, E).transpose(3, 1, 0, 2, 4, 5)
@@ -129,7 +128,9 @@
     prefix = jnp.concatenate(
         [jnp.where(first, own_rows, other_rows), jnp.where(first, other_rows, own_rows)], axis=1
     )
-    before_me = jnp.where(first, 0.0, other_state).astype(jnp.bfloat16)
+    before_me = jnp.concatenate(
+        [jnp.where(first, 0.0, first_half), jnp.where(first, 0.0, partner_half).astype(jnp.bfloat16)], axis=1
+    ).astype(jnp.bfloat16)
 
     return gated_attention(queries, key_vectors, values, prefix, before_me, gate_logits, norm_gain)
 

time: 127 us -> 125 us (0.984)
  blocking collectives: 82 us -> 45.1 us
  waiting for transfers between devices: 7.13 us -> 31.7 us
  local copies, waits for them, and re-layouts: 2.95 us -> 11.3 us
  starting transfers between devices: 3.31 us -> 9.92 us
  Pallas kernels: 21.8 us -> 18.1 us
    all_to_all x1 -> x0, blocking collectives: 36.9 us -> none  [on_device(): lax.all_to_all(before.reshape(shards * chips * 2, pieces_of, rows_of, E),...]
    all_to_all x0 -> x1, waiting for transfers between devices: none -> 27.7 us  [on_device(): lax.all_to_all(before.reshape(shards * chips * 2, pieces_of, rows_of, E),...]
    all_to_all x0 -> x1, starting transfers between devices: none -> 5.18 us  [on_device(): lax.all_to_all(before.reshape(shards * chips * 2, pieces_of, rows_of, E),...]
    convert_element_type x1, other arithmetic: 4.05 us -> 0.27 us  [on_device(): jnp.where(first, 0.0, partner_half).astype(jnp.bfloat16)]
    squeeze x0 -> x1, local copies, waits for them, and re-layouts: none -> 3.17 us  [on_device(): lax.dynamic_index_in_dim(halves, 1 - core, 1, False)]
    ppermute x1 -> x2, waiting for transfers between devices: 7.13 us -> 4 us  [the longest x1 4 us: on_device(): lax.ppermute(lax.dynamic_index_in_dim(halves, 1 - core, 1, False), 'head'...]
    convert_element_type x0 -> x1, local copies, waits for them, and re-layouts: none -> 2.79 us  [on_device(): halves[:, 0].astype(jnp.bfloat16)]
    pallas_call x1, Pallas kernels: 7.42 us -> 5.21 us  [block_states(): pl.pallas_call(state_kernel, grid=(heads // GROUP,), in_specs=[cols, cols...]
  transfers between devices with their start and end apart: 2 -> 4, of which waited for: 1 -> 2; matrix products, arithmetic and copies ran while one was open for 4% -> 6% of each run, Pallas kernels for 0% -> 0%
where the time goes in v6:
time: 125 us
  blocking collectives  45.1 us (36%)
  waiting for transfers between devices  31.7 us (25%)
  Pallas kernels  18.1 us (14%)
  local copies, waits for them, and re-layouts  11.3 us (9%)
  starting transfers between devices  9.92 us (8%)
  other arithmetic  8.38 us (7%)
    all_to_all x1, blocking collectives, on_device(): incoming = lax.all_to_all(outgoing, ('seq', 'head'), 0, 0, tiled=True)  45.1 us
    all_to_all x1, waiting for transfers between devices, on_device(): lax.all_to_all(before.reshape(shards * chips * 2, pieces_of, rows_of, E),...  27.7 us
    pallas_call x1, Pallas kernels, gated_attention(): pl.pallas_call(output_kernel, grid=(heads // GROUP,), in_specs=[cols, col...  12.9 us
    pallas_call x1, Pallas kernels, block_states(): pl.pallas_call(state_kernel, grid=(heads // GROUP,), in_specs=[cols, cols...  5.21 us
    all_to_all x1, starting transfers between devices, on_device(): lax.all_to_all(before.reshape(shards * chips * 2, pieces_of, rows_of, E),...  5.18 us
    ppermute x1, waiting for transfers between devices, on_device(): lax.ppermute(lax.dynamic_index_in_dim(halves, 1 - core, 1, False), 'head'...  4 us
    ppermute x1, starting transfers between devices, on_device(): lax.ppermute(lax.dynamic_index_in_dim(halves, 1 - core, 1, False), 'head'...  3.24 us
    squeeze x1, local copies, waits for them, and re-layouts, on_device(): lax.dynamic_index_in_dim(halves, 1 - core, 1, False)  3.17 us
  transfers between devices with their start and end apart: 4, of which 2 were waited for; matrix products, arithmetic and copies ran while one was open for 6% of the time, Pallas kernels for 0%

profile of v6, /device:TPU:1, one launch (start us, length us, event | category | flops | bytes accessed | tf_op | source)
XLA Modules:
  0.0 124.6 jit_solution(252588162651424563)
XLA Ops:
  0.0 5.2 %shard_map.55 = f32[64,128,128]{2,1,0:T(8,128)} custom-call(bf16[128,8192]{1,0:T(8,128)(2,1)} %key_ref.3, bf16[128,8192]{1,0:T(8,128)(2,1)} %value_ref.3), custom_call_target="tpu_custom_call" | custom-call | tf_op jit(solution)/shard_map/pallas_call | solution.py:25
  5.2 3.2 %dynamic-slice_bitcast_fusion = f32[64,64,128]{2,1,0:T(8,128)} fusion(f32[64,2,64,128]{3,2,1,0:T(8,128)} %bitcast.20, s32[]{:T(128)S(6)} %select_n.41), kind=kLoop, calls=%fused_computation.8 | loop fusion | bytes 4194308 | tf_op jit(solution)/shard_map/jit(dynamic_index_in_dim)/squeeze | solution.py:109
  8.4 3.2 %collective-permute-start = (f32[64,64,128]{2,1,0:T(8,128)}, f32[64,64,128]{2,1,0:T(8,128)S(1)}, u32[]{:S(2)}, u32[]{:S(2)}) collective-permute-start(f32[64,64,128]{2,1,0:T(8,128)} %dynamic-slice_bitcast_fusion), channel_id=1, source_target_pairs={{0,1},{1,0},{2,3},{3,2},{4,5},{5,4},{6,7},{7,6},{8,9},{9,8},{10,11... | collective-permute-start | bytes 6291464 | tf_op jit(solution)/shard_map/ppermute | solution.py:109
  11.6 4.0 %collective-permute-done = f32[64,64,128]{2,1,0:T(8,128)S(1)} collective-permute-done((f32[64,64,128]{2,1,0:T(8,128)}, f32[64,64,128]{2,1,0:T(8,128)S(1)}, u32[]{:S(2)}, u32[]{:S(2)}) %collective-permute-start) | collective-permute-done | bytes 2097184 | tf_op jit(solution)/shard_map/ppermute | solution.py:109
  15.6 2.0 %fusion.2 = bf16[64,64,128]{2,1,0:T(8,128)(2,1)S(1)} fusion(f32[64,64,128]{2,1,0:T(8,128)S(1)} %collective-permute-done, f32[64,2,64,128]{3,2,1,0:T(8,128)} %bitcast.21, s32[]{:T(128)S(6)} %select_n.40), kind=kLoop, calls=%fused_computation.6 | loop fusion | flops 1048576 | bytes 5242884 | tf_op jit(solution)/shard_map/convert_element_type | solution.py:115
  17.6 1.1 copy.11
  18.7 0.8 copy.12
  19.6 45.1 %all_to_all.10 = bf16[256,4,4,128]{3,2,1,0:T(4,128)(2,1)S(1)} all-to-all(bf16[256,4,4,128]{3,2,1,0:T(4,128)(2,1)S(1)} %copy.12), channel_id=1, replica_groups=mesh['seq'=16,'head'=16] {'seq','head'}, dimensions={0} | all-to-all | bytes 2097152 | tf_op jit(solution)/shard_map/all_to_all | solution.py:116
  64.7 0.4 fusion
  65.1 0.4 slice.13
  65.4 1.4 %concatenate.9 = bf16[128,2,4,4,128]{4,3,2,1,0:T(4,128)(2,1)} pad(bf16[127,2,4,4,128]{4,3,2,1,0:T(4,128)(2,1)S(1)} %slice.13, bf16[]{:T(256)} %constant.35.clone.1), padding=1_0x0_0x0_0x0_0x0_0 | pad | bytes 2088962 | tf_op jit(solution)/shard_map/concatenate | solution.py:120
  66.8 5.2 %all-to-all-start.1 = ((bf16[256,4,4,128]{3,2,1,0:T(4,128)(2,1)}), bf16[256,4,4,128]{3,2,1,0:T(4,128)(2,1)S(1)}, u32[]{:S(2)}, u32[]{:S(2)}) async-start(bf16[256,4,4,128]{3,2,1,0:T(4,128)(2,1)} %bitcast.7), calls=%async_computation.1 | async-start | bytes 2097152 | tf_op jit(solution)/shard_map/all_to_all | solution.py:121
  72.0 2.8 %fusion.3 = bf16[64,64,128]{2,1,0:T(8,128)(2,1)} fusion(f32[64,2,64,128]{3,2,1,0:T(8,128)} %bitcast.22), kind=kLoop, calls=%fused_computation.10 | loop fusion | bytes 2097152 | tf_op jit(solution)/shard_map/convert_element_type | solution.py:111
  74.8 1.4 %collective-permute-start.2 = (bf16[64,64,128]{2,1,0:T(8,128)(2,1)}, bf16[64,64,128]{2,1,0:T(8,128)(2,1)}, u32[]{:S(2)}, u32[]{:S(2)}) collective-permute-start(bf16[64,64,128]{2,1,0:T(8,128)(2,1)} %fusion.3), channel_id=1, source_target_pairs={{0,1},{2,3},{4,5},{6,7},{8,9},{10,11},{12,13},{14,15},{16,17},{18,... | collective-permute-start | bytes 3145736 | tf_op jit(solution)/shard_map/ppermute | solution.py:111
  76.2 27.7 %all-to-all-done.1 = bf16[256,4,4,128]{3,2,1,0:T(4,128)(2,1)S(1)} async-done(((bf16[256,4,4,128]{3,2,1,0:T(4,128)(2,1)}), bf16[256,4,4,128]{3,2,1,0:T(4,128)(2,1)S(1)}, u32[]{:S(2)}, u32[]{:S(2)}) %all-to-all-start.1) | async-done | bytes 1048608 | tf_op jit(solution)/shard_map/all_to_all | solution.py:121
  103.9 0.3 copy.13
  104.2 0.8 copy.14
  105.1 0.6 reshape.27.gain_ref
  105.7 1.3 %broadcast_select_fusion = bf16[64,64,128]{2,1,0:T(8,128)(2,1)S(1)} fusion(bf16[64,64,128]{2,1,0:T(8,128)(2,1)} %collective-permute-done.2, pred[]{:T(512)S(6)} %eq.5), kind=kLoop, calls=%fused_computation.11 | loop fusion | flops 524288 | bytes 2097153 | tf_op jit(solution)/shard_map/jit(_where)/select_n | solution.py:132
  107.0 0.3 select_convert_fusion
  107.3 1.5 %pad_maximum_fusion.1.before_ref = bf16[64,128,128]{2,1,0:T(8,128)(2,1)} fusion(bf16[64,64,128]{2,1,0:T(8,128)(2,1)S(1)} %select_convert_fusion, bf16[64,64,128]{2,1,0:T(8,128)(2,1)S(1)} %broadcast_select_fusion), kind=kLoop, calls=%fused_computation.2 | loop fusion | flops 4194304 | bytes 4194304 | tf_op jit(solution)/shard_map/concatenate | solution.py:131
  108.8 1.4 %broadcast_select_fusion.2 = (bf16[64,64,128]{2,1,0:T(8,128)(2,1)S(1)}, bf16[64,64,128]{2,1,0:T(8,128)(2,1)S(1)}) fusion(bf16[64,64,128]{2,1,0:T(8,128)(2,1)S(1)} %bitcast.24, bf16[64,64,128]{2,1,0:T(8,128)(2,1)} %collective-permute-done.1, pred[]{:T(512)S(6)} %eq.5), kind=kLoop, calls=%fused_computation.13 | loop fusion | flops 1048576 | bytes 4194305 | tf_op jit(solution)/shard_map/jit(_where)/select_n | solution.py:129
  110.2 1.5 %pad_maximum_fusion.prefix_ref = bf16[64,128,128]{2,1,0:T(8,128)(2,1)} fusion(bf16[64,64,128]{2,1,0:T(8,128)(2,1)S(1)} %get-tuple-element.6, bf16[64,64,128]{2,1,0:T(8,128)(2,1)S(1)} %get-tuple-element.5), kind=kLoop, calls=%fused_computation.1 | loop fusion | flops 4194304 | bytes 4194304 | tf_op jit(solution)/shard_map/concatenate | solution.py:128
  111.7 12.9 %shard_map.56 = bf16[128,8192]{1,0:T(8,128)(2,1)} custom-call(bf16[128,8192]{1,0:T(8,128)(2,1)} %query_ref.1, bf16[128,8192]{1,0:T(8,128)(2,1)} %key_ref.3, bf16[128,8192]{1,0:T(8,128)(2,1)} %value_ref.3, bf16[64,128,128]{2,1,0:T(8,128)(2,1)} %pad_maximum_fusion.prefix_ref, bf16[64,128,128]{2,1,0:T(8,128)(2,1)} %pad_maximum_fusion.1.before_ref, ...), custom_call_target="tpu_custom_call" | custom-call | tf_op jit(solution)/shard_map/pallas_call | solution.py:89
  (5 shorter events, 0.1 us)
Async XLA Ops:
  8.4 7.2 %collective-permute-start = (f32[64,64,128]{2,1,0:T(8,128)}, f32[64,64,128]{2,1,0:T(8,128)S(1)}, u32[]{:S(2)}, u32[]{:S(2)}) collective-permute-start(f32[64,64,128]{2,1,0:T(8,128)} %dynamic-slice_bitcast_fusion), channel_id=1, source_target_pairs={{0,1},{1,0},{2,3},{3,2},{4,5},{5,4},{6,7},{7,6},{8,9},{9,8},{10,11... | collective-permute-start | bytes 6291464 | tf_op jit(solution)/shard_map/ppermute | solution.py:109
  66.8 37.1 %all-to-all-start.1 = ((bf16[256,4,4,128]{3,2,1,0:T(4,128)(2,1)}), bf16[256,4,4,128]{3,2,1,0:T(4,128)(2,1)S(1)}, u32[]{:S(2)}, u32[]{:S(2)}) async-start(bf16[256,4,4,128]{3,2,1,0:T(4,128)(2,1)} %bitcast.7), calls=%async_computation.1 | async-start | bytes 2097152 | tf_op jit(solution)/shard_map/all_to_all | solution.py:121
  74.8 30.3 %copy-start = (bf16[8192]{0:T(1024)(128)(2,1)S(1)}, bf16[8192]{0:T(1024)(128)(2,1)}, u32[]{:S(2)}) copy-start(bf16[8192]{0:T(1024)(128)(2,1)} %param.9) | copy-start | bytes 49156
  74.8 30.9 %collective-permute-start.2 = (bf16[64,64,128]{2,1,0:T(8,128)(2,1)}, bf16[64,64,128]{2,1,0:T(8,128)(2,1)}, u32[]{:S(2)}, u32[]{:S(2)}) collective-permute-start(bf16[64,64,128]{2,1,0:T(8,128)(2,1)} %fusion.3), channel_id=1, source_target_pairs={{0,1},{2,3},{4,5},{6,7},{8,9},{10,11},{12,13},{14,15},{16,17},{18,... | collective-permute-start | bytes 3145736 | tf_op jit(solution)/shard_map/ppermute | solution.py:111
  105.0 3.8 %collective-permute-start.1 = (bf16[64,64,128]{2,1,0:T(8,128)(2,1)S(1)}, bf16[64,64,128]{2,1,0:T(8,128)(2,1)}, u32[]{:S(2)}, u32[]{:S(2)}) collective-permute-start(bf16[64,64,128]{2,1,0:T(8,128)(2,1)S(1)} %bitcast.23), channel_id=1, source_target_pairs={{0,1},{1,0},{2,3},{3,2},{4,5},{5,4},{6,7},{7,6},{8,9},{9,8},{10,11... | collective-permute-start | bytes 3145736 | tf_op jit(solution)/shard_map/ppermute | solution.py:126

commit v7 on v6

--- a/solution.py
+++ b/solution.py
@@ -31,10 +31,11 @@
     )(key_vectors, values)
 
 
-def output_kernel(query_ref, key_ref, value_ref, prefix_ref, before_ref, gate_ref, gain_ref,
-                  out_ref, attended_ref, square_ref):
+def output_kernel(core_ref, query_ref, key_ref, value_ref, own_ref, other_ref, first_ref, partner_ref,
+                  gate_ref, gain_ref, out_ref, attended_ref, square_ref):
     step = pl.program_id(0)
     tokens = query_ref.shape[0]
+    first = core_ref[0] == 0
 
     @pl.when(step == 0)
     def _():
@@ -52,8 +53,13 @@
         )
         weights = jnp.where(lower_mask, scores, 0.0).astype(jnp.bfloat16)
         total = jnp.dot(weights, value, preferred_element_type=jnp.float32)
-        total += jnp.dot(query, prefix_ref[j], preferred_element_type=jnp.float32)
-        total += jnp.dot(query, before_ref[j], preferred_element_type=jnp.float32)
+        own = own_ref[j]
+        other = other_ref[j]
+        prefix = jnp.concatenate([jnp.where(first, own, other), jnp.where(first, other, own)], axis=0)
+        total += jnp.dot(query, prefix, preferred_element_type=jnp.float32)
+        before = jnp.concatenate([first_ref[j], partner_ref[j].astype(jnp.bfloat16)], axis=0)
+        before_part = jnp.dot(query, before, preferred_element_type=jnp.float32)
+        total += jnp.where(first, 0.0, before_part)
         attended = total.astype(jnp.bfloat16)
         start = pl.multiple_of((step * GROUP + j) * E, E)
         attended_ref[:, pl.ds(start, E)] = attended
@@ -80,20 +86,26 @@
         lax.fori_loop(0, width // E, chunk, 0)
 
 
-def gated_attention(queries, key_vectors, values, prefix, before, gate_logits, norm_gain):
+def gated_attention(core, queries, key_vectors, values, own, other, first_half, partner_half,
+                    gate_logits, norm_gain):
     tokens, width = queries.shape
     heads = width // E
-    cols = pl.BlockSpec((tokens, GROUP * E), lambda i: (0, i))
-    states = pl.BlockSpec((GROUP, E, E), lambda i: (i, 0, 0))
-    whole = pl.BlockSpec((tokens, width), lambda i: (0, 0))
+    cols = pl.BlockSpec((tokens, GROUP * E), lambda i, core: (0, i))
+    halves = pl.BlockSpec((GROUP, E // 2, E), lambda i, core: (i, 0, 0))
+    whole = pl.BlockSpec((tokens, width), lambda i, core: (0, 0))
     return pl.pallas_call(
         output_kernel,
-        grid=(heads // GROUP,),
-        in_specs=[cols, cols, cols, states, states, whole, pl.BlockSpec((1, width), lambda i: (0, 0))],
-        out_specs=whole,
+        grid_spec=pltpu.PrefetchScalarGridSpec(
+            num_scalar_prefetch=1,
+            grid=(heads // GROUP,),
+            in_specs=[cols, cols, cols, halves, halves, halves, halves, whole,
+                      pl.BlockSpec((1, width), lambda i, core: (0, 0))],
+            out_specs=whole,
+            scratch_shapes=[pltpu.VMEM((tokens, width), jnp.bfloat16), pltpu.VMEM((tokens, E), jnp.float32)],
+        ),
         out_shape=jax.ShapeDtypeStruct((tokens, width), jnp.bfloat16),
-        scratch_shapes=[pltpu.VMEM((tokens, width), jnp.bfloat16), pltpu.VMEM((tokens, E), jnp.float32)],
-    )(queries, key_vectors, values, prefix, before, gate_logits, norm_gain.reshape(1, width))
+    )(core.reshape(1), queries, key_vectors, values, own, other, first_half, partner_half, gate_logits,
+      norm_gain.reshape(1, width))
 
 
 def on_device(queries, key_vectors, values, gate_logits, norm_gain):
@@ -109,30 +121,18 @@
     partner_half = lax.ppermute(lax.dynamic_index_in_dim(halves, 1 - core, 1, False), "head", pairs)
     my_rows = lax.dynamic_index_in_dim(halves, core, 1, False) + partner_half
     first_half = lax.ppermute(halves[:, 0].astype(jnp.bfloat16), "head", [(h, h + 1) for h in range(0, 2 * chips, 2)])
-    shards = lax.axis_size("seq")
-    rows_of = E // 2 // shards
-    outgoing = my_rows.reshape(2, chips, pieces_of, shards, rows_of, E).transpose(3, 1, 0, 2, 4, 5)
-    outgoing = outgoing.reshape(shards * 2 * chips, pieces_of, rows_of, E).astype(jnp.bfloat16)
+    devices = lax.axis_size("seq") * 2 * chips
+    outgoing = my_rows.astype(jnp.bfloat16).reshape(devices, -1, E)
     incoming = lax.all_to_all(outgoing, ("seq", "head"), 0, 0, tiled=True)
-    by_chip = incoming.reshape(shards * chips, 2, pieces_of, rows_of, E).astype(jnp.float32)
+    by_chip = incoming.reshape(devices // 2, 2, -1, E).astype(jnp.float32)
 
     running = jnp.cumsum(by_chip, axis=0)
     before = jnp.concatenate([jnp.zeros_like(running[:1]), running[:-1]], axis=0).astype(jnp.bfloat16)
-    returned = lax.all_to_all(
-        before.reshape(shards * chips * 2, pieces_of, rows_of, E), ("seq", "head"), 0, 0, tiled=True
-    )
-    own_rows = returned.reshape(shards, chips, 2, pieces_of, rows_of, E).transpose(2, 1, 3, 0, 4, 5)
-    own_rows = own_rows.reshape(heads, E // 2, E)
+    returned = lax.all_to_all(before.reshape(devices, -1, E), ("seq", "head"), 0, 0, tiled=True)
+    own_rows = returned.reshape(heads, E // 2, E)
     other_rows = lax.ppermute(own_rows, "head", pairs)
-    first = core == 0
-    prefix = jnp.concatenate(
-        [jnp.where(first, own_rows, other_rows), jnp.where(first, other_rows, own_rows)], axis=1
-    )
-    before_me = jnp.concatenate(
-        [jnp.where(first, 0.0, first_half), jnp.where(first, 0.0, partner_half).astype(jnp.bfloat16)], axis=1
-    ).astype(jnp.bfloat16)
-
-    return gated_attention(queries, key_vectors, values, prefix, before_me, gate_logits, norm_gain)
+    return gated_attention(core, queries, key_vectors, values, own_rows, other_rows, first_half, partner_half,
+                           gate_logits, norm_gain)
 
 
 def solution(mesh):

time: 125 us -> 123 us (0.984)
  other arithmetic: 8.38 us -> 3.03 us
  Pallas kernels: 18.1 us -> 22.2 us
  local copies, waits for them, and re-layouts: 11.3 us -> 8.92 us
  waiting for transfers between devices: 31.7 us -> 33.6 us
    pallas_call x1, Pallas kernels: 12.9 us -> 17 us  [gated_attention(): pl.pallas_call(output_kernel, grid_spec=pltpu.PrefetchScalarGridSpec(num_...]
    concatenate x2 -> x0, other arithmetic: 3.01 us -> none  [the longest x1 1.52 us: on_device(): jnp.concatenate([jnp.where(first, 0.0, first_half), jnp.where(first, 0.0,...]
    select_n x2 -> x0, other arithmetic: 2.66 us -> none  [the longest x1 1.36 us: on_device(): jnp.where(first, own_rows, other_rows)]
    ppermute x1, waiting for transfers between devices: 0.01 us -> 1.95 us  [on_device(): other_rows = lax.ppermute(own_rows, 'head', pairs)]
    convert_element_type x2 -> x0, local copies, waits for them, and re-layouts: 1.89 us -> none  [on_device(): outgoing.reshape(shards * 2 * chips, pieces_of, rows_of, E)]
    convert_element_type x2 -> x1, other arithmetic: 2.3 us -> 2.79 us  [on_device(): outgoing = my_rows.astype(jnp.bfloat16).reshape(devices, -1, E)]
  transfers between devices with their start and end apart: 4 -> 4, of which waited for: 2 -> 3; matrix products, arithmetic and copies ran while one was open for 6% -> 3% of each run, Pallas kernels for 0% -> 0%
where the time goes in v7:
time: 123 us
  blocking collectives  45.1 us (37%)
  waiting for transfers between devices  33.6 us (27%)
  Pallas kernels  22.2 us (18%)
  starting transfers between devices  9.83 us (8%)
  local copies, waits for them, and re-layouts  8.92 us (7%)
  other arithmetic  3.03 us (2%)
    all_to_all x1, blocking collectives, on_device(): incoming = lax.all_to_all(outgoing, ('seq', 'head'), 0, 0, tiled=True)  45.1 us
    all_to_all x1, waiting for transfers between devices, on_device(): lax.all_to_all(before.reshape(devices, -1, E), ('seq', 'head'), 0, 0, til...  27.7 us
    pallas_call x1, Pallas kernels, gated_attention(): pl.pallas_call(output_kernel, grid_spec=pltpu.PrefetchScalarGridSpec(num_...  17 us
    all_to_all x1, starting transfers between devices, on_device(): lax.all_to_all(before.reshape(devices, -1, E), ('seq', 'head'), 0, 0, til...  5.31 us
    pallas_call x1, Pallas kernels, block_states(): pl.pallas_call(state_kernel, grid=(heads // GROUP,), in_specs=[cols, cols...  5.21 us
    ppermute x1, waiting for transfers between devices, on_device(): lax.ppermute(lax.dynamic_index_in_dim(halves, 1 - core, 1, False), 'head'...  4 us
    ppermute x1, starting transfers between devices, on_device(): lax.ppermute(lax.dynamic_index_in_dim(halves, 1 - core, 1, False), 'head'...  3.24 us
    squeeze x1, local copies, waits for them, and re-layouts, on_device(): lax.dynamic_index_in_dim(halves, 1 - core, 1, False)  3.17 us
  transfers between devices with their start and end apart: 4, of which 3 were waited for; matrix products, arithmetic and copies ran while one was open for 3% of the time, Pallas kernels for 0%

profile of v7, /device:TPU:1, one launch (start us, length us, event | category | flops | bytes accessed | tf_op | source)
XLA Modules:
  0.0 122.8 jit_solution(9583926625828678298)
XLA Ops:
  0.0 5.2 %shard_map.55 = f32[64,128,128]{2,1,0:T(8,128)} custom-call(bf16[128,8192]{1,0:T(8,128)(2,1)} %key_ref.3, bf16[128,8192]{1,0:T(8,128)(2,1)} %value_ref.3), custom_call_target="tpu_custom_call" | custom-call | tf_op jit(solution)/shard_map/pallas_call | solution.py:25
  5.2 3.2 %dynamic-slice_bitcast_fusion = f32[64,64,128]{2,1,0:T(8,128)} fusion(f32[64,2,64,128]{3,2,1,0:T(8,128)} %bitcast.15, s32[]{:T(128)S(6)} %select_n.16), kind=kLoop, calls=%fused_computation.5 | loop fusion | bytes 4194308 | tf_op jit(solution)/shard_map/jit(dynamic_index_in_dim)/squeeze | solution.py:121
  8.4 3.2 %collective-permute-start = (f32[64,64,128]{2,1,0:T(8,128)}, f32[64,64,128]{2,1,0:T(8,128)S(1)}, u32[]{:S(2)}, u32[]{:S(2)}) collective-permute-start(f32[64,64,128]{2,1,0:T(8,128)} %dynamic-slice_bitcast_fusion), channel_id=1, source_target_pairs={{0,1},{1,0},{2,3},{3,2},{4,5},{5,4},{6,7},{7,6},{8,9},{9,8},{10,11... | collective-permute-start | bytes 6291464 | tf_op jit(solution)/shard_map/ppermute | solution.py:121
  11.6 4.0 %collective-permute-done.partner_ref = f32[64,64,128]{2,1,0:T(8,128)S(1)} collective-permute-done((f32[64,64,128]{2,1,0:T(8,128)}, f32[64,64,128]{2,1,0:T(8,128)S(1)}, u32[]{:S(2)}, u32[]{:S(2)}) %collective-permute-start) | collective-permute-done | bytes 2097184 | tf_op jit(solution)/shard_map/ppermute | solution.py:121
  15.6 0.0 copy-start
  15.6 2.8 %fusion.2 = bf16[64,64,128]{2,1,0:T(8,128)(2,1)S(1)} fusion(f32[64,64,128]{2,1,0:T(8,128)S(1)} %collective-permute-done.partner_ref, f32[64,2,64,128]{3,2,1,0:T(8,128)} %bitcast.16, s32[]{:T(128)S(6)} %select_n.15), kind=kLoop, calls=%fused_computation.4 | loop fusion | flops 1048576 | bytes 5242884 | tf_op jit(solution)/shard_map/convert_element_type | solution.py:125
  18.4 0.0 copy-done
  18.4 45.1 %all_to_all.10 = bf16[256,16,128]{2,1,0:T(8,128)(2,1)S(1)} all-to-all(bf16[256,16,128]{2,1,0:T(8,128)(2,1)S(1)} %bitcast.21), channel_id=1, replica_groups=mesh['seq'=16,'head'=16] {'seq','head'}, dimensions={0} | all-to-all | bytes 2097152 | tf_op jit(solution)/shard_map/all_to_all | solution.py:126
  63.5 0.2 fusion
  63.8 0.1 slice.13
  63.9 1.1 concatenate.3
  65.0 5.3 %all-to-all-start.1 = ((bf16[256,16,128]{2,1,0:T(8,128)(2,1)}), bf16[256,16,128]{2,1,0:T(8,128)(2,1)S(1)}, u32[]{:S(2)}, u32[]{:S(2)}) async-start(bf16[256,16,128]{2,1,0:T(8,128)(2,1)} %bitcast.6), calls=%async_computation.1 | async-start | bytes 2097152 | tf_op jit(solution)/shard_map/all_to_all | solution.py:131
  70.3 2.8 %fusion.3 = bf16[64,64,128]{2,1,0:T(8,128)(2,1)} fusion(f32[64,2,64,128]{3,2,1,0:T(8,128)} %bitcast.17), kind=kLoop, calls=%fused_computation.7 | loop fusion | bytes 2097152 | tf_op jit(solution)/shard_map/convert_element_type | solution.py:123
  73.1 1.3 %collective-permute-start.2 = (bf16[64,64,128]{2,1,0:T(8,128)(2,1)}, bf16[64,64,128]{2,1,0:T(8,128)(2,1)S(1)}, u32[]{:S(2)}, u32[]{:S(2)}) collective-permute-start(bf16[64,64,128]{2,1,0:T(8,128)(2,1)} %fusion.3), channel_id=1, source_target_pairs={{0,1},{2,3},{4,5},{6,7},{8,9},{10,11},{12,13},{14,15},{16,17},{18,... | collective-permute-start | bytes 3145736 | tf_op jit(solution)/shard_map/ppermute | solution.py:123
  74.4 27.7 %all-to-all-done.1 = bf16[256,16,128]{2,1,0:T(8,128)(2,1)S(1)} async-done(((bf16[256,16,128]{2,1,0:T(8,128)(2,1)}), bf16[256,16,128]{2,1,0:T(8,128)(2,1)S(1)}, u32[]{:S(2)}, u32[]{:S(2)}) %all-to-all-start.1) | async-done | bytes 1048608 | tf_op jit(solution)/shard_map/all_to_all | solution.py:131
  102.1 0.0 collective-permute-start.1
  102.1 0.0 copy-done.4
  102.1 0.7 reshape.27.gain_ref
  102.8 0.0 collective-permute-done.2.first_ref
  102.8 1.9 %collective-permute-done.1.other_ref = bf16[64,64,128]{2,1,0:T(8,128)(2,1)S(1)} collective-permute-done((bf16[64,64,128]{2,1,0:T(8,128)(2,1)S(1)}, bf16[64,64,128]{2,1,0:T(8,128)(2,1)S(1)}, u32[]{:S(2)}, u32[]{:S(2)}) %collective-permute-start.1) | collective-permute-done | bytes 1048608 | tf_op jit(solution)/shard_map/ppermute | solution.py:133
  104.7 0.0 copy-done.1
  104.8 0.0 copy-done.2
  104.8 1.0 copy-done.3
  105.8 17.0 %shard_map.56 = bf16[128,8192]{1,0:T(8,128)(2,1)} custom-call(s32[1]{0:T(128)} %bitcast.core_ref, bf16[128,8192]{1,0:T(8,128)(2,1)} %query_ref.1, bf16[128,8192]{1,0:T(8,128)(2,1)} %key_ref.3, bf16[128,8192]{1,0:T(8,128)(2,1)} %value_ref.3, bf16[64,64,128]{2,1,0:T(8,128)(2,1)} %bitcast.19, bf16[64,64,128]{2,1,0:T(8,128)(2,1)} %copy-done.3, ...), custom_call_target="tpu_custom_call" | custom-call | tf_op jit(solution)/shard_map/pallas_call | solution.py:96
  (4 shorter events, 0.0 us)
Async XLA Ops:
  8.4 7.2 %collective-permute-start = (f32[64,64,128]{2,1,0:T(8,128)}, f32[64,64,128]{2,1,0:T(8,128)S(1)}, u32[]{:S(2)}, u32[]{:S(2)}) collective-permute-start(f32[64,64,128]{2,1,0:T(8,128)} %dynamic-slice_bitcast_fusion), channel_id=1, source_target_pairs={{0,1},{1,0},{2,3},{3,2},{4,5},{5,4},{6,7},{7,6},{8,9},{9,8},{10,11... | collective-permute-start | bytes 6291464 | tf_op jit(solution)/shard_map/ppermute | solution.py:121
  15.6 2.8 %copy-start = (f32[64,64,128]{2,1,0:T(8,128)}, f32[64,64,128]{2,1,0:T(8,128)S(1)}, u32[]{:S(2)}) copy-start(f32[64,64,128]{2,1,0:T(8,128)S(1)} %collective-permute-done.partner_ref) | copy-start | bytes 6291460
  65.0 37.1 %copy-start.4 = (bf16[8192]{0:T(1024)(128)(2,1)S(1)}, bf16[8192]{0:T(1024)(128)(2,1)}, u32[]{:S(2)}) copy-start(bf16[8192]{0:T(1024)(128)(2,1)} %param.9) | copy-start | bytes 49156
  65.0 37.1 %all-to-all-start.1 = ((bf16[256,16,128]{2,1,0:T(8,128)(2,1)}), bf16[256,16,128]{2,1,0:T(8,128)(2,1)S(1)}, u32[]{:S(2)}, u32[]{:S(2)}) async-start(bf16[256,16,128]{2,1,0:T(8,128)(2,1)} %bitcast.6), calls=%async_computation.1 | async-start | bytes 2097152 | tf_op jit(solution)/shard_map/all_to_all | solution.py:131
  73.1 29.7 %collective-permute-start.2 = (bf16[64,64,128]{2,1,0:T(8,128)(2,1)}, bf16[64,64,128]{2,1,0:T(8,128)(2,1)S(1)}, u32[]{:S(2)}, u32[]{:S(2)}) collective-permute-start(bf16[64,64,128]{2,1,0:T(8,128)(2,1)} %fusion.3), channel_id=1, source_target_pairs={{0,1},{2,3},{4,5},{6,7},{8,9},{10,11},{12,13},{14,15},{16,17},{18,... | collective-permute-start | bytes 3145736 | tf_op jit(solution)/shard_map/ppermute | solution.py:123
  102.1 2.7 %copy-start.1 = (bf16[256,16,128]{2,1,0:T(8,128)(2,1)}, bf16[256,16,128]{2,1,0:T(8,128)(2,1)S(1)}, u32[]{:S(2)}) copy-start(bf16[256,16,128]{2,1,0:T(8,128)(2,1)S(1)} %all-to-all-done.1) | copy-start | bytes 3145732
  102.1 2.7 %collective-permute-start.1 = (bf16[64,64,128]{2,1,0:T(8,128)(2,1)S(1)}, bf16[64,64,128]{2,1,0:T(8,128)(2,1)S(1)}, u32[]{:S(2)}, u32[]{:S(2)}) collective-permute-start(bf16[64,64,128]{2,1,0:T(8,128)(2,1)S(1)} %bitcast.18), channel_id=1, source_target_pairs={{0,1},{1,0},{2,3},{3,2},{4,5},{5,4},{6,7},{7,6},{8,9},{9,8},{10,11... | collective-permute-start | bytes 3145736 | tf_op jit(solution)/shard_map/ppermute | solution.py:133
  102.8 2.0 %copy-start.2 = (bf16[64,64,128]{2,1,0:T(8,128)(2,1)}, bf16[64,64,128]{2,1,0:T(8,128)(2,1)S(1)}, u32[]{:S(2)}) copy-start(bf16[64,64,128]{2,1,0:T(8,128)(2,1)S(1)} %collective-permute-done.2.first_ref) | copy-start | bytes 3145732
  104.7 1.0 copy-start.3

commit v8 on v7

v8 whole, which is shorter than its diff:
```python
import jax
import jax.numpy as jnp
from jax import lax
from jax.experimental import pallas as pl
from jax.experimental.pallas import tpu as pltpu
from jax.sharding import PartitionSpec as P

E = 128
GROUP = 16


def state_kernel(core_ref, key_ref, value_ref, mine_ref, partner_ref, first_ref):
    first = core_ref[0] == 0
    half = E // 2
    for j in range(GROUP):
        cols = slice(j * E, (j + 1) * E)
        state = lax.dot_general(
            key_ref[:, cols], value_ref[:, cols], (((0,), (0,)), ((), ())),
            preferred_element_type=jnp.float32,
        )
        upper, lower = state[:half], state[half:]
        mine_ref[j] = jnp.where(first, upper, lower)
        partner_ref[j] = jnp.where(first, lower, upper)
        first_ref[j] = upper.astype(jnp.bfloat16)


def block_states(core, key_vectors, values):
    tokens, width = key_vectors.shape
    heads = width // E
    cols = pl.BlockSpec((tokens, GROUP * E), lambda i, core: (0, i))
    halves = pl.BlockSpec((GROUP, E // 2, E), lambda i, core: (i, 0, 0))
    shape = (heads, E // 2, E)
    return pl.pallas_call(
        state_kernel,
        grid_spec=pltpu.PrefetchScalarGridSpec(
            num_scalar_prefetch=1, grid=(heads // GROUP,), in_specs=[cols, cols], out_specs=[halves] * 3
        ),
        out_shape=[jax.ShapeDtypeStruct(shape, jnp.float32), jax.ShapeDtypeStruct(shape, jnp.float32),
                   jax.ShapeDtypeStruct(shape, jnp.bfloat16)],
    )(core.reshape(1), key_vectors, values)


def near_kernel(core_ref, query_ref, key_ref, value_ref, first_ref, partner_ref, near_ref):
    tokens = query_ref.shape[0]
    first = core_ref[0] == 0
    lower_mask = lax.broadcasted_iota(jnp.int32, (tokens, tokens), 0) >= lax.broadcasted_iota(
        jnp.int32, (tokens, tokens), 1
    )
    for j in range(GROUP):
        cols = slice(j * E, (j + 1) * E)
        query = query_ref[:, cols]
        scores = lax.dot_general(
            query, key_ref[:, cols], (((1,), (1,)), ((), ())), preferred_element_type=jnp.float32
        )
        weights = jnp.where(lower_mask, scores, 0.0).astype(jnp.bfloat16)
        total = jnp.dot(weights, value_ref[:, cols], preferred_element_type=jnp.float32)
        before = jnp.concatenate([first_ref[j], partner_ref[j].astype(jnp.bfloat16)], axis=0)
        before_part = jnp.dot(query, before, preferred_element_type=jnp.float32)
        near_ref[:, cols] = total + jnp.where(first, 0.0, before_part)


def near_attention(core, queries, key_vectors, values, first_half, partner_half):
    tokens, width = queries.shape
    heads = width // E
    cols = pl.BlockSpec((tokens, GROUP * E), lambda i, core: (0, i))
    halves = pl.BlockSpec((GROUP, E // 2, E), lambda i, core: (i, 0, 0))
    return pl.pallas_call(
        near_kernel,
        grid_spec=pltpu.PrefetchScalarGridSpec(
            num_scalar_prefetch=1, grid=(heads // GROUP,), in_specs=[cols, cols, cols, halves, halves],
            out_specs=cols,
        ),
        out_shape=jax.ShapeDtypeStruct((tokens, width), jnp.float32),
    )(core.reshape(1), queries, key_vectors, values, first_half, partner_half)


def output_kernel(core_ref, query_ref, near_ref, own_ref, other_ref, gate_ref, gain_ref,
                  out_ref, attended_ref, square_ref):
    step = pl.program_id(0)
    first = core_ref[0] == 0

    @pl.when(step == 0)
    def _():
        square_ref[...] = jnp.zeros_like(square_ref)

    for j in range(GROUP):
        cols = slice(j * E, (j + 1) * E)
        own = own_ref[j]
        other = other_ref[j]
        prefix = jnp.concatenate([jnp.where(first, own, other), jnp.where(first, other, own)], axis=0)
        total = near_ref[:, cols] + jnp.dot(query_ref[:, cols], prefix, preferred_element_type=jnp.float32)
        attended = total.astype(jnp.bfloat16)
        start = pl.multiple_of((step * GROUP + j) * E, E)
        attended_ref[:, pl.ds(start, E)] = attended
        features = attended.astype(jnp.float32)
        square_ref[...] += features * features

    @pl.when(step == pl.num_programs(0) - 1)
    def _():
        width = attended_ref.shape[1]
        mean_square = jnp.sum(square_ref[...], axis=1, keepdims=True) / width
        scale = lax.rsqrt(mean_square + 1e-06)

        def chunk(c, carry):
            start = pl.multiple_of(c * E, E)
            window = pl.ds(start, E)
            features = attended_ref[:, window].astype(jnp.float32)
            gain = gain_ref[:, window].astype(jnp.float32)
            gate = gate_ref[:, window].astype(jnp.float32)
            scaled = features * scale * gain
            scaled = scaled * (1.0 / (1.0 + jnp.exp(-gate)))
            out_ref[:, window] = scaled.astype(out_ref.dtype)
            return carry

        lax.fori_loop(0, width // E, chunk, 0)


def gated_attention(core, queries, near, own, other, gate_logits, norm_gain):
    tokens, width = queries.shape
    heads = width // E
    cols = pl.BlockSpec((tokens, GROUP * E), lambda i, core: (0, i))
    halves = pl.BlockSpec((GROUP, E // 2, E), lambda i, core: (i, 0, 0))
    whole = pl.BlockSpec((tokens, width), lambda i, core: (0, 0))
    return pl.pallas_call(
        output_kernel,
        grid_spec=pltpu.PrefetchScalarGridSpec(
            num_scalar_prefetch=1,
            grid=(heads // GROUP,),
            in_specs=[cols, pl.BlockSpec((tokens, GROUP * E), lambda i, core: (0, i)), halves, halves, whole,
                      pl.BlockSpec((1, width), lambda i, core: (0, 0))],
            out_specs=whole,
            scratch_shapes=[pltpu.VMEM((tokens, width), jnp.bfloat16), pltpu.VMEM((tokens, E), jnp.float32)],
        ),
        out_shape=jax.ShapeDtypeStruct((tokens, width), jnp.bfloat16),
    )(core.reshape(1), queries, near, own, other, gate_logits,
      norm_gain.reshape(1, width))


def on_device(queries, key_vectors, values, gate_logits, norm_gain):
    heads = queries.shape[1] // E
    chips = lax.axis_size("head") // 2
    core = lax.axis_index("head") % 2
    pairs = [(h, h ^ 1) for h in range(2 * chips)]

    mine, for_partner, first_rows = block_states(core, key_vectors, values)
    partner_half = lax.ppermute(for_partner, "head", pairs)
    my_rows = mine + partner_half
    first_half = lax.ppermute(first_rows, "head", [(h, h + 1) for h in range(0, 2 * chips, 2)])
    devices = lax.axis_size("seq") * 2 * chips
    outgoing = my_rows.astype(jnp.bfloat16).reshape(devices, -1, E)
    incoming = lax.all_to_all(outgoing, ("seq", "head"), 0, 0, tiled=True)
    by_chip = incoming.reshape(devices // 2, 2, -1, E).astype(jnp.float32)

    running = jnp.cumsum(by_chip, axis=0)
    before = jnp.concatenate([jnp.zeros_like(running[:1]), running[:-1]], axis=0).astype(jnp.bfloat16)
    returned = lax.all_to_all(before.reshape(devices, -1, E), ("seq", "head"), 0, 0, tiled=True)
    near = near_attention(core, queries, key_vectors, values, first_half, partner_half)
    own_rows = returned.reshape(heads, E // 2, E)
    other_rows = lax.ppermute(own_rows, "head", pairs)
    return gated_attention(core, queries, near, own_rows, other_rows, gate_logits, norm_gain)


def solution(mesh):
    rows = P(("seq", "head"), None)
    return jax.shard_map(
        on_device,
        mesh=mesh,
        in_specs=(rows, rows, rows, rows, P()),
        out_specs=rows,
        check_vma=False,
    )
```

time: 123 us -> 119 us (0.967)
  local copies, waits for them, and re-layouts: 8.92 us -> 3.85 us
    pallas_call x1 -> x2, Pallas kernels: 5.21 us -> 13.1 us  [the longest x1 7.64 us: near_attention(): pl.pallas_call(near_kernel, grid_spec=pltpu.PrefetchScalarGridSpec(num_sc...]
    pallas_call x1, Pallas kernels: 17 us -> 9.29 us  [gated_attention(): pl.pallas_call(output_kernel, grid_spec=pltpu.PrefetchScalarGridSpec(num_...]
    squeeze x1 -> x0, local copies, waits for them, and re-layouts: 3.17 us -> none  [on_device(): lax.dynamic_index_in_dim(halves, 1 - core, 1, False)]
    all_to_all x1, waiting for transfers between devices: 27.7 us -> 30.6 us  [on_device(): lax.all_to_all(before.reshape(devices, -1, E), ('seq', 'head'), 0, 0, til...]
    convert_element_type x1 -> x0, local copies, waits for them, and re-layouts: 2.8 us -> none  [on_device(): halves[:, 0].astype(jnp.bfloat16)]
    ppermute x1, waiting for transfers between devices: 1.95 us -> 0.01 us  [on_device(): other_rows = lax.ppermute(own_rows, 'head', pairs)]
  transfers between devices with their start and end apart: 4 -> 4, of which waited for: 3 -> 2; matrix products, arithmetic and copies ran while one was open for 3% -> 1% of each run, Pallas kernels for 0% -> 6%
where the time goes in v8:
time: 119 us
  blocking collectives  45.1 us (38%)
  waiting for transfers between devices  34.6 us (29%)
  Pallas kernels  22.4 us (19%)
  starting transfers between devices  9.71 us (8%)
  local copies, waits for them, and re-layouts  3.85 us (3%)
  other arithmetic  3.03 us (3%)
    all_to_all x1, blocking collectives, on_device(): incoming = lax.all_to_all(outgoing, ('seq', 'head'), 0, 0, tiled=True)  45.1 us
    all_to_all x1, waiting for transfers between devices, on_device(): lax.all_to_all(before.reshape(devices, -1, E), ('seq', 'head'), 0, 0, til...  30.6 us
    pallas_call x1, Pallas kernels, gated_attention(): pl.pallas_call(output_kernel, grid_spec=pltpu.PrefetchScalarGridSpec(num_...  9.29 us
    pallas_call x1, Pallas kernels, near_attention(): pl.pallas_call(near_kernel, grid_spec=pltpu.PrefetchScalarGridSpec(num_sc...  7.64 us
    pallas_call x1, Pallas kernels, block_states(): pl.pallas_call(state_kernel, grid_spec=pltpu.PrefetchScalarGridSpec(num_s...  5.5 us
    all_to_all x1, starting transfers between devices, on_device(): lax.all_to_all(before.reshape(devices, -1, E), ('seq', 'head'), 0, 0, til...  5.18 us
    ppermute x1, waiting for transfers between devices, on_device(): partner_half = lax.ppermute(for_partner, 'head', pairs)  4 us
    ppermute x1, starting transfers between devices, on_device(): partner_half = lax.ppermute(for_partner, 'head', pairs)  3.24 us
  transfers between devices with their start and end apart: 4, of which 2 were waited for; matrix products, arithmetic and copies ran while one was open for 1% of the time, Pallas kernels for 6%

profile of v8, /device:TPU:1, one launch (start us, length us, event | category | flops | bytes accessed | tf_op | source)
XLA Modules:
  0.0 118.8 jit_solution(14925409514096250513)
XLA Ops:
  0.0 5.5 %shard_map.55 = (f32[64,64,128]{2,1,0:T(8,128)}, f32[64,64,128]{2,1,0:T(8,128)}, bf16[64,64,128]{2,1,0:T(8,128)(2,1)}) custom-call(s32[1]{0:T(128)} %bitcast.core_ref, bf16[128,8192]{1,0:T(8,128)(2,1)} %key_ref.3, bf16[128,8192]{1,0:T(8,128)(2,1)} %value_ref.3), custom_call_target="tpu_custom_call" | custom-call | tf_op jit(solution)/shard_map/pallas_call | solution.py:33
  5.5 3.2 %collective-permute-start.1 = (f32[64,64,128]{2,1,0:T(8,128)}, f32[64,64,128]{2,1,0:T(8,128)S(1)}, u32[]{:S(2)}, u32[]{:S(2)}) collective-permute-start(f32[64,64,128]{2,1,0:T(8,128)} %get-tuple-element.9), channel_id=1, source_target_pairs={{0,1},{1,0},{2,3},{3,2},{4,5},{5,4},{6,7},{7,6},{8,9},{9,8},{10,11... | collective-permute-start | bytes 6291464 | tf_op jit(solution)/shard_map/ppermute | solution.py:146
  8.7 4.0 %collective-permute-done.1.partner_ref = f32[64,64,128]{2,1,0:T(8,128)S(1)} collective-permute-done((f32[64,64,128]{2,1,0:T(8,128)}, f32[64,64,128]{2,1,0:T(8,128)S(1)}, u32[]{:S(2)}, u32[]{:S(2)}) %collective-permute-start.1) | collective-permute-done | bytes 2097184 | tf_op jit(solution)/shard_map/ppermute | solution.py:146
  12.7 2.8 %add_convert_fusion = bf16[64,64,128]{2,1,0:T(8,128)(2,1)S(1)} fusion(f32[64,64,128]{2,1,0:T(8,128)} %get-tuple-element.10, f32[64,64,128]{2,1,0:T(8,128)S(1)} %collective-permute-done.1.partner_ref), kind=kLoop, calls=%fused_computation.2 | loop fusion | flops 1048576 | bytes 5242880 | tf_op jit(solution)/shard_map/convert_element_type | solution.py:150
  15.5 0.0 copy-done
  15.5 45.1 %all_to_all.10 = bf16[256,16,128]{2,1,0:T(8,128)(2,1)S(1)} all-to-all(bf16[256,16,128]{2,1,0:T(8,128)(2,1)S(1)} %bitcast.8), channel_id=1, replica_groups=mesh['seq'=16,'head'=16] {'seq','head'}, dimensions={0} | all-to-all | bytes 2097152 | tf_op jit(solution)/shard_map/all_to_all | solution.py:151
  60.6 0.2 fusion
  60.9 0.1 slice.7
  61.0 0.0 copy-start.4
  61.0 1.1 concatenate.3
  62.1 5.2 %all-to-all-start.1 = ((bf16[256,16,128]{2,1,0:T(8,128)(2,1)}), bf16[256,16,128]{2,1,0:T(8,128)(2,1)S(1)}, u32[]{:S(2)}, u32[]{:S(2)}) async-start(bf16[256,16,128]{2,1,0:T(8,128)(2,1)} %bitcast.3), calls=%async_computation.1 | async-start | bytes 2097152 | tf_op jit(solution)/shard_map/all_to_all | solution.py:156
  67.3 1.3 %collective-permute-start = (bf16[64,64,128]{2,1,0:T(8,128)(2,1)}, bf16[64,64,128]{2,1,0:T(8,128)(2,1)S(1)}, u32[]{:S(2)}, u32[]{:S(2)}) collective-permute-start(bf16[64,64,128]{2,1,0:T(8,128)(2,1)} %get-tuple-element.8), channel_id=1, source_target_pairs={{0,1},{2,3},{4,5},{6,7},{8,9},{10,11},{12,13},{14,15},{16,17},{18,... | collective-permute-start | bytes 3145736 | tf_op jit(solution)/shard_map/ppermute | solution.py:148
  68.6 30.6 %all-to-all-done.1 = bf16[256,16,128]{2,1,0:T(8,128)(2,1)S(1)} async-done(((bf16[256,16,128]{2,1,0:T(8,128)(2,1)}), bf16[256,16,128]{2,1,0:T(8,128)(2,1)S(1)}, u32[]{:S(2)}, u32[]{:S(2)}) %all-to-all-start.1) | async-done | bytes 1048608 | tf_op jit(solution)/shard_map/all_to_all | solution.py:156
  99.2 0.0 collective-permute-start.2
  99.2 0.0 copy-done.4
  99.2 0.7 reshape.24.gain_ref
  99.9 0.0 collective-permute-done.first_ref
  99.9 1.0 copy-done.3
  100.9 7.6 %shard_map.56.near_ref = f32[128,8192]{1,0:T(8,128)} custom-call(s32[1]{0:T(128)} %bitcast.core_ref, bf16[128,8192]{1,0:T(8,128)(2,1)} %query_ref.3, bf16[128,8192]{1,0:T(8,128)(2,1)} %key_ref.3, bf16[128,8192]{1,0:T(8,128)(2,1)} %value_ref.3, bf16[64,64,128]{2,1,0:T(8,128)(2,1)} %copy-done.3, f32[64,64,128]{2,1,0:T(8,128)} %copy-done), custom_call_target="tpu_custom_call" | custom-call | tf_op jit(solution)/shard_map/pallas_call | solution.py:67
  108.5 0.0 copy-done.1
  108.5 0.0 collective-permute-done.2.other_ref
  108.5 0.0 copy-start.2
  108.5 1.0 copy-done.2
  109.5 9.3 %shard_map.57 = bf16[128,8192]{1,0:T(8,128)(2,1)} custom-call(s32[1]{0:T(128)} %bitcast.core_ref, bf16[128,8192]{1,0:T(8,128)(2,1)} %query_ref.3, f32[128,8192]{1,0:T(8,128)} %shard_map.56.near_ref, bf16[64,64,128]{2,1,0:T(8,128)(2,1)} %bitcast.7, bf16[64,64,128]{2,1,0:T(8,128)(2,1)} %copy-done.2, bf16[128,8192]{1,0:T(8,128)(2,1)} %gate_ref.1, ...), custom_call_target="tpu_custom_call" | custom-call | tf_op jit(solution)/shard_map/pallas_call | solution.py:124
  (3 shorter events, 0.0 us)
Async XLA Ops:
  5.5 7.2 %collective-permute-start.1 = (f32[64,64,128]{2,1,0:T(8,128)}, f32[64,64,128]{2,1,0:T(8,128)S(1)}, u32[]{:S(2)}, u32[]{:S(2)}) collective-permute-start(f32[64,64,128]{2,1,0:T(8,128)} %get-tuple-element.9), channel_id=1, source_target_pairs={{0,1},{1,0},{2,3},{3,2},{4,5},{5,4},{6,7},{7,6},{8,9},{9,8},{10,11... | collective-permute-start | bytes 6291464 | tf_op jit(solution)/shard_map/ppermute | solution.py:146
  12.7 2.8 %copy-start = (f32[64,64,128]{2,1,0:T(8,128)}, f32[64,64,128]{2,1,0:T(8,128)S(1)}, u32[]{:S(2)}) copy-start(f32[64,64,128]{2,1,0:T(8,128)S(1)} %collective-permute-done.1.partner_ref) | copy-start | bytes 6291460
  61.0 38.2 %copy-start.4 = (bf16[8192]{0:T(1024)(128)(2,1)S(1)}, bf16[8192]{0:T(1024)(128)(2,1)}, u32[]{:S(2)}) copy-start(bf16[8192]{0:T(1024)(128)(2,1)} %param.9) | copy-start | bytes 49156
  62.1 37.1 %all-to-all-start.1 = ((bf16[256,16,128]{2,1,0:T(8,128)(2,1)}), bf16[256,16,128]{2,1,0:T(8,128)(2,1)S(1)}, u32[]{:S(2)}, u32[]{:S(2)}) async-start(bf16[256,16,128]{2,1,0:T(8,128)(2,1)} %bitcast.3), calls=%async_computation.1 | async-start | bytes 2097152 | tf_op jit(solution)/shard_map/all_to_all | solution.py:156
  67.3 32.6 %collective-permute-start = (bf16[64,64,128]{2,1,0:T(8,128)(2,1)}, bf16[64,64,128]{2,1,0:T(8,128)(2,1)S(1)}, u32[]{:S(2)}, u32[]{:S(2)}) collective-permute-start(bf16[64,64,128]{2,1,0:T(8,128)(2,1)} %get-tuple-element.8), channel_id=1, source_target_pairs={{0,1},{2,3},{4,5},{6,7},{8,9},{10,11},{12,13},{14,15},{16,17},{18,... | collective-permute-start | bytes 3145736 | tf_op jit(solution)/shard_map/ppermute | solution.py:148
  99.2 9.3 %copy-start.1 = (bf16[256,16,128]{2,1,0:T(8,128)(2,1)}, bf16[256,16,128]{2,1,0:T(8,128)(2,1)S(1)}, u32[]{:S(2)}) copy-start(bf16[256,16,128]{2,1,0:T(8,128)(2,1)S(1)} %all-to-all-done.1) | copy-start | bytes 3145732
  99.2 9.3 %collective-permute-start.2 = (bf16[64,64,128]{2,1,0:T(8,128)(2,1)S(1)}, bf16[64,64,128]{2,1,0:T(8,128)(2,1)S(1)}, u32[]{:S(2)}, u32[]{:S(2)}) collective-permute-start(bf16[64,64,128]{2,1,0:T(8,128)(2,1)S(1)} %bitcast.6), channel_id=1, source_target_pairs={{0,1},{1,0},{2,3},{3,2},{4,5},{5,4},{6,7},{7,6},{8,9},{9,8},{10,11... | collective-permute-start | bytes 3145736 | tf_op jit(solution)/shard_map/ppermute | solution.py:159
  99.9 1.0 copy-start.3
  108.5 1.0 copy-start.2

commit v9 on v8

--- a/solution.py
+++ b/solution.py
@@ -40,7 +40,7 @@
     )(core.reshape(1), key_vectors, values)
 
 
-def near_kernel(core_ref, query_ref, key_ref, value_ref, first_ref, partner_ref, near_ref):
+def near_kernel(core_ref, query_ref, key_ref, value_ref, first_ref, partner_ref, mine_ref, near_ref, chip_ref):
     tokens = query_ref.shape[0]
     first = core_ref[0] == 0
     lower_mask = lax.broadcasted_iota(jnp.int32, (tokens, tokens), 0) >= lax.broadcasted_iota(
@@ -57,9 +57,10 @@
         before = jnp.concatenate([first_ref[j], partner_ref[j].astype(jnp.bfloat16)], axis=0)
         before_part = jnp.dot(query, before, preferred_element_type=jnp.float32)
         near_ref[:, cols] = total + jnp.where(first, 0.0, before_part)
+        chip_ref[j] = (mine_ref[j] + partner_ref[j]).astype(jnp.bfloat16)
 
 
-def near_attention(core, queries, key_vectors, values, first_half, partner_half):
+def near_attention(core, queries, key_vectors, values, first_half, partner_half, mine):
     tokens, width = queries.shape
     heads = width // E
     cols = pl.BlockSpec((tokens, GROUP * E), lambda i, core: (0, i))
@@ -67,15 +68,16 @@
     return pl.pallas_call(
         near_kernel,
         grid_spec=pltpu.PrefetchScalarGridSpec(
-            num_scalar_prefetch=1, grid=(heads // GROUP,), in_specs=[cols, cols, cols, halves, halves],
-            out_specs=cols,
+            num_scalar_prefetch=1, grid=(heads // GROUP,), in_specs=[cols, cols, cols, halves, halves, halves],
+            out_specs=[cols, halves],
         ),
-        out_shape=jax.ShapeDtypeStruct((tokens, width), jnp.float32),
-    )(core.reshape(1), queries, key_vectors, values, first_half, partner_half)
+        out_shape=[jax.ShapeDtypeStruct((tokens, width), jnp.float32),
+                   jax.ShapeDtypeStruct((heads, E // 2, E), jnp.bfloat16)],
+    )(core.reshape(1), queries, key_vectors, values, first_half, partner_half, mine)
 
 
 def output_kernel(core_ref, query_ref, near_ref, own_ref, other_ref, gate_ref, gain_ref,
-                  out_ref, attended_ref, square_ref):
+                  out_ref, attended_ref, square_ref, opening_ref):
     step = pl.program_id(0)
     first = core_ref[0] == 0
 
@@ -94,6 +96,8 @@
         attended_ref[:, pl.ds(start, E)] = attended
         features = attended.astype(jnp.float32)
         square_ref[...] += features * features
+        gate = gate_ref[:, cols].astype(jnp.float32)
+        opening_ref[:, pl.ds(start, E)] = 1.0 / (1.0 + jnp.exp(-gate))
 
     @pl.when(step == pl.num_programs(0) - 1)
     def _():
@@ -106,9 +110,8 @@
             window = pl.ds(start, E)
             features = attended_ref[:, window].astype(jnp.float32)
             gain = gain_ref[:, window].astype(jnp.float32)
-            gate = gate_ref[:, window].astype(jnp.float32)
             scaled = features * scale * gain
-            scaled = scaled * (1.0 / (1.0 + jnp.exp(-gate)))
+            scaled = scaled * opening_ref[:, window]
             out_ref[:, window] = scaled.astype(out_ref.dtype)
             return carry
 
@@ -126,10 +129,11 @@
         grid_spec=pltpu.PrefetchScalarGridSpec(
             num_scalar_prefetch=1,
             grid=(heads // GROUP,),
-            in_specs=[cols, pl.BlockSpec((tokens, GROUP * E), lambda i, core: (0, i)), halves, halves, whole,
+            in_specs=[cols, cols, halves, halves, cols,
                       pl.BlockSpec((1, width), lambda i, core: (0, 0))],
             out_specs=whole,
-            scratch_shapes=[pltpu.VMEM((tokens, width), jnp.bfloat16), pltpu.VMEM((tokens, E), jnp.float32)],
+            scratch_shapes=[pltpu.VMEM((tokens, width), jnp.bfloat16), pltpu.VMEM((tokens, E), jnp.float32),
+                            pltpu.VMEM((tokens, width), jnp.float32)],
         ),
         out_shape=jax.ShapeDtypeStruct((tokens, width), jnp.bfloat16),
     )(core.reshape(1), queries, near, own, other, gate_logits,
@@ -144,17 +148,16 @@
 
     mine, for_partner, first_rows = block_states(core, key_vectors, values)
     partner_half = lax.ppermute(for_partner, "head", pairs)
-    my_rows = mine + partner_half
     first_half = lax.ppermute(first_rows, "head", [(h, h + 1) for h in range(0, 2 * chips, 2)])
+    near, my_rows = near_attention(core, queries, key_vectors, values, first_half, partner_half, mine)
     devices = lax.axis_size("seq") * 2 * chips
-    outgoing = my_rows.astype(jnp.bfloat16).reshape(devices, -1, E)
+    outgoing = my_rows.reshape(devices, -1, E)
     incoming = lax.all_to_all(outgoing, ("seq", "head"), 0, 0, tiled=True)
     by_chip = incoming.reshape(devices // 2, 2, -1, E).astype(jnp.float32)
 
     running = jnp.cumsum(by_chip, axis=0)
     before = jnp.concatenate([jnp.zeros_like(running[:1]), running[:-1]], axis=0).astype(jnp.bfloat16)
     returned = lax.all_to_all(before.reshape(devices, -1, E), ("seq", "head"), 0, 0, tiled=True)
-    near = near_attention(core, queries, key_vectors, values, first_half, partner_half)
     own_rows = returned.reshape(heads, E // 2, E)
     other_rows = lax.ppermute(own_rows, "head", pairs)
     return gated_attention(core, queries, near, own_rows, other_rows, gate_logits, norm_gain)

time: 119 us -> 119 us (level)
  blocking collectives: 45.1 us -> 82 us
  waiting for transfers between devices: 34.6 us -> 6.04 us
  starting transfers between devices: 9.71 us -> 4.53 us
  other arithmetic: 3.03 us -> 0.25 us
    all_to_all x0 -> x1, blocking collectives: none -> 36.9 us  [on_device(): lax.all_to_all(before.reshape(devices, -1, E), ('seq', 'head'), 0, 0, til...]
    all_to_all x1 -> x0, waiting for transfers between devices: 30.6 us -> none  [on_device(): lax.all_to_all(before.reshape(devices, -1, E), ('seq', 'head'), 0, 0, til...]
    all_to_all x1 -> x0, starting transfers between devices: 5.18 us -> none  [on_device(): lax.all_to_all(before.reshape(devices, -1, E), ('seq', 'head'), 0, 0, til...]
    ppermute x1, waiting for transfers between devices: 0.01 us -> 4.07 us  [on_device(): lax.ppermute(first_rows, 'head', [(h, h + 1) for h in range(0, 2 * chips,...]
    ppermute x1, waiting for transfers between devices: 4 us -> 0.01 us  [on_device(): partner_half = lax.ppermute(for_partner, 'head', pairs)]
    convert_element_type x1 -> x0, other arithmetic: 2.78 us -> none  [on_device(): outgoing = my_rows.astype(jnp.bfloat16).reshape(devices, -1, E)]
    ppermute x1, waiting for transfers between devices: 0.01 us -> 1.96 us  [on_device(): other_rows = lax.ppermute(own_rows, 'head', pairs)]
  transfers between devices with their start and end apart: 4 -> 3, of which waited for: 2 -> 2; matrix products, arithmetic and copies ran while one was open for 1% -> 1% of each run, Pallas kernels for 6% -> 0%
where the time goes in v9:
time: 119 us
  blocking collectives  82 us (69%)
  Pallas kernels  22.4 us (19%)
  waiting for transfers between devices  6.04 us (5%)
  starting transfers between devices  4.53 us (4%)
  local copies, waits for them, and re-layouts  3.6 us (3%)
    all_to_all x1, blocking collectives, on_device(): incoming = lax.all_to_all(outgoing, ('seq', 'head'), 0, 0, tiled=True)  45.1 us
    all_to_all x1, blocking collectives, on_device(): lax.all_to_all(before.reshape(devices, -1, E), ('seq', 'head'), 0, 0, til...  36.9 us
    pallas_call x1, Pallas kernels, gated_attention(): pl.pallas_call(output_kernel, grid_spec=pltpu.PrefetchScalarGridSpec(num_...  8.69 us
    pallas_call x1, Pallas kernels, near_attention(): pl.pallas_call(near_kernel, grid_spec=pltpu.PrefetchScalarGridSpec(num_sc...  8.25 us
    pallas_call x1, Pallas kernels, block_states(): pl.pallas_call(state_kernel, grid_spec=pltpu.PrefetchScalarGridSpec(num_s...  5.49 us
    ppermute x1, waiting for transfers between devices, on_device(): lax.ppermute(first_rows, 'head', [(h, h + 1) for h in range(0, 2 * chips,...  4.07 us
    ppermute x1, starting transfers between devices, on_device(): partner_half = lax.ppermute(for_partner, 'head', pairs)  3.24 us
    unnamed x10, local copies, waits for them, and re-layouts  2.65 us
  transfers between devices with their start and end apart: 3, of which 2 were waited for; matrix products, arithmetic and copies ran while one was open for 1% of the time, Pallas kernels for 0%

profile of v9, /device:TPU:1, one launch (start us, length us, event | category | flops | bytes accessed | tf_op | source)
XLA Modules:
  0.0 118.9 jit_solution(15469918533798081959)
XLA Ops:
  0.0 5.5 %shard_map.55 = (f32[64,64,128]{2,1,0:T(8,128)}, f32[64,64,128]{2,1,0:T(8,128)}, bf16[64,64,128]{2,1,0:T(8,128)(2,1)}) custom-call(s32[1]{0:T(128)} %bitcast.core_ref, bf16[128,8192]{1,0:T(8,128)(2,1)} %key_ref.3, bf16[128,8192]{1,0:T(8,128)(2,1)} %value_ref.3), custom_call_target="tpu_custom_call" | custom-call | tf_op jit(solution)/shard_map/pallas_call | solution.py:33
  5.5 3.2 %collective-permute-start.1 = (f32[64,64,128]{2,1,0:T(8,128)}, f32[64,64,128]{2,1,0:T(8,128)S(1)}, u32[]{:S(2)}, u32[]{:S(2)}) collective-permute-start(f32[64,64,128]{2,1,0:T(8,128)} %get-tuple-element.11), channel_id=1, source_target_pairs={{0,1},{1,0},{2,3},{3,2},{4,5},{5,4},{6,7},{7,6},{8,9},{9,8},{10,11... | collective-permute-start | bytes 6291464 | tf_op jit(solution)/shard_map/ppermute | solution.py:150
  8.7 1.3 %collective-permute-start = (bf16[64,64,128]{2,1,0:T(8,128)(2,1)}, bf16[64,64,128]{2,1,0:T(8,128)(2,1)S(1)}, u32[]{:S(2)}, u32[]{:S(2)}) collective-permute-start(bf16[64,64,128]{2,1,0:T(8,128)(2,1)} %get-tuple-element.10), channel_id=1, source_target_pairs={{0,1},{2,3},{4,5},{6,7},{8,9},{10,11},{12,13},{14,15},{16,17},{18,... | collective-permute-start | bytes 3145736 | tf_op jit(solution)/shard_map/ppermute | solution.py:151
  10.0 4.1 %collective-permute-done.first_ref = bf16[64,64,128]{2,1,0:T(8,128)(2,1)S(1)} collective-permute-done((bf16[64,64,128]{2,1,0:T(8,128)(2,1)}, bf16[64,64,128]{2,1,0:T(8,128)(2,1)S(1)}, u32[]{:S(2)}, u32[]{:S(2)}) %collective-permute-start) | collective-permute-done | bytes 1048608 | tf_op jit(solution)/shard_map/ppermute | solution.py:151
  14.1 0.0 copy-start.2
  14.1 0.0 collective-permute-done.1.partner_ref
  14.1 0.0 copy-start.1
  14.1 1.0 copy-done.2
  15.1 0.6 copy-done.1
  15.7 8.3 %shard_map.56 = (f32[128,8192]{1,0:T(8,128)}, bf16[64,64,128]{2,1,0:T(8,128)(2,1)}) custom-call(s32[1]{0:T(128)} %bitcast.core_ref, bf16[128,8192]{1,0:T(8,128)(2,1)} %query_ref.3, bf16[128,8192]{1,0:T(8,128)(2,1)} %key_ref.3, bf16[128,8192]{1,0:T(8,128)(2,1)} %value_ref.3, bf16[64,64,128]{2,1,0:T(8,128)(2,1)} %copy-done.2, f32[64,64,128]{2,1,0:T(8,128)} %copy-done.1, ...), custom_call_target="tpu_custom_call" | custom-call | tf_op jit(solution)/shard_map/pallas_call | solution.py:68
  24.0 45.1 %all_to_all.10 = bf16[256,16,128]{2,1,0:T(8,128)(2,1)S(1)} all-to-all(bf16[256,16,128]{2,1,0:T(8,128)(2,1)} %bitcast.10), channel_id=1, replica_groups=mesh['seq'=16,'head'=16] {'seq','head'}, dimensions={0} | all-to-all | bytes 2097152 | tf_op jit(solution)/shard_map/all_to_all | solution.py:155
  69.1 0.2 fusion
  69.3 0.1 slice.7
  69.5 0.0 copy-start.4
  69.5 0.1 concatenate.3
  69.6 36.9 %all_to_all.11 = bf16[256,16,128]{2,1,0:T(8,128)(2,1)S(1)} all-to-all(bf16[256,16,128]{2,1,0:T(8,128)(2,1)S(1)} %bitcast.8), channel_id=1, replica_groups=mesh['seq'=16,'head'=16] {'seq','head'}, dimensions={0} | all-to-all | bytes 2097152 | tf_op jit(solution)/shard_map/all_to_all | solution.py:160
  106.5 0.0 copy-start
  106.5 0.0 collective-permute-start.2
  106.5 0.0 copy-done.4
  106.5 0.7 reshape.24.gain_ref
  107.2 2.0 %collective-permute-done.2.other_ref = bf16[64,64,128]{2,1,0:T(8,128)(2,1)S(1)} collective-permute-done((bf16[64,64,128]{2,1,0:T(8,128)(2,1)S(1)}, bf16[64,64,128]{2,1,0:T(8,128)(2,1)S(1)}, u32[]{:S(2)}, u32[]{:S(2)}) %collective-permute-start.2) | collective-permute-done | bytes 1048608 | tf_op jit(solution)/shard_map/ppermute | solution.py:162
  109.1 0.0 copy-done
  109.2 1.0 copy-done.3
  110.2 8.7 %shard_map.57 = bf16[128,8192]{1,0:T(8,128)(2,1)} custom-call(s32[1]{0:T(128)} %bitcast.core_ref, bf16[128,8192]{1,0:T(8,128)(2,1)} %query_ref.3, f32[128,8192]{1,0:T(8,128)} %get-tuple-element.13.near_ref, bf16[64,64,128]{2,1,0:T(8,128)(2,1)} %bitcast.7, bf16[64,64,128]{2,1,0:T(8,128)(2,1)} %copy-done.3, bf16[128,8192]{1,0:T(8,128)(2,1)} %gate_ref.1, ...), custom_call_target="tpu_custom_call" | custom-call | tf_op jit(solution)/shard_map/pallas_call | solution.py:127
  (1 shorter events, 0.0 us)
Async XLA Ops:
  5.5 8.6 %collective-permute-start.1 = (f32[64,64,128]{2,1,0:T(8,128)}, f32[64,64,128]{2,1,0:T(8,128)S(1)}, u32[]{:S(2)}, u32[]{:S(2)}) collective-permute-start(f32[64,64,128]{2,1,0:T(8,128)} %get-tuple-element.11), channel_id=1, source_target_pairs={{0,1},{1,0},{2,3},{3,2},{4,5},{5,4},{6,7},{7,6},{8,9},{9,8},{10,11... | collective-permute-start | bytes 6291464 | tf_op jit(solution)/shard_map/ppermute | solution.py:150
  8.7 5.4 %collective-permute-start = (bf16[64,64,128]{2,1,0:T(8,128)(2,1)}, bf16[64,64,128]{2,1,0:T(8,128)(2,1)S(1)}, u32[]{:S(2)}, u32[]{:S(2)}) collective-permute-start(bf16[64,64,128]{2,1,0:T(8,128)(2,1)} %get-tuple-element.10), channel_id=1, source_target_pairs={{0,1},{2,3},{4,5},{6,7},{8,9},{10,11},{12,13},{14,15},{16,17},{18,... | collective-permute-start | bytes 3145736 | tf_op jit(solution)/shard_map/ppermute | solution.py:151
  14.1 1.0 copy-start.2
  14.1 1.6 %copy-start.1 = (f32[64,64,128]{2,1,0:T(8,128)}, f32[64,64,128]{2,1,0:T(8,128)S(1)}, u32[]{:S(2)}) copy-start(f32[64,64,128]{2,1,0:T(8,128)S(1)} %collective-permute-done.1.partner_ref) | copy-start | bytes 6291460
  69.5 37.0 %copy-start.4 = (bf16[8192]{0:T(1024)(128)(2,1)S(1)}, bf16[8192]{0:T(1024)(128)(2,1)}, u32[]{:S(2)}) copy-start(bf16[8192]{0:T(1024)(128)(2,1)} %param.9) | copy-start | bytes 49156
  106.5 2.7 %copy-start = (bf16[256,16,128]{2,1,0:T(8,128)(2,1)}, bf16[256,16,128]{2,1,0:T(8,128)(2,1)S(1)}, u32[]{:S(2)}) copy-start(bf16[256,16,128]{2,1,0:T(8,128)(2,1)S(1)} %all_to_all.11) | copy-start | bytes 3145732
  106.5 2.7 %collective-permute-start.2 = (bf16[64,64,128]{2,1,0:T(8,128)(2,1)S(1)}, bf16[64,64,128]{2,1,0:T(8,128)(2,1)S(1)}, u32[]{:S(2)}, u32[]{:S(2)}) collective-permute-start(bf16[64,64,128]{2,1,0:T(8,128)(2,1)S(1)} %bitcast.6), channel_id=1, source_target_pairs={{0,1},{1,0},{2,3},{3,2},{4,5},{5,4},{6,7},{7,6},{8,9},{9,8},{10,11... | collective-permute-start | bytes 3145736 | tf_op jit(solution)/shard_map/ppermute | solution.py:162
  109.1 1.0 copy-start.3

commit v10 on v9

--- a/solution.py
+++ b/solution.py
@@ -6,7 +6,7 @@
 from jax.sharding import PartitionSpec as P
 
 E = 128
-GROUP = 16
+GROUP = 32
 
 
 def state_kernel(core_ref, key_ref, value_ref, mine_ref, partner_ref, first_ref):

time: 119 us -> 117 us (0.983)
  Pallas kernels: 22.4 us -> 20.3 us
where the time goes in v10:
time: 117 us
  blocking collectives  82 us (70%)
  Pallas kernels  20.3 us (17%)
  waiting for transfers between devices  6.04 us (5%)
  starting transfers between devices  4.52 us (4%)
  local copies, waits for them, and re-layouts  3.6 us (3%)
    all_to_all x1, blocking collectives, on_device(): incoming = lax.all_to_all(outgoing, ('seq', 'head'), 0, 0, tiled=True)  45.1 us
    all_to_all x1, blocking collectives, on_device(): lax.all_to_all(before.reshape(devices, -1, E), ('seq', 'head'), 0, 0, til...  36.9 us
    pallas_call x1, Pallas kernels, gated_attention(): pl.pallas_call(output_kernel, grid_spec=pltpu.PrefetchScalarGridSpec(num_...  8.46 us
    pallas_call x1, Pallas kernels, near_attention(): pl.pallas_call(near_kernel, grid_spec=pltpu.PrefetchScalarGridSpec(num_sc...  7.41 us
    pallas_call x1, Pallas kernels, block_states(): pl.pallas_call(state_kernel, grid_spec=pltpu.PrefetchScalarGridSpec(num_s...  4.39 us
    ppermute x1, waiting for transfers between devices, on_device(): lax.ppermute(first_rows, 'head', [(h, h + 1) for h in range(0, 2 * chips,...  4.07 us
    ppermute x1, starting transfers between devices, on_device(): partner_half = lax.ppermute(for_partner, 'head', pairs)  3.24 us
    unnamed x10, local copies, waits for them, and re-layouts  2.65 us
  transfers between devices with their start and end apart: 3, of which 2 were waited for; matrix products, arithmetic and copies ran while one was open for 1% of the time, Pallas kernels for 0%

profile of v10, /device:TPU:1, one launch (start us, length us, event | category | flops | bytes accessed | tf_op | source)
XLA Modules:
  0.0 116.7 jit_solution(9362955573449834338)
XLA Ops:
  0.0 4.4 %shard_map.55 = (f32[64,64,128]{2,1,0:T(8,128)}, f32[64,64,128]{2,1,0:T(8,128)}, bf16[64,64,128]{2,1,0:T(8,128)(2,1)}) custom-call(s32[1]{0:T(128)} %bitcast.core_ref, bf16[128,8192]{1,0:T(8,128)(2,1)} %key_ref.3, bf16[128,8192]{1,0:T(8,128)(2,1)} %value_ref.3), custom_call_target="tpu_custom_call" | custom-call | tf_op jit(solution)/shard_map/pallas_call | solution.py:33
  4.4 3.2 %collective-permute-start.1 = (f32[64,64,128]{2,1,0:T(8,128)}, f32[64,64,128]{2,1,0:T(8,128)S(1)}, u32[]{:S(2)}, u32[]{:S(2)}) collective-permute-start(f32[64,64,128]{2,1,0:T(8,128)} %get-tuple-element.11), channel_id=1, source_target_pairs={{0,1},{1,0},{2,3},{3,2},{4,5},{5,4},{6,7},{7,6},{8,9},{9,8},{10,11... | collective-permute-start | bytes 6291464 | tf_op jit(solution)/shard_map/ppermute | solution.py:150
  7.6 1.3 %collective-permute-start = (bf16[64,64,128]{2,1,0:T(8,128)(2,1)}, bf16[64,64,128]{2,1,0:T(8,128)(2,1)S(1)}, u32[]{:S(2)}, u32[]{:S(2)}) collective-permute-start(bf16[64,64,128]{2,1,0:T(8,128)(2,1)} %get-tuple-element.10), channel_id=1, source_target_pairs={{0,1},{2,3},{4,5},{6,7},{8,9},{10,11},{12,13},{14,15},{16,17},{18,... | collective-permute-start | bytes 3145736 | tf_op jit(solution)/shard_map/ppermute | solution.py:151
  8.9 4.1 %collective-permute-done.first_ref = bf16[64,64,128]{2,1,0:T(8,128)(2,1)S(1)} collective-permute-done((bf16[64,64,128]{2,1,0:T(8,128)(2,1)}, bf16[64,64,128]{2,1,0:T(8,128)(2,1)S(1)}, u32[]{:S(2)}, u32[]{:S(2)}) %collective-permute-start) | collective-permute-done | bytes 1048608 | tf_op jit(solution)/shard_map/ppermute | solution.py:151
  13.0 0.0 copy-start.2
  13.0 0.0 collective-permute-done.1.partner_ref
  13.0 0.0 copy-start.1
  13.0 1.0 copy-done.2
  14.0 0.6 copy-done.1
  14.6 7.4 %shard_map.56 = (f32[128,8192]{1,0:T(8,128)}, bf16[64,64,128]{2,1,0:T(8,128)(2,1)}) custom-call(s32[1]{0:T(128)} %bitcast.core_ref, bf16[128,8192]{1,0:T(8,128)(2,1)} %query_ref.3, bf16[128,8192]{1,0:T(8,128)(2,1)} %key_ref.3, bf16[128,8192]{1,0:T(8,128)(2,1)} %value_ref.3, bf16[64,64,128]{2,1,0:T(8,128)(2,1)} %copy-done.2, f32[64,64,128]{2,1,0:T(8,128)} %copy-done.1, ...), custom_call_target="tpu_custom_call" | custom-call | tf_op jit(solution)/shard_map/pallas_call | solution.py:68
  22.1 45.1 %all_to_all.10 = bf16[256,16,128]{2,1,0:T(8,128)(2,1)S(1)} all-to-all(bf16[256,16,128]{2,1,0:T(8,128)(2,1)} %bitcast.10), channel_id=1, replica_groups=mesh['seq'=16,'head'=16] {'seq','head'}, dimensions={0} | all-to-all | bytes 2097152 | tf_op jit(solution)/shard_map/all_to_all | solution.py:155
  67.1 0.2 fusion
  67.4 0.1 slice.7
  67.5 0.0 copy-start.4
  67.5 0.1 concatenate.3
  67.7 36.9 %all_to_all.11 = bf16[256,16,128]{2,1,0:T(8,128)(2,1)S(1)} all-to-all(bf16[256,16,128]{2,1,0:T(8,128)(2,1)S(1)} %bitcast.8), channel_id=1, replica_groups=mesh['seq'=16,'head'=16] {'seq','head'}, dimensions={0} | all-to-all | bytes 2097152 | tf_op jit(solution)/shard_map/all_to_all | solution.py:160
  104.5 0.0 copy-start
  104.5 0.0 collective-permute-start.2
  104.6 0.0 copy-done.4
  104.6 0.7 reshape.24.gain_ref
  105.3 2.0 %collective-permute-done.2.other_ref = bf16[64,64,128]{2,1,0:T(8,128)(2,1)S(1)} collective-permute-done((bf16[64,64,128]{2,1,0:T(8,128)(2,1)S(1)}, bf16[64,64,128]{2,1,0:T(8,128)(2,1)S(1)}, u32[]{:S(2)}, u32[]{:S(2)}) %collective-permute-start.2) | collective-permute-done | bytes 1048608 | tf_op jit(solution)/shard_map/ppermute | solution.py:162
  107.2 0.0 copy-done
  107.2 1.0 copy-done.3
  108.2 8.5 %shard_map.57 = bf16[128,8192]{1,0:T(8,128)(2,1)} custom-call(s32[1]{0:T(128)} %bitcast.core_ref, bf16[128,8192]{1,0:T(8,128)(2,1)} %query_ref.3, f32[128,8192]{1,0:T(8,128)} %get-tuple-element.13.near_ref, bf16[64,64,128]{2,1,0:T(8,128)(2,1)} %bitcast.7, bf16[64,64,128]{2,1,0:T(8,128)(2,1)} %copy-done.3, bf16[128,8192]{1,0:T(8,128)(2,1)} %gate_ref.1, ...), custom_call_target="tpu_custom_call" | custom-call | tf_op jit(solution)/shard_map/pallas_call | solution.py:127
  (1 shorter events, 0.0 us)
Async XLA Ops:
  4.4 8.6 %collective-permute-start.1 = (f32[64,64,128]{2,1,0:T(8,128)}, f32[64,64,128]{2,1,0:T(8,128)S(1)}, u32[]{:S(2)}, u32[]{:S(2)}) collective-permute-start(f32[64,64,128]{2,1,0:T(8,128)} %get-tuple-element.11), channel_id=1, source_target_pairs={{0,1},{1,0},{2,3},{3,2},{4,5},{5,4},{6,7},{7,6},{8,9},{9,8},{10,11... | collective-permute-start | bytes 6291464 | tf_op jit(solution)/shard_map/ppermute | solution.py:150
  7.6 5.4 %collective-permute-start = (bf16[64,64,128]{2,1,0:T(8,128)(2,1)}, bf16[64,64,128]{2,1,0:T(8,128)(2,1)S(1)}, u32[]{:S(2)}, u32[]{:S(2)}) collective-permute-start(bf16[64,64,128]{2,1,0:T(8,128)(2,1)} %get-tuple-element.10), channel_id=1, source_target_pairs={{0,1},{2,3},{4,5},{6,7},{8,9},{10,11},{12,13},{14,15},{16,17},{18,... | collective-permute-start | bytes 3145736 | tf_op jit(solution)/shard_map/ppermute | solution.py:151
  13.0 1.0 copy-start.2
  13.0 1.6 %copy-start.1 = (f32[64,64,128]{2,1,0:T(8,128)}, f32[64,64,128]{2,1,0:T(8,128)S(1)}, u32[]{:S(2)}) copy-start(f32[64,64,128]{2,1,0:T(8,128)S(1)} %collective-permute-done.1.partner_ref) | copy-start | bytes 6291460
  67.5 37.0 %copy-start.4 = (bf16[8192]{0:T(1024)(128)(2,1)S(1)}, bf16[8192]{0:T(1024)(128)(2,1)}, u32[]{:S(2)}) copy-start(bf16[8192]{0:T(1024)(128)(2,1)} %param.9) | copy-start | bytes 49156
  104.5 2.7 %copy-start = (bf16[256,16,128]{2,1,0:T(8,128)(2,1)}, bf16[256,16,128]{2,1,0:T(8,128)(2,1)S(1)}, u32[]{:S(2)}) copy-start(bf16[256,16,128]{2,1,0:T(8,128)(2,1)S(1)} %all_to_all.11) | copy-start | bytes 3145732
  104.5 2.7 %collective-permute-start.2 = (bf16[64,64,128]{2,1,0:T(8,128)(2,1)S(1)}, bf16[64,64,128]{2,1,0:T(8,128)(2,1)S(1)}, u32[]{:S(2)}, u32[]{:S(2)}) collective-permute-start(bf16[64,64,128]{2,1,0:T(8,128)(2,1)S(1)} %bitcast.6), channel_id=1, source_target_pairs={{0,1},{1,0},{2,3},{3,2},{4,5},{5,4},{6,7},{7,6},{8,9},{9,8},{10,11... | collective-permute-start | bytes 3145736 | tf_op jit(solution)/shard_map/ppermute | solution.py:162
  107.2 1.0 copy-start.3

commit v11 on v10

--- a/solution.py
+++ b/solution.py
@@ -40,27 +40,45 @@
     )(core.reshape(1), key_vectors, values)
 
 
-def near_kernel(core_ref, query_ref, key_ref, value_ref, first_ref, partner_ref, mine_ref, near_ref, chip_ref):
+def local_kernel(query_ref, key_ref, value_ref, local_ref):
     tokens = query_ref.shape[0]
-    first = core_ref[0] == 0
     lower_mask = lax.broadcasted_iota(jnp.int32, (tokens, tokens), 0) >= lax.broadcasted_iota(
         jnp.int32, (tokens, tokens), 1
     )
     for j in range(GROUP):
         cols = slice(j * E, (j + 1) * E)
-        query = query_ref[:, cols]
         scores = lax.dot_general(
-            query, key_ref[:, cols], (((1,), (1,)), ((), ())), preferred_element_type=jnp.float32
+            query_ref[:, cols], key_ref[:, cols], (((1,), (1,)), ((), ())),
+            preferred_element_type=jnp.float32,
         )
         weights = jnp.where(lower_mask, scores, 0.0).astype(jnp.bfloat16)
-        total = jnp.dot(weights, value_ref[:, cols], preferred_element_type=jnp.float32)
-        before = jnp.concatenate([first_ref[j], partner_ref[j].astype(jnp.bfloat16)], axis=0)
-        before_part = jnp.dot(query, before, preferred_element_type=jnp.float32)
-        near_ref[:, cols] = total + jnp.where(first, 0.0, before_part)
-        chip_ref[j] = (mine_ref[j] + partner_ref[j]).astype(jnp.bfloat16)
+        local_ref[:, cols] = jnp.dot(weights, value_ref[:, cols], preferred_element_type=jnp.float32)
 
 
-def near_attention(core, queries, key_vectors, values, first_half, partner_half, mine):
+def local_attention(queries, key_vectors, values):
+    tokens, width = queries.shape
+    cols = pl.BlockSpec((tokens, GROUP * E), lambda i: (0, i))
+    return pl.pallas_call(
+        local_kernel,
+        grid=(width // E // GROUP,),
+        in_specs=[cols, cols, cols],
+        out_specs=cols,
+        out_shape=jax.ShapeDtypeStruct((tokens, width), jnp.float32),
+    )(queries, key_vectors, values)
+
+
+def near_kernel(core_ref, query_ref, local_ref, first_ref, partner_ref, mine_ref, near_ref, chip_ref):
+    first = core_ref[0] == 0
+    for j in range(GROUP):
+        cols = slice(j * E, (j + 1) * E)
+        partner = partner_ref[j]
+        before = jnp.concatenate([first_ref[j], partner.astype(jnp.bfloat16)], axis=0)
+        before_part = jnp.dot(query_ref[:, cols], before, preferred_element_type=jnp.float32)
+        near_ref[:, cols] = local_ref[:, cols] + jnp.where(first, 0.0, before_part)
+        chip_ref[j] = (mine_ref[j] + partner).astype(jnp.bfloat16)
+
+
+def near_attention(core, queries, local, first_half, partner_half, mine):
     tokens, width = queries.shape
     heads = width // E
     cols = pl.BlockSpec((tokens, GROUP * E), lambda i, core: (0, i))
@@ -68,12 +86,12 @@
     return pl.pallas_call(
         near_kernel,
         grid_spec=pltpu.PrefetchScalarGridSpec(
-            num_scalar_prefetch=1, grid=(heads // GROUP,), in_specs=[cols, cols, cols, halves, halves, halves],
+            num_scalar_prefetch=1, grid=(heads // GROUP,), in_specs=[cols, cols, halves, halves, halves],
             out_specs=[cols, halves],
         ),
         out_shape=[jax.ShapeDtypeStruct((tokens, width), jnp.float32),
                    jax.ShapeDtypeStruct((heads, E // 2, E), jnp.bfloat16)],
-    )(core.reshape(1), queries, key_vectors, values, first_half, partner_half, mine)
+    )(core.reshape(1), queries, local, first_half, partner_half, mine)
 
 
 def output_kernel(core_ref, query_ref, near_ref, own_ref, other_ref, gate_ref, gain_ref,
@@ -149,7 +167,8 @@
     mine, for_partner, first_rows = block_states(core, key_vectors, values)
     partner_half = lax.ppermute(for_partner, "head", pairs)
     first_half = lax.ppermute(first_rows, "head", [(h, h + 1) for h in range(0, 2 * chips, 2)])
-    near, my_rows = near_attention(core, queries, key_vectors, values, first_half, partner_half, mine)
+    local = local_attention(queries, key_vectors, values)
+    near, my_rows = near_attention(core, queries, local, first_half, partner_half, mine)
     devices = lax.axis_size("seq") * 2 * chips
     outgoing = my_rows.reshape(devices, -1, E)
     incoming = lax.all_to_all(outgoing, ("seq", "head"), 0, 0, tiled=True)

time: 117 us -> 127 us (1.085)
  Pallas kernels: 20.3 us -> 33.1 us
  waiting for transfers between devices: 6.04 us -> 1.96 us
    pallas_call x0 -> x1, Pallas kernels: none -> 13.2 us  [local_attention(): pl.pallas_call(local_kernel, grid=(width // E // GROUP,), in_specs=[cols,...]
    ppermute x1, waiting for transfers between devices: 4.07 us -> 0.01 us  [on_device(): lax.ppermute(first_rows, 'head', [(h, h + 1) for h in range(0, 2 * chips,...]
  transfers between devices with their start and end apart: 3 -> 3, of which waited for: 2 -> 1; matrix products, arithmetic and copies ran while one was open for 1% -> 1% of each run, Pallas kernels for 0% -> 10%
where the time goes in v11:
time: 127 us
  blocking collectives  83 us (65%)
  Pallas kernels  33.1 us (26%)
  starting transfers between devices  4.52 us (4%)
  local copies, waits for them, and re-layouts  3.67 us (3%)
  waiting for transfers between devices  1.96 us (2%)
    all_to_all x1, blocking collectives, on_device(): incoming = lax.all_to_all(outgoing, ('seq', 'head'), 0, 0, tiled=True)  46.1 us
    all_to_all x1, blocking collectives, on_device(): lax.all_to_all(before.reshape(devices, -1, E), ('seq', 'head'), 0, 0, til...  36.9 us
    pallas_call x1, Pallas kernels, local_attention(): pl.pallas_call(local_kernel, grid=(width // E // GROUP,), in_specs=[cols,...  13.2 us
    pallas_call x1, Pallas kernels, gated_attention(): pl.pallas_call(output_kernel, grid_spec=pltpu.PrefetchScalarGridSpec(num_...  8.43 us
    pallas_call x1, Pallas kernels, near_attention(): pl.pallas_call(near_kernel, grid_spec=pltpu.PrefetchScalarGridSpec(num_sc...  6.99 us
    pallas_call x1, Pallas kernels, block_states(): pl.pallas_call(state_kernel, grid_spec=pltpu.PrefetchScalarGridSpec(num_s...  4.39 us
    ppermute x1, starting transfers between devices, on_device(): partner_half = lax.ppermute(for_partner, 'head', pairs)  3.24 us
    unnamed x10, local copies, waits for them, and re-layouts  2.73 us
  transfers between devices with their start and end apart: 3, of which 1 were waited for; matrix products, arithmetic and copies ran while one was open for 1% of the time, Pallas kernels for 10%

profile of v11, /device:TPU:1, one launch (start us, length us, event | category | flops | bytes accessed | tf_op | source)
XLA Modules:
  0.0 126.5 jit_solution(17741818180443913408)
XLA Ops:
  0.0 4.4 %shard_map.56 = (f32[64,64,128]{2,1,0:T(8,128)}, f32[64,64,128]{2,1,0:T(8,128)}, bf16[64,64,128]{2,1,0:T(8,128)(2,1)}) custom-call(s32[1]{0:T(128)} %bitcast.core_ref, bf16[128,8192]{1,0:T(8,128)(2,1)} %key_ref.3, bf16[128,8192]{1,0:T(8,128)(2,1)} %value_ref.3), custom_call_target="tpu_custom_call" | custom-call | tf_op jit(solution)/shard_map/pallas_call | solution.py:33
  4.4 3.2 %collective-permute-start.1 = (f32[64,64,128]{2,1,0:T(8,128)}, f32[64,64,128]{2,1,0:T(8,128)S(1)}, u32[]{:S(2)}, u32[]{:S(2)}) collective-permute-start(f32[64,64,128]{2,1,0:T(8,128)} %get-tuple-element.11), channel_id=1, source_target_pairs={{0,1},{1,0},{2,3},{3,2},{4,5},{5,4},{6,7},{7,6},{8,9},{9,8},{10,11... | collective-permute-start | bytes 6291464 | tf_op jit(solution)/shard_map/ppermute | solution.py:168
  7.6 1.3 %collective-permute-start = (bf16[64,64,128]{2,1,0:T(8,128)(2,1)}, bf16[64,64,128]{2,1,0:T(8,128)(2,1)S(1)}, u32[]{:S(2)}, u32[]{:S(2)}) collective-permute-start(bf16[64,64,128]{2,1,0:T(8,128)(2,1)} %get-tuple-element.10), channel_id=1, source_target_pairs={{0,1},{2,3},{4,5},{6,7},{8,9},{10,11},{12,13},{14,15},{16,17},{18,... | collective-permute-start | bytes 3145736 | tf_op jit(solution)/shard_map/ppermute | solution.py:169
  8.9 13.2 %shard_map.55.local_ref = f32[128,8192]{1,0:T(8,128)} custom-call(bf16[128,8192]{1,0:T(8,128)(2,1)} %query_ref.5, bf16[128,8192]{1,0:T(8,128)(2,1)} %key_ref.3, bf16[128,8192]{1,0:T(8,128)(2,1)} %value_ref.3), custom_call_target="tpu_custom_call" | custom-call | tf_op jit(solution)/shard_map/pallas_call | solution.py:61
  22.2 0.0 collective-permute-done.first_ref
  22.2 0.0 copy-start.2
  22.2 0.0 collective-permute-done.1.partner_ref
  22.2 0.0 copy-start.1
  22.2 1.0 copy-done.2
  23.2 0.7 copy-done.1
  23.9 7.0 %shard_map.57 = (f32[128,8192]{1,0:T(8,128)}, bf16[64,64,128]{2,1,0:T(8,128)(2,1)}) custom-call(s32[1]{0:T(128)} %bitcast.core_ref, bf16[128,8192]{1,0:T(8,128)(2,1)} %query_ref.5, f32[128,8192]{1,0:T(8,128)} %shard_map.55.local_ref, bf16[64,64,128]{2,1,0:T(8,128)(2,1)} %copy-done.2, f32[64,64,128]{2,1,0:T(8,128)} %copy-done.1, ...), custom_call_target="tpu_custom_call" | custom-call | tf_op jit(solution)/shard_map/pallas_call | solution.py:86
  30.9 46.1 %all_to_all.10 = bf16[256,16,128]{2,1,0:T(8,128)(2,1)S(1)} all-to-all(bf16[256,16,128]{2,1,0:T(8,128)(2,1)} %bitcast.10), channel_id=1, replica_groups=mesh['seq'=16,'head'=16] {'seq','head'}, dimensions={0} | all-to-all | bytes 2097152 | tf_op jit(solution)/shard_map/all_to_all | solution.py:174
  77.0 0.2 fusion
  77.2 0.1 slice.7
  77.4 0.0 copy-start.4
  77.4 0.1 concatenate.3
  77.5 36.9 %all_to_all.11 = bf16[256,16,128]{2,1,0:T(8,128)(2,1)S(1)} all-to-all(bf16[256,16,128]{2,1,0:T(8,128)(2,1)S(1)} %bitcast.8), channel_id=1, replica_groups=mesh['seq'=16,'head'=16] {'seq','head'}, dimensions={0} | all-to-all | bytes 2097152 | tf_op jit(solution)/shard_map/all_to_all | solution.py:179
  114.4 0.0 collective-permute-start.2
  114.4 0.0 copy-done.4
  114.4 0.7 reshape.24.gain_ref
  115.1 2.0 %collective-permute-done.2.other_ref = bf16[64,64,128]{2,1,0:T(8,128)(2,1)S(1)} collective-permute-done((bf16[64,64,128]{2,1,0:T(8,128)(2,1)S(1)}, bf16[64,64,128]{2,1,0:T(8,128)(2,1)S(1)}, u32[]{:S(2)}, u32[]{:S(2)}) %collective-permute-start.2) | collective-permute-done | bytes 1048608 | tf_op jit(solution)/shard_map/ppermute | solution.py:181
  117.1 0.0 copy-done
  117.1 1.0 copy-done.3
  118.1 8.4 %shard_map.58 = bf16[128,8192]{1,0:T(8,128)(2,1)} custom-call(s32[1]{0:T(128)} %bitcast.core_ref, bf16[128,8192]{1,0:T(8,128)(2,1)} %query_ref.5, f32[128,8192]{1,0:T(8,128)} %get-tuple-element.13.near_ref, bf16[64,64,128]{2,1,0:T(8,128)(2,1)} %bitcast.7, bf16[64,64,128]{2,1,0:T(8,128)(2,1)} %copy-done.3, bf16[128,8192]{1,0:T(8,128)(2,1)} %gate_ref.1, ...), custom_call_target="tpu_custom_call" | custom-call | tf_op jit(solution)/shard_map/pallas_call | solution.py:145
  (2 shorter events, 0.0 us)
Async XLA Ops:
  4.4 17.8 %collective-permute-start.1 = (f32[64,64,128]{2,1,0:T(8,128)}, f32[64,64,128]{2,1,0:T(8,128)S(1)}, u32[]{:S(2)}, u32[]{:S(2)}) collective-permute-start(f32[64,64,128]{2,1,0:T(8,128)} %get-tuple-element.11), channel_id=1, source_target_pairs={{0,1},{1,0},{2,3},{3,2},{4,5},{5,4},{6,7},{7,6},{8,9},{9,8},{10,11... | collective-permute-start | bytes 6291464 | tf_op jit(solution)/shard_map/ppermute | solution.py:168
  7.6 14.5 %collective-permute-start = (bf16[64,64,128]{2,1,0:T(8,128)(2,1)}, bf16[64,64,128]{2,1,0:T(8,128)(2,1)S(1)}, u32[]{:S(2)}, u32[]{:S(2)}) collective-permute-start(bf16[64,64,128]{2,1,0:T(8,128)(2,1)} %get-tuple-element.10), channel_id=1, source_target_pairs={{0,1},{2,3},{4,5},{6,7},{8,9},{10,11},{12,13},{14,15},{16,17},{18,... | collective-permute-start | bytes 3145736 | tf_op jit(solution)/shard_map/ppermute | solution.py:169
  22.2 1.0 copy-start.2
  22.2 1.7 %copy-start.1 = (f32[64,64,128]{2,1,0:T(8,128)}, f32[64,64,128]{2,1,0:T(8,128)S(1)}, u32[]{:S(2)}) copy-start(f32[64,64,128]{2,1,0:T(8,128)S(1)} %collective-permute-done.1.partner_ref) | copy-start | bytes 6291460
  77.4 37.0 %copy-start.4 = (bf16[8192]{0:T(1024)(128)(2,1)S(1)}, bf16[8192]{0:T(1024)(128)(2,1)}, u32[]{:S(2)}) copy-start(bf16[8192]{0:T(1024)(128)(2,1)} %param.9) | copy-start | bytes 49156
  114.4 2.7 %copy-start = (bf16[256,16,128]{2,1,0:T(8,128)(2,1)}, bf16[256,16,128]{2,1,0:T(8,128)(2,1)S(1)}, u32[]{:S(2)}) copy-start(bf16[256,16,128]{2,1,0:T(8,128)(2,1)S(1)} %all_to_all.11) | copy-start | bytes 3145732
  114.4 2.7 %collective-permute-start.2 = (bf16[64,64,128]{2,1,0:T(8,128)(2,1)S(1)}, bf16[64,64,128]{2,1,0:T(8,128)(2,1)S(1)}, u32[]{:S(2)}, u32[]{:S(2)}) collective-permute-start(bf16[64,64,128]{2,1,0:T(8,128)(2,1)S(1)} %bitcast.6), channel_id=1, source_target_pairs={{0,1},{1,0},{2,3},{3,2},{4,5},{5,4},{6,7},{7,6},{8,9},{9,8},{10,11... | collective-permute-start | bytes 3145736 | tf_op jit(solution)/shard_map/ppermute | solution.py:181
  117.1 1.0 copy-start.3

commit v12 on v10

--- a/solution.py
+++ b/solution.py
@@ -148,7 +148,7 @@
 
     mine, for_partner, first_rows = block_states(core, key_vectors, values)
     partner_half = lax.ppermute(for_partner, "head", pairs)
-    first_half = lax.ppermute(first_rows, "head", [(h, h + 1) for h in range(0, 2 * chips, 2)])
+    first_half = lax.ppermute(first_rows, "head", pairs)
     near, my_rows = near_attention(core, queries, key_vectors, values, first_half, partner_half, mine)
     devices = lax.axis_size("seq") * 2 * chips
     outgoing = my_rows.reshape(devices, -1, E)

time: 117 us -> 117 us (level)
  waiting for transfers between devices: 6.04 us -> 7.45 us
  starting transfers between devices: 4.52 us -> 3.25 us
    ppermute x1, waiting for transfers between devices: 4.07 us -> 5.49 us  [on_device(): first_half = lax.ppermute(first_rows, 'head', pairs)]
    ppermute x1, starting transfers between devices: 1.28 us -> 0.01 us  [on_device(): first_half = lax.ppermute(first_rows, 'head', pairs)]
where the time goes in v12:
time: 117 us
  blocking collectives  82.2 us (70%)
  Pallas kernels  20.3 us (17%)
  waiting for transfers between devices  7.45 us (6%)
  local copies, waits for them, and re-layouts  3.6 us (3%)
  starting transfers between devices  3.25 us (3%)
    all_to_all x1, blocking collectives, on_device(): incoming = lax.all_to_all(outgoing, ('seq', 'head'), 0, 0, tiled=True)  45.3 us
    all_to_all x1, blocking collectives, on_device(): lax.all_to_all(before.reshape(devices, -1, E), ('seq', 'head'), 0, 0, til...  36.9 us
    pallas_call x1, Pallas kernels, gated_attention(): pl.pallas_call(output_kernel, grid_spec=pltpu.PrefetchScalarGridSpec(num_...  8.45 us
    pallas_call x1, Pallas kernels, near_attention(): pl.pallas_call(near_kernel, grid_spec=pltpu.PrefetchScalarGridSpec(num_sc...  7.41 us
    ppermute x1, waiting for transfers between devices, on_device(): first_half = lax.ppermute(first_rows, 'head', pairs)  5.49 us
    pallas_call x1, Pallas kernels, block_states(): pl.pallas_call(state_kernel, grid_spec=pltpu.PrefetchScalarGridSpec(num_s...  4.39 us
    ppermute x1, starting transfers between devices, on_device(): partner_half = lax.ppermute(for_partner, 'head', pairs)  3.24 us
    unnamed x10, local copies, waits for them, and re-layouts  2.65 us
  transfers between devices with their start and end apart: 3, of which 2 were waited for; matrix products, arithmetic and copies ran while one was open for 1% of the time, Pallas kernels for 0%

profile of v12, /device:TPU:1, one launch (start us, length us, event | category | flops | bytes accessed | tf_op | source)
XLA Modules:
  0.0 117.0 jit_solution(13832229253171182276)
XLA Ops:
  0.0 4.4 %shard_map.55 = (f32[64,64,128]{2,1,0:T(8,128)}, f32[64,64,128]{2,1,0:T(8,128)}, bf16[64,64,128]{2,1,0:T(8,128)(2,1)}) custom-call(s32[1]{0:T(128)} %bitcast.core_ref, bf16[128,8192]{1,0:T(8,128)(2,1)} %key_ref.3, bf16[128,8192]{1,0:T(8,128)(2,1)} %value_ref.3), custom_call_target="tpu_custom_call" | custom-call | tf_op jit(solution)/shard_map/pallas_call | solution.py:33
  4.4 3.2 %collective-permute-start.1 = (f32[64,64,128]{2,1,0:T(8,128)}, f32[64,64,128]{2,1,0:T(8,128)S(1)}, u32[]{:S(2)}, u32[]{:S(2)}) collective-permute-start(f32[64,64,128]{2,1,0:T(8,128)} %get-tuple-element.11), channel_id=1, source_target_pairs={{0,1},{1,0},{2,3},{3,2},{4,5},{5,4},{6,7},{7,6},{8,9},{9,8},{10,11... | collective-permute-start | bytes 6291464 | tf_op jit(solution)/shard_map/ppermute | solution.py:150
  7.6 0.0 collective-permute-start
  7.6 5.5 %collective-permute-done.first_ref = bf16[64,64,128]{2,1,0:T(8,128)(2,1)S(1)} collective-permute-done((bf16[64,64,128]{2,1,0:T(8,128)(2,1)}, bf16[64,64,128]{2,1,0:T(8,128)(2,1)S(1)}, u32[]{:S(2)}, u32[]{:S(2)}) %collective-permute-start) | collective-permute-done | bytes 1048608 | tf_op jit(solution)/shard_map/ppermute | solution.py:151
  13.1 0.0 copy-start.2
  13.1 0.0 collective-permute-done.1.partner_ref
  13.1 0.0 copy-start.1
  13.1 1.0 copy-done.2
  14.1 0.6 copy-done.1
  14.8 7.4 %shard_map.56 = (f32[128,8192]{1,0:T(8,128)}, bf16[64,64,128]{2,1,0:T(8,128)(2,1)}) custom-call(s32[1]{0:T(128)} %bitcast.core_ref, bf16[128,8192]{1,0:T(8,128)(2,1)} %query_ref.3, bf16[128,8192]{1,0:T(8,128)(2,1)} %key_ref.3, bf16[128,8192]{1,0:T(8,128)(2,1)} %value_ref.3, bf16[64,64,128]{2,1,0:T(8,128)(2,1)} %copy-done.2, f32[64,64,128]{2,1,0:T(8,128)} %copy-done.1, ...), custom_call_target="tpu_custom_call" | custom-call | tf_op jit(solution)/shard_map/pallas_call | solution.py:68
  22.2 45.3 %all_to_all.10 = bf16[256,16,128]{2,1,0:T(8,128)(2,1)S(1)} all-to-all(bf16[256,16,128]{2,1,0:T(8,128)(2,1)} %bitcast.10), channel_id=1, replica_groups=mesh['seq'=16,'head'=16] {'seq','head'}, dimensions={0} | all-to-all | bytes 2097152 | tf_op jit(solution)/shard_map/all_to_all | solution.py:155
  67.5 0.2 fusion
  67.7 0.1 slice.7
  67.9 0.0 copy-start.4
  67.9 0.1 concatenate.3
  68.0 36.9 %all_to_all.11 = bf16[256,16,128]{2,1,0:T(8,128)(2,1)S(1)} all-to-all(bf16[256,16,128]{2,1,0:T(8,128)(2,1)S(1)} %bitcast.8), channel_id=1, replica_groups=mesh['seq'=16,'head'=16] {'seq','head'}, dimensions={0} | all-to-all | bytes 2097152 | tf_op jit(solution)/shard_map/all_to_all | solution.py:160
  104.9 0.0 copy-start
  104.9 0.0 collective-permute-start.2
  104.9 0.0 copy-done.4
  104.9 0.7 reshape.24.gain_ref
  105.6 2.0 %collective-permute-done.2.other_ref = bf16[64,64,128]{2,1,0:T(8,128)(2,1)S(1)} collective-permute-done((bf16[64,64,128]{2,1,0:T(8,128)(2,1)S(1)}, bf16[64,64,128]{2,1,0:T(8,128)(2,1)S(1)}, u32[]{:S(2)}, u32[]{:S(2)}) %collective-permute-start.2) | collective-permute-done | bytes 1048608 | tf_op jit(solution)/shard_map/ppermute | solution.py:162
  107.6 0.0 copy-done
  107.6 1.0 copy-done.3
  108.6 8.5 %shard_map.57 = bf16[128,8192]{1,0:T(8,128)(2,1)} custom-call(s32[1]{0:T(128)} %bitcast.core_ref, bf16[128,8192]{1,0:T(8,128)(2,1)} %query_ref.3, f32[128,8192]{1,0:T(8,128)} %get-tuple-element.13.near_ref, bf16[64,64,128]{2,1,0:T(8,128)(2,1)} %bitcast.7, bf16[64,64,128]{2,1,0:T(8,128)(2,1)} %copy-done.3, bf16[128,8192]{1,0:T(8,128)(2,1)} %gate_ref.1, ...), custom_call_target="tpu_custom_call" | custom-call | tf_op jit(solution)/shard_map/pallas_call | solution.py:127
  (1 shorter events, 0.0 us)
Async XLA Ops:
  4.4 8.7 %collective-permute-start.1 = (f32[64,64,128]{2,1,0:T(8,128)}, f32[64,64,128]{2,1,0:T(8,128)S(1)}, u32[]{:S(2)}, u32[]{:S(2)}) collective-permute-start(f32[64,64,128]{2,1,0:T(8,128)} %get-tuple-element.11), channel_id=1, source_target_pairs={{0,1},{1,0},{2,3},{3,2},{4,5},{5,4},{6,7},{7,6},{8,9},{9,8},{10,11... | collective-permute-start | bytes 6291464 | tf_op jit(solution)/shard_map/ppermute | solution.py:150
  7.6 5.5 %collective-permute-start = (bf16[64,64,128]{2,1,0:T(8,128)(2,1)}, bf16[64,64,128]{2,1,0:T(8,128)(2,1)S(1)}, u32[]{:S(2)}, u32[]{:S(2)}) collective-permute-start(bf16[64,64,128]{2,1,0:T(8,128)(2,1)} %get-tuple-element.10), channel_id=1, source_target_pairs={{0,1},{1,0},{2,3},{3,2},{4,5},{5,4},{6,7},{7,6},{8,9},{9,8},{10,11... | collective-permute-start | bytes 3145736 | tf_op jit(solution)/shard_map/ppermute | solution.py:151
  13.1 1.0 copy-start.2
  13.1 1.6 %copy-start.1 = (f32[64,64,128]{2,1,0:T(8,128)}, f32[64,64,128]{2,1,0:T(8,128)S(1)}, u32[]{:S(2)}) copy-start(f32[64,64,128]{2,1,0:T(8,128)S(1)} %collective-permute-done.1.partner_ref) | copy-start | bytes 6291460
  67.9 37.0 %copy-start.4 = (bf16[8192]{0:T(1024)(128)(2,1)S(1)}, bf16[8192]{0:T(1024)(128)(2,1)}, u32[]{:S(2)}) copy-start(bf16[8192]{0:T(1024)(128)(2,1)} %param.9) | copy-start | bytes 49156
  104.9 2.7 %copy-start = (bf16[256,16,128]{2,1,0:T(8,128)(2,1)}, bf16[256,16,128]{2,1,0:T(8,128)(2,1)S(1)}, u32[]{:S(2)}) copy-start(bf16[256,16,128]{2,1,0:T(8,128)(2,1)S(1)} %all_to_all.11) | copy-start | bytes 3145732
  104.9 2.7 %collective-permute-start.2 = (bf16[64,64,128]{2,1,0:T(8,128)(2,1)S(1)}, bf16[64,64,128]{2,1,0:T(8,128)(2,1)S(1)}, u32[]{:S(2)}, u32[]{:S(2)}) collective-permute-start(bf16[64,64,128]{2,1,0:T(8,128)(2,1)S(1)} %bitcast.6), channel_id=1, source_target_pairs={{0,1},{1,0},{2,3},{3,2},{4,5},{5,4},{6,7},{7,6},{8,9},{9,8},{10,11... | collective-permute-start | bytes 3145736 | tf_op jit(solution)/shard_map/ppermute | solution.py:162
  107.6 1.0 copy-start.3

commit v13 on v10

--- a/solution.py
+++ b/solution.py
@@ -97,7 +97,8 @@
         features = attended.astype(jnp.float32)
         square_ref[...] += features * features
         gate = gate_ref[:, cols].astype(jnp.float32)
-        opening_ref[:, pl.ds(start, E)] = 1.0 / (1.0 + jnp.exp(-gate))
+        gain = gain_ref[:, pl.ds(start, E)].astype(jnp.float32)
+        opening_ref[:, pl.ds(start, E)] = gain * (0.5 + 0.5 * jnp.tanh(0.5 * gate))
 
     @pl.when(step == pl.num_programs(0) - 1)
     def _():
@@ -109,9 +110,7 @@
             start = pl.multiple_of(c * E, E)
             window = pl.ds(start, E)
             features = attended_ref[:, window].astype(jnp.float32)
-            gain = gain_ref[:, window].astype(jnp.float32)
-            scaled = features * scale * gain
-            scaled = scaled * opening_ref[:, window]
+            scaled = features * scale * opening_ref[:, window]
             out_ref[:, window] = scaled.astype(out_ref.dtype)
             return carry
 

time: 117 us -> 117 us (level)
  no operation moved by 1% of the time
where the time goes in v13:
time: 117 us
  blocking collectives  82 us (70%)
  Pallas kernels  20.4 us (17%)
  waiting for transfers between devices  6.04 us (5%)
  starting transfers between devices  4.52 us (4%)
  local copies, waits for them, and re-layouts  3.6 us (3%)
    all_to_all x1, blocking collectives, on_device(): incoming = lax.all_to_all(outgoing, ('seq', 'head'), 0, 0, tiled=True)  45.1 us
    all_to_all x1, blocking collectives, on_device(): lax.all_to_all(before.reshape(devices, -1, E), ('seq', 'head'), 0, 0, til...  36.9 us
    pallas_call x1, Pallas kernels, gated_attention(): pl.pallas_call(output_kernel, grid_spec=pltpu.PrefetchScalarGridSpec(num_...  8.63 us
    pallas_call x1, Pallas kernels, near_attention(): pl.pallas_call(near_kernel, grid_spec=pltpu.PrefetchScalarGridSpec(num_sc...  7.41 us
    pallas_call x1, Pallas kernels, block_states(): pl.pallas_call(state_kernel, grid_spec=pltpu.PrefetchScalarGridSpec(num_s...  4.39 us
    ppermute x1, waiting for transfers between devices, on_device(): lax.ppermute(first_rows, 'head', [(h, h + 1) for h in range(0, 2 * chips,...  4.07 us
    ppermute x1, starting transfers between devices, on_device(): partner_half = lax.ppermute(for_partner, 'head', pairs)  3.24 us
    unnamed x10, local copies, waits for them, and re-layouts  2.65 us
  transfers between devices with their start and end apart: 3, of which 2 were waited for; matrix products, arithmetic and copies ran while one was open for 1% of the time, Pallas kernels for 0%

profile of v13, /device:TPU:1, one launch (start us, length us, event | category | flops | bytes accessed | tf_op | source)
XLA Modules:
  0.0 116.9 jit_solution(17264655987157579774)
XLA Ops:
  0.0 4.4 %shard_map.55 = (f32[64,64,128]{2,1,0:T(8,128)}, f32[64,64,128]{2,1,0:T(8,128)}, bf16[64,64,128]{2,1,0:T(8,128)(2,1)}) custom-call(s32[1]{0:T(128)} %bitcast.core_ref, bf16[128,8192]{1,0:T(8,128)(2,1)} %key_ref.3, bf16[128,8192]{1,0:T(8,128)(2,1)} %value_ref.3), custom_call_target="tpu_custom_call" | custom-call | tf_op jit(solution)/shard_map/pallas_call | solution.py:33
  4.4 3.2 %collective-permute-start.1 = (f32[64,64,128]{2,1,0:T(8,128)}, f32[64,64,128]{2,1,0:T(8,128)S(1)}, u32[]{:S(2)}, u32[]{:S(2)}) collective-permute-start(f32[64,64,128]{2,1,0:T(8,128)} %get-tuple-element.11), channel_id=1, source_target_pairs={{0,1},{1,0},{2,3},{3,2},{4,5},{5,4},{6,7},{7,6},{8,9},{9,8},{10,11... | collective-permute-start | bytes 6291464 | tf_op jit(solution)/shard_map/ppermute | solution.py:149
  7.6 1.3 %collective-permute-start = (bf16[64,64,128]{2,1,0:T(8,128)(2,1)}, bf16[64,64,128]{2,1,0:T(8,128)(2,1)S(1)}, u32[]{:S(2)}, u32[]{:S(2)}) collective-permute-start(bf16[64,64,128]{2,1,0:T(8,128)(2,1)} %get-tuple-element.10), channel_id=1, source_target_pairs={{0,1},{2,3},{4,5},{6,7},{8,9},{10,11},{12,13},{14,15},{16,17},{18,... | collective-permute-start | bytes 3145736 | tf_op jit(solution)/shard_map/ppermute | solution.py:150
  8.9 4.1 %collective-permute-done.first_ref = bf16[64,64,128]{2,1,0:T(8,128)(2,1)S(1)} collective-permute-done((bf16[64,64,128]{2,1,0:T(8,128)(2,1)}, bf16[64,64,128]{2,1,0:T(8,128)(2,1)S(1)}, u32[]{:S(2)}, u32[]{:S(2)}) %collective-permute-start) | collective-permute-done | bytes 1048608 | tf_op jit(solution)/shard_map/ppermute | solution.py:150
  13.0 0.0 copy-start.2
  13.0 0.0 collective-permute-done.1.partner_ref
  13.0 0.0 copy-start.1
  13.0 1.0 copy-done.2
  14.0 0.6 copy-done.1
  14.6 7.4 %shard_map.56 = (f32[128,8192]{1,0:T(8,128)}, bf16[64,64,128]{2,1,0:T(8,128)(2,1)}) custom-call(s32[1]{0:T(128)} %bitcast.core_ref, bf16[128,8192]{1,0:T(8,128)(2,1)} %query_ref.3, bf16[128,8192]{1,0:T(8,128)(2,1)} %key_ref.3, bf16[128,8192]{1,0:T(8,128)(2,1)} %value_ref.3, bf16[64,64,128]{2,1,0:T(8,128)(2,1)} %copy-done.2, f32[64,64,128]{2,1,0:T(8,128)} %copy-done.1, ...), custom_call_target="tpu_custom_call" | custom-call | tf_op jit(solution)/shard_map/pallas_call | solution.py:68
  22.1 45.1 %all_to_all.10 = bf16[256,16,128]{2,1,0:T(8,128)(2,1)S(1)} all-to-all(bf16[256,16,128]{2,1,0:T(8,128)(2,1)} %bitcast.10), channel_id=1, replica_groups=mesh['seq'=16,'head'=16] {'seq','head'}, dimensions={0} | all-to-all | bytes 2097152 | tf_op jit(solution)/shard_map/all_to_all | solution.py:154
  67.1 0.2 fusion
  67.4 0.1 slice.7
  67.5 0.0 copy-start.4
  67.5 0.1 concatenate.3
  67.7 36.9 %all_to_all.11 = bf16[256,16,128]{2,1,0:T(8,128)(2,1)S(1)} all-to-all(bf16[256,16,128]{2,1,0:T(8,128)(2,1)S(1)} %bitcast.8), channel_id=1, replica_groups=mesh['seq'=16,'head'=16] {'seq','head'}, dimensions={0} | all-to-all | bytes 2097152 | tf_op jit(solution)/shard_map/all_to_all | solution.py:159
  104.5 0.0 copy-start
  104.5 0.0 collective-permute-start.2
  104.6 0.0 copy-done.4
  104.6 0.7 reshape.24.gain_ref
  105.3 2.0 %collective-permute-done.2.other_ref = bf16[64,64,128]{2,1,0:T(8,128)(2,1)S(1)} collective-permute-done((bf16[64,64,128]{2,1,0:T(8,128)(2,1)S(1)}, bf16[64,64,128]{2,1,0:T(8,128)(2,1)S(1)}, u32[]{:S(2)}, u32[]{:S(2)}) %collective-permute-start.2) | collective-permute-done | bytes 1048608 | tf_op jit(solution)/shard_map/ppermute | solution.py:161
  107.2 0.0 copy-done
  107.2 1.0 copy-done.3
  108.2 8.6 %shard_map.57 = bf16[128,8192]{1,0:T(8,128)(2,1)} custom-call(s32[1]{0:T(128)} %bitcast.core_ref, bf16[128,8192]{1,0:T(8,128)(2,1)} %query_ref.3, f32[128,8192]{1,0:T(8,128)} %get-tuple-element.13.near_ref, bf16[64,64,128]{2,1,0:T(8,128)(2,1)} %bitcast.7, bf16[64,64,128]{2,1,0:T(8,128)(2,1)} %copy-done.3, bf16[128,8192]{1,0:T(8,128)(2,1)} %gate_ref.1, ...), custom_call_target="tpu_custom_call" | custom-call | tf_op jit(solution)/shard_map/pallas_call | solution.py:126
  (1 shorter events, 0.0 us)
Async XLA Ops:
  4.4 8.6 %collective-permute-start.1 = (f32[64,64,128]{2,1,0:T(8,128)}, f32[64,64,128]{2,1,0:T(8,128)S(1)}, u32[]{:S(2)}, u32[]{:S(2)}) collective-permute-start(f32[64,64,128]{2,1,0:T(8,128)} %get-tuple-element.11), channel_id=1, source_target_pairs={{0,1},{1,0},{2,3},{3,2},{4,5},{5,4},{6,7},{7,6},{8,9},{9,8},{10,11... | collective-permute-start | bytes 6291464 | tf_op jit(solution)/shard_map/ppermute | solution.py:149
  7.6 5.4 %collective-permute-start = (bf16[64,64,128]{2,1,0:T(8,128)(2,1)}, bf16[64,64,128]{2,1,0:T(8,128)(2,1)S(1)}, u32[]{:S(2)}, u32[]{:S(2)}) collective-permute-start(bf16[64,64,128]{2,1,0:T(8,128)(2,1)} %get-tuple-element.10), channel_id=1, source_target_pairs={{0,1},{2,3},{4,5},{6,7},{8,9},{10,11},{12,13},{14,15},{16,17},{18,... | collective-permute-start | bytes 3145736 | tf_op jit(solution)/shard_map/ppermute | solution.py:150
  13.0 1.0 copy-start.2
  13.0 1.6 %copy-start.1 = (f32[64,64,128]{2,1,0:T(8,128)}, f32[64,64,128]{2,1,0:T(8,128)S(1)}, u32[]{:S(2)}) copy-start(f32[64,64,128]{2,1,0:T(8,128)S(1)} %collective-permute-done.1.partner_ref) | copy-start | bytes 6291460
  67.5 37.0 %copy-start.4 = (bf16[8192]{0:T(1024)(128)(2,1)S(1)}, bf16[8192]{0:T(1024)(128)(2,1)}, u32[]{:S(2)}) copy-start(bf16[8192]{0:T(1024)(128)(2,1)} %param.9) | copy-start | bytes 49156
  104.5 2.7 %copy-start = (bf16[256,16,128]{2,1,0:T(8,128)(2,1)}, bf16[256,16,128]{2,1,0:T(8,128)(2,1)S(1)}, u32[]{:S(2)}) copy-start(bf16[256,16,128]{2,1,0:T(8,128)(2,1)S(1)} %all_to_all.11) | copy-start | bytes 3145732
  104.5 2.7 %collective-permute-start.2 = (bf16[64,64,128]{2,1,0:T(8,128)(2,1)S(1)}, bf16[64,64,128]{2,1,0:T(8,128)(2,1)S(1)}, u32[]{:S(2)}, u32[]{:S(2)}) collective-permute-start(bf16[64,64,128]{2,1,0:T(8,128)(2,1)S(1)} %bitcast.6), channel_id=1, source_target_pairs={{0,1},{1,0},{2,3},{3,2},{4,5},{5,4},{6,7},{7,6},{8,9},{9,8},{10,11... | collective-permute-start | bytes 3145736 | tf_op jit(solution)/shard_map/ppermute | solution.py:161
  107.2 1.0 copy-start.3

commit v14 on v13

--- a/solution.py
+++ b/solution.py
@@ -3,6 +3,7 @@
 from jax import lax
 from jax.experimental import pallas as pl
 from jax.experimental.pallas import tpu as pltpu
+from jax.sharding import Mesh
 from jax.sharding import PartitionSpec as P
 
 E = 128
@@ -141,32 +142,34 @@
 
 def on_device(queries, key_vectors, values, gate_logits, norm_gain):
     heads = queries.shape[1] // E
-    chips = lax.axis_size("head") // 2
-    core = lax.axis_index("head") % 2
-    pairs = [(h, h ^ 1) for h in range(2 * chips)]
+    chips = lax.axis_size("z")
+    core = lax.axis_index("core")
+    pairs = [(0, 1), (1, 0)]
 
     mine, for_partner, first_rows = block_states(core, key_vectors, values)
-    partner_half = lax.ppermute(for_partner, "head", pairs)
-    first_half = lax.ppermute(first_rows, "head", [(h, h + 1) for h in range(0, 2 * chips, 2)])
+    partner_half = lax.ppermute(for_partner, "core", pairs)
+    first_half = lax.ppermute(first_rows, "core", [(0, 1)])
     near, my_rows = near_attention(core, queries, key_vectors, values, first_half, partner_half, mine)
-    devices = lax.axis_size("seq") * 2 * chips
-    outgoing = my_rows.reshape(devices, -1, E)
-    incoming = lax.all_to_all(outgoing, ("seq", "head"), 0, 0, tiled=True)
-    by_chip = incoming.reshape(devices // 2, 2, -1, E).astype(jnp.float32)
+    owners = lax.axis_size("seq") * chips
+    outgoing = my_rows.reshape(owners, -1, E)
+    by_chip = lax.all_to_all(outgoing, ("seq", "z"), 0, 0, tiled=True).astype(jnp.float32)
 
     running = jnp.cumsum(by_chip, axis=0)
     before = jnp.concatenate([jnp.zeros_like(running[:1]), running[:-1]], axis=0).astype(jnp.bfloat16)
-    returned = lax.all_to_all(before.reshape(devices, -1, E), ("seq", "head"), 0, 0, tiled=True)
+    returned = lax.all_to_all(before, ("seq", "z"), 0, 0, tiled=True)
     own_rows = returned.reshape(heads, E // 2, E)
-    other_rows = lax.ppermute(own_rows, "head", pairs)
+    other_rows = lax.ppermute(own_rows, "core", pairs)
     return gated_attention(core, queries, near, own_rows, other_rows, gate_logits, norm_gain)
 
 
 def solution(mesh):
-    rows = P(("seq", "head"), None)
+    seq = mesh.shape["seq"]
+    cores = 2
+    split = Mesh(mesh.devices.reshape(seq, mesh.shape["head"] // cores, cores), ("seq", "z", "core"))
+    rows = P(("seq", "z", "core"), None)
     return jax.shard_map(
         on_device,
-        mesh=mesh,
+        mesh=split,
         in_specs=(rows, rows, rows, rows, P()),
         out_specs=rows,
         check_vma=False,

time: 117 us -> 118 us (level)
  starting transfers between devices: 4.52 us -> 8.41 us
  blocking collectives: 82 us -> 79.2 us
    ppermute x3, starting transfers between devices: 4.52 us -> 8.41 us  [the longest x1 3.88 us: on_device(): other_rows = lax.ppermute(own_rows, 'core', pairs)]
    all_to_all x2, blocking collectives: 82 us -> 79.2 us  [the longest x1 44.7 us: on_device(): lax.all_to_all(outgoing, ('seq', 'z'), 0, 0, tiled=True).astype(jnp.float32)]
where the time goes in v14:
time: 118 us
  blocking collectives  79.2 us (67%)
  Pallas kernels  20.4 us (17%)
  starting transfers between devices  8.41 us (7%)
  waiting for transfers between devices  5.74 us (5%)
  local copies, waits for them, and re-layouts  3.41 us (3%)
    all_to_all x1, blocking collectives, on_device(): lax.all_to_all(outgoing, ('seq', 'z'), 0, 0, tiled=True).astype(jnp.float32)  44.7 us
    all_to_all x1, blocking collectives, on_device(): returned = lax.all_to_all(before, ('seq', 'z'), 0, 0, tiled=True)  34.5 us
    pallas_call x1, Pallas kernels, gated_attention(): pl.pallas_call(output_kernel, grid_spec=pltpu.PrefetchScalarGridSpec(num_...  8.63 us
    pallas_call x1, Pallas kernels, near_attention(): pl.pallas_call(near_kernel, grid_spec=pltpu.PrefetchScalarGridSpec(num_sc...  7.41 us
    pallas_call x1, Pallas kernels, block_states(): pl.pallas_call(state_kernel, grid_spec=pltpu.PrefetchScalarGridSpec(num_s...  4.39 us
    ppermute x1, waiting for transfers between devices, on_device(): first_half = lax.ppermute(first_rows, 'core', [(0, 1)])  4.07 us
    ppermute x1, starting transfers between devices, on_device(): other_rows = lax.ppermute(own_rows, 'core', pairs)  3.88 us
    ppermute x1, starting transfers between devices, on_device(): partner_half = lax.ppermute(for_partner, 'core', pairs)  3.24 us
  transfers between devices with their start and end apart: 3, of which 2 were waited for; matrix products, arithmetic and copies ran while one was open for 1% of the time, Pallas kernels for 0%

profile of v14, /device:TPU:1, one launch (start us, length us, event | category | flops | bytes accessed | tf_op | source)
XLA Modules:
  0.0 117.5 jit_solution(4328974134192889094)
XLA Ops:
  0.0 4.4 %shard_map.55 = (f32[64,64,128]{2,1,0:T(8,128)}, f32[64,64,128]{2,1,0:T(8,128)}, bf16[64,64,128]{2,1,0:T(8,128)(2,1)}) custom-call(s32[1]{0:T(128)} %bitcast.core_ref, bf16[128,8192]{1,0:T(8,128)(2,1)} %key_ref.3, bf16[128,8192]{1,0:T(8,128)(2,1)} %value_ref.3), custom_call_target="tpu_custom_call" | custom-call | tf_op jit(solution)/shard_map/pallas_call | solution.py:34
  4.4 3.2 %collective-permute-start.1 = (f32[64,64,128]{2,1,0:T(8,128)}, f32[64,64,128]{2,1,0:T(8,128)S(1)}, u32[]{:S(2)}, u32[]{:S(2)}) collective-permute-start(f32[64,64,128]{2,1,0:T(8,128)} %get-tuple-element.11), channel_id=1, source_target_pairs={{0,1},{1,0},{2,3},{3,2},{4,5},{5,4},{6,7},{7,6},{8,9},{9,8},{10,11... | collective-permute-start | bytes 6291464 | tf_op jit(solution)/shard_map/ppermute | solution.py:150
  7.6 1.3 %collective-permute-start = (bf16[64,64,128]{2,1,0:T(8,128)(2,1)}, bf16[64,64,128]{2,1,0:T(8,128)(2,1)S(1)}, u32[]{:S(2)}, u32[]{:S(2)}) collective-permute-start(bf16[64,64,128]{2,1,0:T(8,128)(2,1)} %get-tuple-element.10), channel_id=1, source_target_pairs={{0,1},{2,3},{4,5},{6,7},{8,9},{10,11},{12,13},{14,15},{16,17},{18,... | collective-permute-start | bytes 3145736 | tf_op jit(solution)/shard_map/ppermute | solution.py:151
  8.9 4.1 %collective-permute-done.first_ref = bf16[64,64,128]{2,1,0:T(8,128)(2,1)S(1)} collective-permute-done((bf16[64,64,128]{2,1,0:T(8,128)(2,1)}, bf16[64,64,128]{2,1,0:T(8,128)(2,1)S(1)}, u32[]{:S(2)}, u32[]{:S(2)}) %collective-permute-start) | collective-permute-done | bytes 1048608 | tf_op jit(solution)/shard_map/ppermute | solution.py:151
  13.0 0.0 copy-start.2
  13.0 0.0 collective-permute-done.1.partner_ref
  13.0 0.0 copy-start.1
  13.0 1.0 copy-done.2
  14.0 0.6 copy-done.1
  14.6 7.4 %shard_map.56 = (f32[128,8192]{1,0:T(8,128)}, bf16[64,64,128]{2,1,0:T(8,128)(2,1)}) custom-call(s32[1]{0:T(128)} %bitcast.core_ref, bf16[128,8192]{1,0:T(8,128)(2,1)} %query_ref.3, bf16[128,8192]{1,0:T(8,128)(2,1)} %key_ref.3, bf16[128,8192]{1,0:T(8,128)(2,1)} %value_ref.3, bf16[64,64,128]{2,1,0:T(8,128)(2,1)} %copy-done.2, f32[64,64,128]{2,1,0:T(8,128)} %copy-done.1, ...), custom_call_target="tpu_custom_call" | custom-call | tf_op jit(solution)/shard_map/pallas_call | solution.py:69
  22.1 44.7 %all_to_all.10 = bf16[128,32,128]{2,1,0:T(8,128)(2,1)S(1)} all-to-all(bf16[128,32,128]{2,1,0:T(8,128)(2,1)} %bitcast.5), channel_id=1, replica_groups=mesh['seq'=16,'z'=8,'core'=2] {'seq','z'}, dimensions={0} | all-to-all | bytes 2097152 | tf_op jit(solution)/shard_map/all_to_all | solution.py:155
  66.7 0.3 fusion
  67.0 0.1 slice.7
  67.1 0.0 copy-start.4
  67.1 0.1 concatenate.3
  67.2 34.5 %all_to_all.11 = bf16[128,32,128]{2,1,0:T(8,128)(2,1)S(1)} all-to-all(bf16[128,32,128]{2,1,0:T(8,128)(2,1)S(1)} %concatenate.3), channel_id=1, replica_groups=mesh['seq'=16,'z'=8,'core'=2] {'seq','z'}, dimensions={0} | all-to-all | bytes 2097152 | tf_op jit(solution)/shard_map/all_to_all | solution.py:159
  101.7 0.0 copy-start
  101.7 3.9 %collective-permute-start.2 = (bf16[64,64,128]{2,1,0:T(8,128)(2,1)S(1)}, bf16[64,64,128]{2,1,0:T(8,128)(2,1)S(1)}, u32[]{:S(2)}, u32[]{:S(2)}) collective-permute-start(bf16[64,64,128]{2,1,0:T(8,128)(2,1)S(1)} %bitcast.3), channel_id=1, source_target_pairs={{0,1},{1,0},{2,3},{3,2},{4,5},{5,4},{6,7},{7,6},{8,9},{9,8},{10,11... | collective-permute-start | bytes 3145736 | tf_op jit(solution)/shard_map/ppermute | solution.py:161
  105.6 0.0 copy-done.4
  105.6 0.6 reshape.17.gain_ref
  106.2 1.7 %collective-permute-done.2.other_ref = bf16[64,64,128]{2,1,0:T(8,128)(2,1)S(1)} collective-permute-done((bf16[64,64,128]{2,1,0:T(8,128)(2,1)S(1)}, bf16[64,64,128]{2,1,0:T(8,128)(2,1)S(1)}, u32[]{:S(2)}, u32[]{:S(2)}) %collective-permute-start.2) | collective-permute-done | bytes 1048608 | tf_op jit(solution)/shard_map/ppermute | solution.py:161
  107.9 0.0 copy-done
  107.9 1.0 copy-done.3
  108.9 8.6 %shard_map.57 = bf16[128,8192]{1,0:T(8,128)(2,1)} custom-call(s32[1]{0:T(128)} %bitcast.core_ref, bf16[128,8192]{1,0:T(8,128)(2,1)} %query_ref.3, f32[128,8192]{1,0:T(8,128)} %get-tuple-element.13.near_ref, bf16[64,64,128]{2,1,0:T(8,128)(2,1)} %bitcast.4, bf16[64,64,128]{2,1,0:T(8,128)(2,1)} %copy-done.3, bf16[128,8192]{1,0:T(8,128)(2,1)} %gate_ref.1, ...), custom_call_target="tpu_custom_call" | custom-call | tf_op jit(solution)/shard_map/pallas_call | solution.py:127
  (1 shorter events, 0.0 us)
Async XLA Ops:
  4.4 8.6 %collective-permute-start.1 = (f32[64,64,128]{2,1,0:T(8,128)}, f32[64,64,128]{2,1,0:T(8,128)S(1)}, u32[]{:S(2)}, u32[]{:S(2)}) collective-permute-start(f32[64,64,128]{2,1,0:T(8,128)} %get-tuple-element.11), channel_id=1, source_target_pairs={{0,1},{1,0},{2,3},{3,2},{4,5},{5,4},{6,7},{7,6},{8,9},{9,8},{10,11... | collective-permute-start | bytes 6291464 | tf_op jit(solution)/shard_map/ppermute | solution.py:150
  7.6 5.4 %collective-permute-start = (bf16[64,64,128]{2,1,0:T(8,128)(2,1)}, bf16[64,64,128]{2,1,0:T(8,128)(2,1)S(1)}, u32[]{:S(2)}, u32[]{:S(2)}) collective-permute-start(bf16[64,64,128]{2,1,0:T(8,128)(2,1)} %get-tuple-element.10), channel_id=1, source_target_pairs={{0,1},{2,3},{4,5},{6,7},{8,9},{10,11},{12,13},{14,15},{16,17},{18,... | collective-permute-start | bytes 3145736 | tf_op jit(solution)/shard_map/ppermute | solution.py:151
  13.0 1.0 copy-start.2
  13.0 1.6 %copy-start.1 = (f32[64,64,128]{2,1,0:T(8,128)}, f32[64,64,128]{2,1,0:T(8,128)S(1)}, u32[]{:S(2)}) copy-start(f32[64,64,128]{2,1,0:T(8,128)S(1)} %collective-permute-done.1.partner_ref) | copy-start | bytes 6291460
  67.1 38.5 %copy-start.4 = (bf16[8192]{0:T(1024)(128)(2,1)S(1)}, bf16[8192]{0:T(1024)(128)(2,1)}, u32[]{:S(2)}) copy-start(bf16[8192]{0:T(1024)(128)(2,1)} %param.9) | copy-start | bytes 49156
  101.7 6.2 %copy-start = (bf16[128,32,128]{2,1,0:T(8,128)(2,1)}, bf16[128,32,128]{2,1,0:T(8,128)(2,1)S(1)}, u32[]{:S(2)}) copy-start(bf16[128,32,128]{2,1,0:T(8,128)(2,1)S(1)} %all_to_all.11) | copy-start | bytes 3145732
  101.7 6.2 %collective-permute-start.2 = (bf16[64,64,128]{2,1,0:T(8,128)(2,1)S(1)}, bf16[64,64,128]{2,1,0:T(8,128)(2,1)S(1)}, u32[]{:S(2)}, u32[]{:S(2)}) collective-permute-start(bf16[64,64,128]{2,1,0:T(8,128)(2,1)S(1)} %bitcast.3), channel_id=1, source_target_pairs={{0,1},{1,0},{2,3},{3,2},{4,5},{5,4},{6,7},{7,6},{8,9},{9,8},{10,11... | collective-permute-start | bytes 3145736 | tf_op jit(solution)/shard_map/ppermute | solution.py:161
  107.9 1.0 copy-start.3

commit v15 on v13

--- a/solution.py
+++ b/solution.py
@@ -9,7 +9,7 @@
 GROUP = 32
 
 
-def state_kernel(core_ref, key_ref, value_ref, mine_ref, partner_ref, first_ref):
+def state_kernel(core_ref, key_ref, value_ref, mine_ref, whole_ref):
     first = core_ref[0] == 0
     half = E // 2
     for j in range(GROUP):
@@ -18,10 +18,8 @@
             key_ref[:, cols], value_ref[:, cols], (((0,), (0,)), ((), ())),
             preferred_element_type=jnp.float32,
         )
-        upper, lower = state[:half], state[half:]
-        mine_ref[j] = jnp.where(first, upper, lower)
-        partner_ref[j] = jnp.where(first, lower, upper)
-        first_ref[j] = upper.astype(jnp.bfloat16)
+        mine_ref[j] = jnp.where(first, state[:half], state[half:])
+        whole_ref[j] = state.astype(jnp.bfloat16)
 
 
 def block_states(core, key_vectors, values):
@@ -29,20 +27,21 @@
     heads = width // E
     cols = pl.BlockSpec((tokens, GROUP * E), lambda i, core: (0, i))
     halves = pl.BlockSpec((GROUP, E // 2, E), lambda i, core: (i, 0, 0))
-    shape = (heads, E // 2, E)
+    wholes = pl.BlockSpec((GROUP, E, E), lambda i, core: (i, 0, 0))
     return pl.pallas_call(
         state_kernel,
         grid_spec=pltpu.PrefetchScalarGridSpec(
-            num_scalar_prefetch=1, grid=(heads // GROUP,), in_specs=[cols, cols], out_specs=[halves] * 3
+            num_scalar_prefetch=1, grid=(heads // GROUP,), in_specs=[cols, cols], out_specs=[halves, wholes]
         ),
-        out_shape=[jax.ShapeDtypeStruct(shape, jnp.float32), jax.ShapeDtypeStruct(shape, jnp.float32),
-                   jax.ShapeDtypeStruct(shape, jnp.bfloat16)],
+        out_shape=[jax.ShapeDtypeStruct((heads, E // 2, E), jnp.float32),
+                   jax.ShapeDtypeStruct((heads, E, E), jnp.bfloat16)],
     )(core.reshape(1), key_vectors, values)
 
 
-def near_kernel(core_ref, query_ref, key_ref, value_ref, first_ref, partner_ref, mine_ref, near_ref, chip_ref):
+def near_kernel(core_ref, query_ref, key_ref, value_ref, partner_ref, mine_ref, near_ref, chip_ref):
     tokens = query_ref.shape[0]
     first = core_ref[0] == 0
+    half = E // 2
     lower_mask = lax.broadcasted_iota(jnp.int32, (tokens, tokens), 0) >= lax.broadcasted_iota(
         jnp.int32, (tokens, tokens), 1
     )
@@ -54,26 +53,28 @@
         )
         weights = jnp.where(lower_mask, scores, 0.0).astype(jnp.bfloat16)
         total = jnp.dot(weights, value_ref[:, cols], preferred_element_type=jnp.float32)
-        before = jnp.concatenate([first_ref[j], partner_ref[j].astype(jnp.bfloat16)], axis=0)
-        before_part = jnp.dot(query, before, preferred_element_type=jnp.float32)
+        partner = partner_ref[j]
+        before_part = jnp.dot(query, partner, preferred_element_type=jnp.float32)
         near_ref[:, cols] = total + jnp.where(first, 0.0, before_part)
-        chip_ref[j] = (mine_ref[j] + partner_ref[j]).astype(jnp.bfloat16)
+        partner_rows = jnp.where(first, partner[:half], partner[half:]).astype(jnp.float32)
+        chip_ref[j] = (mine_ref[j] + partner_rows).astype(jnp.bfloat16)
 
 
-def near_attention(core, queries, key_vectors, values, first_half, partner_half, mine):
+def near_attention(core, queries, key_vectors, values, partner_state, mine):
     tokens, width = queries.shape
     heads = width // E
     cols = pl.BlockSpec((tokens, GROUP * E), lambda i, core: (0, i))
     halves = pl.BlockSpec((GROUP, E // 2, E), lambda i, core: (i, 0, 0))
+    wholes = pl.BlockSpec((GROUP, E, E), lambda i, core: (i, 0, 0))
     return pl.pallas_call(
         near_kernel,
         grid_spec=pltpu.PrefetchScalarGridSpec(
-            num_scalar_prefetch=1, grid=(heads // GROUP,), in_specs=[cols, cols, cols, halves, halves, halves],
+            num_scalar_prefetch=1, grid=(heads // GROUP,), in_specs=[cols, cols, cols, wholes, halves],
             out_specs=[cols, halves],
         ),
         out_shape=[jax.ShapeDtypeStruct((tokens, width), jnp.float32),
                    jax.ShapeDtypeStruct((heads, E // 2, E), jnp.bfloat16)],
-    )(core.reshape(1), queries, key_vectors, values, first_half, partner_half, mine)
+    )(core.reshape(1), queries, key_vectors, values, partner_state, mine)
 
 
 def output_kernel(core_ref, query_ref, near_ref, own_ref, other_ref, gate_ref, gain_ref,
@@ -145,10 +146,9 @@
     core = lax.axis_index("head") % 2
     pairs = [(h, h ^ 1) for h in range(2 * chips)]
 
-    mine, for_partner, first_rows = block_states(core, key_vectors, values)
-    partner_half = lax.ppermute(for_partner, "head", pairs)
-    first_half = lax.ppermute(first_rows, "head", [(h, h + 1) for h in range(0, 2 * chips, 2)])
-    near, my_rows = near_attention(core, queries, key_vectors, values, first_half, partner_half, mine)
+    mine, whole = block_states(core, key_vectors, values)
+    partner_state = lax.ppermute(whole, "head", pairs)
+    near, my_rows = near_attention(core, queries, key_vectors, values, partner_state, mine)
     devices = lax.axis_size("seq") * 2 * chips
     outgoing = my_rows.reshape(devices, -1, E)
     incoming = lax.all_to_all(outgoing, ("seq", "head"), 0, 0, tiled=True)

time: 117 us -> 115 us (0.983)
  starting transfers between devices: 4.52 us -> 3.24 us
    ppermute x2 -> x1, starting transfers between devices: 4.52 us -> 3.24 us  [on_device(): partner_state = lax.ppermute(whole, 'head', pairs)]
    unnamed x10 -> x8, local copies, waits for them, and re-layouts: 2.65 us -> 2.33 us
    ppermute x2 -> x1, waiting for transfers between devices: 4.08 us -> 4 us  [on_device(): partner_state = lax.ppermute(whole, 'head', pairs)]
  transfers between devices with their start and end apart: 3 -> 2, of which waited for: 2 -> 2; matrix products, arithmetic and copies ran while one was open for 1% -> 1% of each run, Pallas kernels for 0% -> 0%
where the time goes in v15:
time: 115 us
  blocking collectives  82.2 us (71%)
  Pallas kernels  19.6 us (17%)
  waiting for transfers between devices  5.95 us (5%)
  local copies, waits for them, and re-layouts  3.28 us (3%)
  starting transfers between devices  3.24 us (3%)
    all_to_all x1, blocking collectives, on_device(): incoming = lax.all_to_all(outgoing, ('seq', 'head'), 0, 0, tiled=True)  45.3 us
    all_to_all x1, blocking collectives, on_device(): lax.all_to_all(before.reshape(devices, -1, E), ('seq', 'head'), 0, 0, til...  36.9 us
    pallas_call x1, Pallas kernels, gated_attention(): pl.pallas_call(output_kernel, grid_spec=pltpu.PrefetchScalarGridSpec(num_...  8.62 us
    pallas_call x1, Pallas kernels, near_attention(): pl.pallas_call(near_kernel, grid_spec=pltpu.PrefetchScalarGridSpec(num_sc...  6.87 us
    pallas_call x1, Pallas kernels, block_states(): pl.pallas_call(state_kernel, grid_spec=pltpu.PrefetchScalarGridSpec(num_s...  4.09 us
    ppermute x1, waiting for transfers between devices, on_device(): partner_state = lax.ppermute(whole, 'head', pairs)  4 us
    ppermute x1, starting transfers between devices, on_device(): partner_state = lax.ppermute(whole, 'head', pairs)  3.24 us
    unnamed x8, local copies, waits for them, and re-layouts  2.33 us
  transfers between devices with their start and end apart: 2, of which 2 were waited for; matrix products, arithmetic and copies ran while one was open for 1% of the time, Pallas kernels for 0%

profile of v15, /device:TPU:1, one launch (start us, length us, event | category | flops | bytes accessed | tf_op | source)
XLA Modules:
  0.0 114.5 jit_solution(11808136489406861326)
XLA Ops:
  0.0 4.1 %shard_map.55 = (f32[64,64,128]{2,1,0:T(8,128)}, bf16[64,128,128]{2,1,0:T(8,128)(2,1)}) custom-call(s32[1]{0:T(128)} %bitcast.core_ref, bf16[128,8192]{1,0:T(8,128)(2,1)} %key_ref.3, bf16[128,8192]{1,0:T(8,128)(2,1)} %value_ref.3), custom_call_target="tpu_custom_call" | custom-call | tf_op jit(solution)/shard_map/pallas_call | solution.py:31
  4.1 3.2 %collective-permute-start = (bf16[64,128,128]{2,1,0:T(8,128)(2,1)}, bf16[64,128,128]{2,1,0:T(8,128)(2,1)S(1)}, u32[]{:S(2)}, u32[]{:S(2)}) collective-permute-start(bf16[64,128,128]{2,1,0:T(8,128)(2,1)} %get-tuple-element.9), channel_id=1, source_target_pairs={{0,1},{1,0},{2,3},{3,2},{4,5},{5,4},{6,7},{7,6},{8,9},{9,8},{10,11... | collective-permute-start | bytes 6291464 | tf_op jit(solution)/shard_map/ppermute | solution.py:150
  7.3 4.0 %collective-permute-done.partner_ref = bf16[64,128,128]{2,1,0:T(8,128)(2,1)S(1)} collective-permute-done((bf16[64,128,128]{2,1,0:T(8,128)(2,1)}, bf16[64,128,128]{2,1,0:T(8,128)(2,1)S(1)}, u32[]{:S(2)}, u32[]{:S(2)}) %collective-permute-start) | collective-permute-done | bytes 2097184 | tf_op jit(solution)/shard_map/ppermute | solution.py:150
  11.3 0.0 copy-start.1
  11.3 1.3 %copy-done.1 = bf16[64,128,128]{2,1,0:T(8,128)(2,1)} copy-done((bf16[64,128,128]{2,1,0:T(8,128)(2,1)}, bf16[64,128,128]{2,1,0:T(8,128)(2,1)S(1)}, u32[]{:S(2)}) %copy-start.1) | copy-done | bytes 2097176
  12.6 6.9 %shard_map.56 = (f32[128,8192]{1,0:T(8,128)}, bf16[64,64,128]{2,1,0:T(8,128)(2,1)}) custom-call(s32[1]{0:T(128)} %bitcast.core_ref, bf16[128,8192]{1,0:T(8,128)(2,1)} %query_ref.3, bf16[128,8192]{1,0:T(8,128)(2,1)} %key_ref.3, bf16[128,8192]{1,0:T(8,128)(2,1)} %value_ref.3, bf16[64,128,128]{2,1,0:T(8,128)(2,1)} %copy-done.1, ...), custom_call_target="tpu_custom_call" | custom-call | tf_op jit(solution)/shard_map/pallas_call | solution.py:69
  19.5 45.3 %all_to_all.10 = bf16[256,16,128]{2,1,0:T(8,128)(2,1)S(1)} all-to-all(bf16[256,16,128]{2,1,0:T(8,128)(2,1)} %bitcast.10), channel_id=1, replica_groups=mesh['seq'=16,'head'=16] {'seq','head'}, dimensions={0} | all-to-all | bytes 2097152 | tf_op jit(solution)/shard_map/all_to_all | solution.py:154
  64.8 0.2 fusion
  65.1 0.1 slice.7
  65.2 0.0 copy-start.3
  65.2 0.1 concatenate.3
  65.4 36.9 %all_to_all.11 = bf16[256,16,128]{2,1,0:T(8,128)(2,1)S(1)} all-to-all(bf16[256,16,128]{2,1,0:T(8,128)(2,1)S(1)} %bitcast.8), channel_id=1, replica_groups=mesh['seq'=16,'head'=16] {'seq','head'}, dimensions={0} | all-to-all | bytes 2097152 | tf_op jit(solution)/shard_map/all_to_all | solution.py:159
  102.2 0.0 copy-start
  102.2 0.0 collective-permute-start.1
  102.2 0.0 copy-done.3
  102.2 0.7 reshape.24.gain_ref
  102.9 2.0 %collective-permute-done.1.other_ref = bf16[64,64,128]{2,1,0:T(8,128)(2,1)S(1)} collective-permute-done((bf16[64,64,128]{2,1,0:T(8,128)(2,1)S(1)}, bf16[64,64,128]{2,1,0:T(8,128)(2,1)S(1)}, u32[]{:S(2)}, u32[]{:S(2)}) %collective-permute-start.1) | collective-permute-done | bytes 1048608 | tf_op jit(solution)/shard_map/ppermute | solution.py:161
  104.9 0.0 copy-start.2
  104.9 0.0 copy-done
  104.9 1.0 copy-done.2
  105.9 8.6 %shard_map.57 = bf16[128,8192]{1,0:T(8,128)(2,1)} custom-call(s32[1]{0:T(128)} %bitcast.core_ref, bf16[128,8192]{1,0:T(8,128)(2,1)} %query_ref.3, f32[128,8192]{1,0:T(8,128)} %get-tuple-element.11.near_ref, bf16[64,64,128]{2,1,0:T(8,128)(2,1)} %bitcast.7, bf16[64,64,128]{2,1,0:T(8,128)(2,1)} %copy-done.2, bf16[128,8192]{1,0:T(8,128)(2,1)} %gate_ref.1, ...), custom_call_target="tpu_custom_call" | custom-call | tf_op jit(solution)/shard_map/pallas_call | solution.py:127
Async XLA Ops:
  4.1 7.2 %collective-permute-start = (bf16[64,128,128]{2,1,0:T(8,128)(2,1)}, bf16[64,128,128]{2,1,0:T(8,128)(2,1)S(1)}, u32[]{:S(2)}, u32[]{:S(2)}) collective-permute-start(bf16[64,128,128]{2,1,0:T(8,128)(2,1)} %get-tuple-element.9), channel_id=1, source_target_pairs={{0,1},{1,0},{2,3},{3,2},{4,5},{5,4},{6,7},{7,6},{8,9},{9,8},{10,11... | collective-permute-start | bytes 6291464 | tf_op jit(solution)/shard_map/ppermute | solution.py:150
  11.3 1.3 %copy-start.1 = (bf16[64,128,128]{2,1,0:T(8,128)(2,1)}, bf16[64,128,128]{2,1,0:T(8,128)(2,1)S(1)}, u32[]{:S(2)}) copy-start(bf16[64,128,128]{2,1,0:T(8,128)(2,1)S(1)} %collective-permute-done.partner_ref) | copy-start | bytes 6291460
  65.2 37.0 %copy-start.3 = (bf16[8192]{0:T(1024)(128)(2,1)S(1)}, bf16[8192]{0:T(1024)(128)(2,1)}, u32[]{:S(2)}) copy-start(bf16[8192]{0:T(1024)(128)(2,1)} %param.9) | copy-start | bytes 49156
  102.2 2.7 %copy-start = (bf16[256,16,128]{2,1,0:T(8,128)(2,1)}, bf16[256,16,128]{2,1,0:T(8,128)(2,1)S(1)}, u32[]{:S(2)}) copy-start(bf16[256,16,128]{2,1,0:T(8,128)(2,1)S(1)} %all_to_all.11) | copy-start | bytes 3145732
  102.2 2.7 %collective-permute-start.1 = (bf16[64,64,128]{2,1,0:T(8,128)(2,1)S(1)}, bf16[64,64,128]{2,1,0:T(8,128)(2,1)S(1)}, u32[]{:S(2)}, u32[]{:S(2)}) collective-permute-start(bf16[64,64,128]{2,1,0:T(8,128)(2,1)S(1)} %bitcast.6), channel_id=1, source_target_pairs={{0,1},{1,0},{2,3},{3,2},{4,5},{5,4},{6,7},{7,6},{8,9},{9,8},{10,11... | collective-permute-start | bytes 3145736 | tf_op jit(solution)/shard_map/ppermute | solution.py:161
  104.9 1.0 copy-start.2
